TPU v7x, 256 devices: a whole 4x4x8 slice. The times are simulated.
256 devices in a mesh: chan: 16 (over z, core), tm: 16 (over x, y).
Axes of the slice: x: 4, y: 4, z: 8, core: 2. Of those that a mesh axis runs over, the one named last changes fastest.
Arguments:
- signal: bfloat16 [512, 131072], P('chan', 'tm'), may hold values from -6 to 6
- pair_band: int32 [16, 512, 8], P('tm', 'chan'), may hold values from 0 to 255, as said below
- pair_offset: int32 [16, 512, 8], P('tm', 'chan'), may hold values from 1 to 8
- pair_owner: int32 [16, 512, 8, 1], P('tm', 'chan'), may hold values from 0 to 15; in each aligned block of 256 rows (0 to 255, 256 to 511, ..., all dimensions but the last counted through in order) at most 48 rows name the same one
Outputs:
- cyclic_map: bfloat16 [16, 16, 16, 48, 2048], P('tm', 'chan')
Inputs may be any that keep to these rules, and one draw needn't show every extreme that they name: `pair_band`: entry [t, c, q] is a band of the t-th block, t * 16 to (t + 1) * 16 - 1. `pair_owner`: among the 256 rows of one device (one block of bands, one channel group) no owner appears more than 48 times, and in some devices one owner appears exactly 48 times.
All inputs are finite; a program needn't handle non-finite values.
Results may differ from a plain program's by a relative error of at most 0.0079.
Values may be sent and summed in bfloat16 or wider, within the bound.
No kernel may reach another device: no remote copies, remote signals or barrier semaphores. Data moves between devices by JAX's collectives and lax.ppermute only.
A program may use at most 128 MiB of HBM per device.

v0:
```python
import math

import jax
import jax.numpy as jnp
from jax import lax
from jax.sharding import PartitionSpec as P

BANDS = 256
HOP = 64
FRAMES = 2048
KEEP = 1024
DMAX = 8


def passed_along(array, axis, by):
    devices = lax.axis_size(axis)
    pairs = [(i, i + by) for i in range(devices) if 0 <= i + by < devices]
    return lax.ppermute(array, axis, pairs)


def bank_matrix(bands):
    index = jnp.arange(bands, dtype=jnp.int32)
    angle = (index[:, None] * index[None, :] % bands).astype(jnp.float32) * (2.0 * math.pi / bands)
    window = 0.5 - 0.5 * jnp.cos((index.astype(jnp.float32) + 0.5) * (2.0 * math.pi / bands))
    scaled = window / math.sqrt(3.0 * bands / 8.0)
    return jnp.concatenate(
        [scaled[:, None] * jnp.cos(angle), -scaled[:, None] * jnp.sin(angle)], axis=1
    ).astype(jnp.bfloat16)


def fourier_block(start, count, frames, keep):
    moment = start + jnp.arange(count, dtype=jnp.int32)
    cycles = jnp.arange(keep, dtype=jnp.int32)
    angle = (moment[:, None] * cycles[None, :] % frames).astype(jnp.float32) * (
        2.0 * math.pi / frames
    )
    cosine = jnp.cos(angle) / math.sqrt(frames)
    sine = jnp.sin(angle) / math.sqrt(frames)
    upper_half = jnp.concatenate([cosine, -sine], axis=1)
    lower_half = jnp.concatenate([sine, cosine], axis=1)
    return jnp.concatenate([upper_half, lower_half], axis=0).astype(jnp.bfloat16)


def demodulate(first, second, offset, moment_count):
    real_part = first[..., 0, :] * second[..., 0, :] + first[..., 1, :] * second[..., 1, :]
    imag_part = first[..., 1, :] * second[..., 0, :] - first[..., 0, :] * second[..., 1, :]
    shift_bins = (offset * (HOP * FRAMES // BANDS) - KEEP // 2) % FRAMES
    moment = jnp.arange(moment_count, dtype=jnp.int32)
    angle = (shift_bins[..., None] * moment % FRAMES).astype(jnp.float32) * (2.0 * math.pi / FRAMES)
    cosine = jnp.cos(angle)
    sine = jnp.sin(angle)
    return jnp.concatenate(
        [real_part * cosine + imag_part * sine, imag_part * cosine - real_part * sine], axis=-1
    ).astype(jnp.bfloat16)


def transform(products):
    span = min(512, FRAMES)
    total = jnp.zeros((products.shape[0], 2 * KEEP), jnp.float32)
    for start in range(0, FRAMES, span):
        operand = jnp.concatenate(
            [
                products[:, start : start + span],
                products[:, FRAMES + start : FRAMES + start + span],
            ],
            axis=1,
        )
        total = total + jnp.dot(
            operand, fourier_block(start, span, FRAMES, KEEP), preferred_element_type=jnp.float32
        )
    return total.astype(jnp.bfloat16)


def on_device(signal, pair_band, pair_offset, pair_owner):
    channels = signal.shape[0]
    stride_count = BANDS // HOP
    frames_dev = signal.shape[1] // HOP
    bank_table = bank_matrix(BANDS)
    sample_tail = passed_along(signal[:, : BANDS - HOP], "tm", -1)
    records = jnp.concatenate([signal, sample_tail], axis=1)
    pieces = records.reshape(channels, frames_dev + stride_count - 1, HOP)
    framed = jnp.concatenate(
        [pieces[:, part_index : part_index + frames_dev, :] for part_index in range(stride_count)],
        axis=2,
    )
    spectra = jnp.einsum(
        "cmn,nk->ckm", framed, bank_table, preferred_element_type=jnp.float32
    ).astype(jnp.bfloat16)
    spectra = spectra.reshape(channels, 2, BANDS, frames_dev)
    regrouped = lax.all_to_all(spectra, "tm", split_axis=2, concat_axis=3, tiled=True)
    band_dev = regrouped.shape[2]
    upper_bands = passed_along(regrouped[:, :, :DMAX, :], "tm", -1)
    widened = jnp.concatenate([regrouped, upper_bands], axis=2)
    local_band = pair_band[0] - lax.axis_index("tm") * band_dev
    offset = pair_offset[0]
    positions = jnp.arange(band_dev + DMAX, dtype=jnp.int32)
    pick_first = (local_band[..., None] == positions).astype(jnp.bfloat16)
    pick_second = ((local_band + offset)[..., None] == positions).astype(jnp.bfloat16)
    first = jnp.einsum("cqb,cpbm->cqpm", pick_first, widened, preferred_element_type=jnp.float32)
    second = jnp.einsum("cqb,cpbm->cqpm", pick_second, widened, preferred_element_type=jnp.float32)
    demod = demodulate(first, second, offset, FRAMES).reshape(-1, 2 * FRAMES)
    owner = pair_owner[0, :, :, 0].reshape(-1)
    groups = lax.axis_size("chan")
    capacity = max(2, 3 * owner.shape[0] // groups)
    hits = (owner[:, None] == jnp.arange(groups, dtype=jnp.int32)[None, :]).astype(jnp.int32)
    rank = jnp.sum((jnp.cumsum(hits, axis=0) - 1) * hits, axis=1)
    slot = owner * capacity + rank
    placing = (jnp.arange(groups * capacity, dtype=jnp.int32)[:, None] == slot[None, :]).astype(
        jnp.bfloat16
    )
    correlation = transform(demod)
    outgoing = jnp.dot(placing, correlation, preferred_element_type=jnp.float32).astype(
        jnp.bfloat16
    )
    outgoing = outgoing.reshape(groups, capacity, 2 * KEEP)
    arrived = lax.all_to_all(outgoing, "chan", split_axis=0, concat_axis=0, tiled=True)
    return arrived.reshape(1, 1, groups, capacity, 2 * KEEP)


def solution(mesh):
    return jax.shard_map(
        on_device,
        mesh=mesh,
        in_specs=(
            P("chan", "tm"),
            P("tm", "chan", None),
            P("tm", "chan", None),
            P("tm", "chan", None, None),
        ),
        out_specs=P("tm", "chan", None, None, None),
        check_vma=False,
    )
```

profile of v0, /device:TPU:1, one launch (start us, length us, event | category | flops | bytes accessed | tf_op | source)
XLA Modules:
  0.0 259.4 jit_solution(5865167460584121117)
XLA Ops:
  3.2 2.6 %collective-permute-done = bf16[32,192]{1,0:T(8,128)(2,1)S(1)} collective-permute-done((bf16[32,192]{1,0:T(8,128)(2,1)S(1)}, bf16[32,192]{1,0:T(8,128)(2,1)S(1)}, u32[]{:S(2)}, u32[]{:S(2)}) %collective-permute-start) | collective-permute-done | bytes 12320 | tf_op jit(solution)/shard_map/ppermute | solution.py:18
  8.7 2.1 convolution_convert_fusion.1
  10.7 6.3 %copy.19 = bf16[32,2,256,128]{3,1,0,2:T(2,128)(2,1)} copy(bf16[32,2,256,128]{3,2,1,0:T(8,128)(2,1)S(1)} %bitcast.76) | data formatting | bytes 8388608 | tf_op jit(solution)/shard_map/reshape | solution.py:89
  17.0 9.0 %all-to-all-start = ((bf16[32,2,256,128]{3,1,0,2:T(2,128)(2,1)}), bf16[32,2,256,128]{3,1,0,2:T(2,128)(2,1)}, u32[]{:S(2)}, u32[]{:S(2)}) async-start(bf16[32,2,256,128]{3,1,0,2:T(2,128)(2,1)} %copy.19), calls=%async_computation | async-start | bytes 8388608 | tf_op jit(solution)/shard_map/all_to_all | solution.py:90
  27.7 50.2 %all-to-all-done = bf16[32,2,256,128]{3,1,0,2:T(2,128)(2,1)} async-done(((bf16[32,2,256,128]{3,1,0,2:T(2,128)(2,1)}), bf16[32,2,256,128]{3,1,0,2:T(2,128)(2,1)}, u32[]{:S(2)}, u32[]{:S(2)}) %all-to-all-start) | async-done | bytes 4194336 | tf_op jit(solution)/shard_map/all_to_all | solution.py:90
  77.9 9.0 %copy.28 = bf16[32,2,16,16,128]{4,2,3,1,0:T(8,128)(2,1)} copy(bf16[32,2,16,16,128]{4,1,0,3,2:T(2,128)(2,1)} %bitcast.7) | data formatting | bytes 8388608 | tf_op jit(solution)/shard_map/all_to_all | solution.py:90
  86.9 7.3 %all_to_all.19 = bf16[32,2,16,2048]{3,2,1,0:T(8,128)(2,1)} reshape(bf16[32,2,16,16,128]{4,3,2,1,0:T(8,128)(2,1)} %bitcast.74) | data formatting | bytes 8388608 | tf_op jit(solution)/shard_map/all_to_all | solution.py:90
  94.2 1.7 slice.97
  95.9 1.5 collective-permute-start.1
  97.4 7.9 %fusion.85 = bf16[512,1024]{1,0:T(8,128)(2,1)S(1)} fusion(), kind=kLoop, calls=%fused_computation.113 | loop fusion | flops 8388608 | bytes 1048576 | tf_op jit(solution)/shard_map/convert.20
  105.3 8.6 %negate_convert_fusion.3 = (bf16[512,1024]{1,0:T(8,128)(2,1)S(1)}, bf16[512,1024]{1,0:T(8,128)(2,1)S(1)}) fusion(), kind=kLoop, calls=%fused_computation.99 | loop fusion | flops 9961472 | bytes 2097152 | tf_op jit(solution)/shard_map/convert.23
  113.9 9.2 %negate_convert_fusion.2 = (bf16[512,1024]{1,0:T(8,128)(2,1)S(1)}, bf16[512,1024]{1,0:T(8,128)(2,1)S(1)}, bf16[512,1024]{1,0:T(8,128)(2,1)S(1)}) fusion(s32[512]{0:T(512)S(1)} %iota_add_fusion.2), kind=kLoop, calls=%fused_computation.94 | loop fusion | flops 10485760 | bytes 3147776 | tf_op jit(solution)/shard_map/convert.17
  123.2 9.2 %negate_convert_fusion.1 = (bf16[512,1024]{1,0:T(8,128)(2,1)S(1)}, bf16[512,1024]{1,0:T(8,128)(2,1)S(1)}, bf16[512,1024]{1,0:T(8,128)(2,1)S(1)}) fusion(s32[512]{0:T(512)S(1)} %iota_add_fusion.1), kind=kLoop, calls=%fused_computation.89 | loop fusion | flops 10485760 | bytes 3147776 | tf_op jit(solution)/shard_map/convert.11
  132.4 9.2 %negate_convert_fusion = (bf16[512,1024]{1,0:T(8,128)(2,1)S(1)}, bf16[512,1024]{1,0:T(8,128)(2,1)S(1)}, bf16[512,1024]{1,0:T(8,128)(2,1)S(1)}) fusion(s32[512]{0:T(512)S(1)} %iota_add_fusion), kind=kLoop, calls=%fused_computation.84 | loop fusion | flops 10485760 | bytes 3147776 | tf_op jit(solution)/shard_map/convert.5
  142.5 1.6 fusion.113
  144.0 1.6 fusion.116
  145.6 9.5 %fusion.67 = (bf16[256,2048]{1,0:T(8,128)(2,1)S(1)}, f32[32,8,1,2048]{3,1,2,0:T(8,128)S(1)}, f32[32,8,1,2048]{3,1,2,0:T(8,128)S(1)}) fusion(s32[256]{0:T(256)S(1)} %and_select_fusion, f32[32,8,2,2048]{3,1,2,0:T(8,128)S(1)} %fusion.116, f32[32,8,2,2048]{3,1,2,0:T(8,128)S(1)} %fusion.113), kind=kLoop, calls=%fused_computation.79 | loop fusion | flops 12582912 | bytes 13632512 | tf_op jit(solution)/shard_map/convert.24
  155.1 9.4 %fusion.69 = bf16[256,2048]{1,0:T(8,128)(2,1)S(1)} fusion(f32[32,8,1,2048]{3,1,2,0:T(8,128)S(1)} %get-tuple-element.7, f32[32,8,1,2048]{3,1,2,0:T(8,128)S(1)} %get-tuple-element.6, s32[256]{0:T(256)S(1)} %and_select_fusion), kind=kLoop, calls=%fused_computation.81 | loop fusion | flops 9437184 | bytes 5243904 | tf_op jit(solution)/shard_map/convert.25
  164.6 1.3 fusion
  165.9 1.4 fusion.38
  167.3 1.4 fusion.35
  168.8 1.3 fusion.41
  171.1 86.6 %all_to_all.23 = bf16[16,48,2048]{2,1,0:T(8,128)(2,1)S(1)} all-to-all(bf16[16,48,2048]{2,1,0:T(8,128)(2,1)S(1)} %bitcast.73), channel_id=1, replica_groups=mesh['chan'=16,'tm'=16] {'chan'}, dimensions={0} | all-to-all | bytes 6291456 | tf_op jit(solution)/shard_map/all_to_all | solution.py:116
  257.7 1.7 copy.31
  (42 shorter events, 9.5 us)
Async XLA Ops:
  0.7 5.1 %collective-permute-start = (bf16[32,192]{1,0:T(8,128)(2,1)S(1)}, bf16[32,192]{1,0:T(8,128)(2,1)S(1)}, u32[]{:S(2)}, u32[]{:S(2)}) collective-permute-start(bf16[32,192]{1,0:T(8,128)(2,1)S(1)} %slice.74), channel_id=1, source_target_pairs={{1,0},{2,1},{3,2},{4,3},{5,4},{6,5},{7,6},{8,7},{9,8},{10,9},{11,1... | collective-permute-start | bytes 36872 | tf_op jit(solution)/shard_map/ppermute | solution.py:18
  17.0 9.1 %copy-start.2 = (s32[1,32,8,1]{1,3,2,0:T(1,128)S(1)}, s32[1,32,8,1]{1,3,2,0:T(1,128)}, u32[]{:S(2)}) copy-start(s32[1,32,8,1]{1,3,2,0:T(1,128)} %param.7) | copy-start | bytes 3076
  17.0 9.3 %copy-start.1 = (s32[1,32,8]{1,2,0:T(8,128)S(1)}, s32[1,32,8]{1,2,0:T(8,128)}, u32[]{:S(2)}) copy-start(s32[1,32,8]{1,2,0:T(8,128)} %param.6) | copy-start | bytes 3076
  17.0 9.3 %copy-start.3 = (s32[1,32,8]{1,2,0:T(8,128)S(1)}, s32[1,32,8]{1,2,0:T(8,128)}, u32[]{:S(2)}) copy-start(s32[1,32,8]{1,2,0:T(8,128)} %param.5) | copy-start | bytes 3076
  17.0 60.8 %all-to-all-start = ((bf16[32,2,256,128]{3,1,0,2:T(2,128)(2,1)}), bf16[32,2,256,128]{3,1,0,2:T(2,128)(2,1)}, u32[]{:S(2)}, u32[]{:S(2)}) async-start(bf16[32,2,256,128]{3,1,0,2:T(2,128)(2,1)} %copy.19), calls=%async_computation | async-start | bytes 8388608 | tf_op jit(solution)/shard_map/all_to_all | solution.py:90
  95.9 46.3 %collective-permute-start.1 = (bf16[32,2,8,2048]{3,2,1,0:T(8,128)(2,1)S(1)}, bf16[32,2,8,2048]{3,2,1,0:T(8,128)(2,1)S(1)}, u32[]{:S(2)}, u32[]{:S(2)}) collective-permute-start(bf16[32,2,8,2048]{3,2,1,0:T(8,128)(2,1)S(1)} %slice.97), channel_id=1, source_target_pairs={{1,0},{2,1},{3,2},{4,3},{5,4},{6,5},{7,6},{8,7},{9,8},{10,9},{11,1... | collective-permute-start | bytes 6291464 | tf_op jit(solution)/shard_map/ppermute | solution.py:18
  123.1 18.5 %copy-start = (bf16[32,2,16,2048]{3,2,1,0:T(8,128)(2,1)S(1)}, bf16[32,2,16,2048]{3,2,1,0:T(8,128)(2,1)}, u32[]{:S(2)}) copy-start(bf16[32,2,16,2048]{3,2,1,0:T(8,128)(2,1)} %all_to_all.19) | copy-start | bytes 12582916
where the time goes:
time: 261 us; the launch traced here: 259 us
  blocking collectives  86.6 us (33%)
  other arithmetic  66 us (25%)
  waiting for transfers between devices  52.8 us (20%)
  local copies, waits for them, and re-layouts  30.2 us (12%)
  starting transfers between devices  11.8 us (5%)
  matrix products  11.7 us (4%)
    all_to_all x1, blocking collectives, on_device(): lax.all_to_all(outgoing, 'chan', split_axis=0, concat_axis=0, tiled=True)  86.6 us
    another operation x10, other arithmetic  64.7 us
    all_to_all x1, waiting for transfers between devices, on_device(): lax.all_to_all(spectra, 'tm', split_axis=2, concat_axis=3, tiled=True)  50.2 us
    all_to_all x2, local copies, waits for them, and re-layouts, on_device(): lax.all_to_all(spectra, 'tm', split_axis=2, concat_axis=3, tiled=True)  16.3 us
    all_to_all x1, starting transfers between devices, on_device(): lax.all_to_all(spectra, 'tm', split_axis=2, concat_axis=3, tiled=True)  9.03 us
    reshape x1, local copies, waits for them, and re-layouts, on_device(): spectra = spectra.reshape(channels, 2, BANDS, frames_dev)  6.3 us
    dot_general x4, matrix products, transform(): jnp.dot(operand, fourier_block(start, span, FRAMES, KEEP), preferred_elem...  5.47 us
  transfers between devices with their start and end apart: 3, of which 2 were waited for; matrix products, arithmetic and copies ran while one was open for 18% of the time, Pallas kernels for 0%

commit v1 on v0

v1 whole, which is shorter than its diff:
```python
import math

import jax
import jax.numpy as jnp
from jax import lax
from jax.sharding import PartitionSpec as P

BANDS = 256
HOP = 64
FRAMES = 2048
KEEP = 1024
DMAX = 8


def passed_along(array, axis, by):
    devices = lax.axis_size(axis)
    pairs = [(i, i + by) for i in range(devices) if 0 <= i + by < devices]
    return lax.ppermute(array, axis, pairs)


def bank_matrix(bands):
    index = jnp.arange(bands, dtype=jnp.int32)
    angle = (index[:, None] * index[None, :] % bands).astype(jnp.float32) * (2.0 * math.pi / bands)
    window = 0.5 - 0.5 * jnp.cos((index.astype(jnp.float32) + 0.5) * (2.0 * math.pi / bands))
    scaled = window / math.sqrt(3.0 * bands / 8.0)
    return jnp.concatenate(
        [scaled[:, None] * jnp.cos(angle), -scaled[:, None] * jnp.sin(angle)], axis=1
    ).astype(jnp.bfloat16)


def turn_table(moments, cycles):
    angle = (moments[:, None] * cycles[None, :] % FRAMES).astype(jnp.float32) * (
        2.0 * math.pi / FRAMES
    )
    return jnp.cos(angle), jnp.sin(angle)


def fourier_tables():
    cycles = jnp.arange(KEEP, dtype=jnp.int32)
    coarse_cos, coarse_sin = turn_table(32 * jnp.arange(FRAMES // 32, dtype=jnp.int32), cycles)
    fine_cos, fine_sin = turn_table(jnp.arange(32, dtype=jnp.int32), cycles)
    scale = 1.0 / math.sqrt(FRAMES)
    cosine = (
        coarse_cos[:, None, :] * fine_cos[None, :, :] - coarse_sin[:, None, :] * fine_sin[None, :, :]
    ) * scale
    sine = (
        coarse_sin[:, None, :] * fine_cos[None, :, :] + coarse_cos[:, None, :] * fine_sin[None, :, :]
    ) * scale
    return (
        cosine.reshape(FRAMES, KEEP).astype(jnp.bfloat16),
        sine.reshape(FRAMES, KEEP).astype(jnp.bfloat16),
    )


def on_device(signal, pair_band, pair_offset, pair_owner):
    channels = signal.shape[0]
    stride_count = BANDS // HOP
    frames_dev = signal.shape[1] // HOP
    blocks = lax.axis_size("tm")
    bank_table = bank_matrix(BANDS)
    sample_tail = passed_along(signal[:, : BANDS - HOP], "tm", -1)
    records = jnp.concatenate([signal, sample_tail], axis=1)
    pieces = records.reshape(channels, frames_dev + stride_count - 1, HOP)
    framed = jnp.concatenate(
        [pieces[:, part_index : part_index + frames_dev, :] for part_index in range(stride_count)],
        axis=2,
    )
    spectra = jnp.einsum(
        "cmn,nk->ckm", framed, bank_table, preferred_element_type=jnp.float32
    ).astype(jnp.bfloat16)
    spectra = spectra.reshape(channels, 2, BANDS, frames_dev)

    bands_all = lax.all_gather(pair_band[0], "tm", axis=1, tiled=False)
    offsets_all = lax.all_gather(pair_offset[0], "tm", axis=1, tiled=False)
    pairs = bands_all.shape[2]
    band_first = bands_all.reshape(channels, blocks * pairs)
    offset = offsets_all.reshape(channels, blocks * pairs)
    positions = jnp.arange(BANDS, dtype=jnp.int32)
    pick_first = (band_first[..., None] == positions).astype(jnp.bfloat16)
    pick_second = ((band_first + offset)[..., None] == positions).astype(jnp.bfloat16)
    first = jnp.einsum("crb,cpbm->crpm", pick_first, spectra, preferred_element_type=jnp.float32)
    second = jnp.einsum("crb,cpbm->crpm", pick_second, spectra, preferred_element_type=jnp.float32)
    real_part = first[:, :, 0] * second[:, :, 0] + first[:, :, 1] * second[:, :, 1]
    imag_part = first[:, :, 1] * second[:, :, 0] - first[:, :, 0] * second[:, :, 1]

    moment = lax.axis_index("tm") * frames_dev + jnp.arange(frames_dev, dtype=jnp.int32)
    shift_bins = (jnp.arange(1, DMAX + 1, dtype=jnp.int32) * (HOP * FRAMES // BANDS) - KEEP // 2) % FRAMES
    phase_cos, phase_sin = turn_table(shift_bins, moment)
    cosine = jnp.zeros(offset.shape + (frames_dev,), jnp.float32)
    sine = jnp.zeros(offset.shape + (frames_dev,), jnp.float32)
    for index in range(DMAX):
        chosen = (offset == index + 1)[..., None]
        cosine = jnp.where(chosen, phase_cos[index], cosine)
        sine = jnp.where(chosen, phase_sin[index], sine)
    demod_re = (real_part * cosine + imag_part * sine).astype(jnp.bfloat16)
    demod_im = (imag_part * cosine - real_part * sine).astype(jnp.bfloat16)
    demod = jnp.stack([demod_re, demod_im], axis=0)
    demod = demod.reshape(2, channels, blocks, pairs, frames_dev).transpose(0, 1, 3, 2, 4)
    arrived = lax.all_to_all(demod, "tm", split_axis=3, concat_axis=3, tiled=True)
    rows = channels * pairs
    arrived = arrived.reshape(2 * rows, blocks * frames_dev)

    cosine_table, sine_table = fourier_tables()
    with_cos = jnp.dot(arrived, cosine_table, preferred_element_type=jnp.float32)
    with_sin = jnp.dot(arrived, sine_table, preferred_element_type=jnp.float32)
    corr_re = with_cos[:rows] + with_sin[rows:]
    corr_im = with_cos[rows:] - with_sin[:rows]
    correlation = jnp.concatenate([corr_re, corr_im], axis=1).astype(jnp.bfloat16)

    owner = pair_owner[0, :, :, 0].reshape(-1)
    groups = lax.axis_size("chan")
    capacity = max(2, 3 * owner.shape[0] // groups)
    hits = (owner[:, None] == jnp.arange(groups, dtype=jnp.int32)[None, :]).astype(jnp.int32)
    rank = jnp.sum((jnp.cumsum(hits, axis=0) - 1) * hits, axis=1)
    slot = owner * capacity + rank
    placing = (jnp.arange(groups * capacity, dtype=jnp.int32)[:, None] == slot[None, :]).astype(
        jnp.bfloat16
    )
    outgoing = jnp.dot(placing, correlation, preferred_element_type=jnp.float32).astype(
        jnp.bfloat16
    )
    outgoing = outgoing.reshape(groups, capacity, 2 * KEEP)
    arrived = lax.all_to_all(outgoing, "chan", split_axis=0, concat_axis=0, tiled=True)
    return arrived.reshape(1, 1, groups, capacity, 2 * KEEP)


def solution(mesh):
    return jax.shard_map(
        on_device,
        mesh=mesh,
        in_specs=(
            P("chan", "tm"),
            P("tm", "chan", None),
            P("tm", "chan", None),
            P("tm", "chan", None, None),
        ),
        out_specs=P("tm", "chan", None, None, None),
        check_vma=False,
    )
```

time: 261 us -> 192 us (0.74)
  blocking collectives: 86.6 us -> 132 us
  waiting for transfers between devices: 52.8 us -> 10.2 us
  other arithmetic: 66 us -> 23.5 us
  local copies, waits for them, and re-layouts: 30.2 us -> 8.5 us
  starting transfers between devices: 11.8 us -> 5.97 us
    another operation x10 -> x4, other arithmetic: 64.7 us -> 2.3 us
    all_to_all x1, waiting for transfers between devices: 50.2 us -> 10.2 us  [on_device(): lax.all_to_all(demod, 'tm', split_axis=3, concat_axis=3, tiled=True)]
    all_gather x0 -> x2, blocking collectives: none -> 38.6 us  [the longest x1 22.4 us: on_device(): bands_all = lax.all_gather(pair_band[0], 'tm', axis=1, tiled=False)]
    convert_element_type x0 -> x3, other arithmetic: none -> 15.3 us  [the longest x1 5.25 us: fourier_tables(): cosine.reshape(FRAMES, KEEP).astype(jnp.bfloat16)]
    all_to_all x2 -> x1, local copies, waits for them, and re-layouts: 16.3 us -> 2.43 us  [on_device(): lax.all_to_all(demod, 'tm', split_axis=3, concat_axis=3, tiled=True)]
    all_to_all x1, blocking collectives: 86.6 us -> 93.8 us  [on_device(): lax.all_to_all(outgoing, 'chan', split_axis=0, concat_axis=0, tiled=True)]
    reshape x1 -> x0, local copies, waits for them, and re-layouts: 6.3 us -> none  [on_device(): spectra = spectra.reshape(channels, 2, BANDS, frames_dev)]
    all_to_all x1, starting transfers between devices: 9.03 us -> 4.69 us  [on_device(): lax.all_to_all(demod, 'tm', split_axis=3, concat_axis=3, tiled=True)]
  transfers between devices with their start and end apart: 3 -> 2, of which waited for: 2 -> 1; matrix products, arithmetic and copies ran while one was open for 18% -> 6% of each run, Pallas kernels for 0% -> 0%
where the time goes in v1:
time: 192 us
  blocking collectives  132 us (69%)
  other arithmetic  23.5 us (12%)
  matrix products  10.6 us (6%)
  waiting for transfers between devices  10.2 us (5%)
  local copies, waits for them, and re-layouts  8.5 us (4%)
  starting transfers between devices  5.97 us (3%)
    all_to_all x1, blocking collectives, on_device(): lax.all_to_all(outgoing, 'chan', split_axis=0, concat_axis=0, tiled=True)  93.8 us
    all_gather x1, blocking collectives, on_device(): bands_all = lax.all_gather(pair_band[0], 'tm', axis=1, tiled=False)  22.4 us
    all_gather x1, blocking collectives, on_device(): offsets_all = lax.all_gather(pair_offset[0], 'tm', axis=1, tiled=False)  16.3 us
    all_to_all x1, waiting for transfers between devices, on_device(): lax.all_to_all(demod, 'tm', split_axis=3, concat_axis=3, tiled=True)  10.2 us
    convert_element_type x1, other arithmetic, fourier_tables(): cosine.reshape(FRAMES, KEEP).astype(jnp.bfloat16)  5.25 us
    convert_element_type x1, other arithmetic, on_device(): demod_re = (real_part * cosine + imag_part * sine).astype(jnp.bfloat16)  5.04 us
    convert_element_type x1, other arithmetic, on_device(): demod_im = (imag_part * cosine - real_part * sine).astype(jnp.bfloat16)  5.04 us
    all_to_all x1, starting transfers between devices, on_device(): lax.all_to_all(demod, 'tm', split_axis=3, concat_axis=3, tiled=True)  4.69 us
  transfers between devices with their start and end apart: 2, of which 1 were waited for; matrix products, arithmetic and copies ran while one was open for 6% of the time, Pallas kernels for 0%

profile of v1, /device:TPU:1, one launch (start us, length us, event | category | flops | bytes accessed | tf_op | source)
XLA Modules:
  0.0 191.5 jit_solution(595436357364433193)
XLA Ops:
  0.7 1.3 collective-permute-start
  2.1 22.4 %all-gather = s32[1,32,128]{1,2,0:T(8,128)S(1)} all-gather(s32[1,32,8]{1,2,0:T(8,128)} %param.5), channel_id=2, replica_groups=mesh['chan'=16,'tm'=16] {'tm'}, dimensions={2}, use_global_device_ids=true | all-gather | bytes 17408 | tf_op jit(solution)/shard_map/all_gather | solution.py:73
  24.5 16.3 %all-gather.1 = s32[1,32,128]{1,2,0:T(8,128)S(1)} all-gather(s32[1,32,8]{1,2,0:T(8,128)} %param.6), channel_id=3, replica_groups=mesh['chan'=16,'tm'=16] {'tm'}, dimensions={2}, use_global_device_ids=true | all-gather | bytes 17408 | tf_op jit(solution)/shard_map/all_gather | solution.py:74
  40.8 1.1 multiply_convert_fusion.2
  43.7 1.1 pad_maximum_fusion
  44.8 0.8 reshape.504
  45.6 0.9 fusion.63
  46.5 2.1 %convolution_convert_fusion.1 = bf16[512,32,128]{2,0,1:T(8,128)(2,1)S(1)} fusion(bf16[32,128,64]{2,1,0:T(8,128)(2,1)S(1)} %get-tuple-element.10, bf16[32,128,64]{2,1,0:T(8,128)(2,1)S(1)} %get-tuple-element.11, bf16[32,128,64]{2,1,0:T(8,128)(2,1)S(1)} %get-tuple-element.12, bf16[32,128,64]{2,1,0:T(8,128)(2,1)S(1)} %get-tuple-element.9, ...), kind=kOutput, calls=%fused_computation.9 | convolution fusion | flops 1084751872 | bytes 6553600 | tf_op jit(solution)/shard_map/cmn,nk->ckm/dot_general | solution.py:68
  48.6 1.4 fusion.4
  50.0 1.4 fusion.1
  51.5 1.3 add_bitcast_fusion
  52.7 5.0 %add_convert_fusion = bf16[1,32,16,8,128]{4,3,1,0,2:T(8,128)(2,1)S(1)} fusion(f32[1,32,16,8,128]{4,3,2,1,0:T(8,128)S(1)} %get-tuple-element.6, f32[1,32,16,8,128]{4,3,2,1,0:T(8,128)S(1)} %get-tuple-element.5, f32[128]{0:T(128)S(1)} %get-tuple-element.32, f32[128]{0:T(128)S(1)} %get-tuple-element.33, f32[128]{0:T(128)S(1)} %get-tuple-element.34, ...), kind=kLoop, calls=%fused_computation.23 | loop fusion | flops 10485760 | bytes 5283840 | tf_op jit(solution)/shard_map/convert_element_type | solution.py:95
  57.8 5.0 %subtract_convert_fusion = bf16[1,32,16,8,128]{4,3,1,0,2:T(8,128)(2,1)S(1)} fusion(f32[1,32,16,8,128]{4,3,2,1,0:T(8,128)S(1)} %get-tuple-element.6, f32[1,32,16,8,128]{4,3,2,1,0:T(8,128)S(1)} %get-tuple-element.5, f32[128]{0:T(128)S(1)} %get-tuple-element.32, f32[128]{0:T(128)S(1)} %get-tuple-element.33, f32[128]{0:T(128)S(1)} %get-tuple-element.34, ...), kind=kLoop, calls=%fused_computation.22 | loop fusion | flops 10485760 | bytes 5283840 | tf_op jit(solution)/shard_map/convert_element_type | solution.py:96
  62.8 1.5 maximum_bitcast_fusion
  64.3 4.7 %all-to-all-start = ((bf16[2,32,8,16,128]{4,2,1,0,3:T(8,128)(2,1)}), bf16[2,32,8,16,128]{4,2,1,0,3:T(8,128)(2,1)S(1)}, u32[]{:S(2)}, u32[]{:S(2)}) async-start(bf16[2,32,8,16,128]{4,2,1,0,3:T(8,128)(2,1)} %maximum_bitcast_fusion), calls=%async_computation | async-start | bytes 4194304 | tf_op jit(solution)/shard_map/all_to_all | solution.py:99
  70.8 1.1 fusion.47
  71.9 5.2 %multiply_convert_fusion.1 = (bf16[64,32,1024]{2,1,0:T(8,128)(2,1)}, bf16[64,32,1024]{2,1,0:T(8,128)(2,1)}) fusion(f32[32,1024]{1,0:T(8,128)S(1)} %get-tuple-element.43, f32[64,1024]{1,0:T(8,128)S(1)} %get-tuple-element.42, f32[32,1024]{1,0:T(8,128)S(1)} %get-tuple-element.44, f32[64,1024]{1,0:T(8,128)S(1)} %get-tuple-element.41), kind=kLoop, calls=%fused_computation.1 | loop fusion | flops 20971520 | bytes 9175040 | tf_op jit(solution)/shard_map/convert_element_type | solution.py:50
  77.1 10.2 %all-to-all-done = bf16[2,32,8,16,128]{4,2,1,0,3:T(8,128)(2,1)S(1)} async-done(((bf16[2,32,8,16,128]{4,2,1,0,3:T(8,128)(2,1)}), bf16[2,32,8,16,128]{4,2,1,0,3:T(8,128)(2,1)S(1)}, u32[]{:S(2)}, u32[]{:S(2)}) %all-to-all-start) | async-done | bytes 2097184 | tf_op jit(solution)/shard_map/all_to_all | solution.py:99
  87.3 2.4 %copy.62 = bf16[2,32,8,16,128]{4,3,2,1,0:T(8,128)(2,1)S(1)} copy(bf16[2,32,8,16,128]{4,2,1,0,3:T(8,128)(2,1)S(1)} %all-to-all-done) | data formatting | bytes 4194304 | tf_op jit(solution)/shard_map/all_to_all | solution.py:99
  89.8 2.4 %fusion.8 = f32[512,1024]{1,0:T(8,128)S(1)} fusion(bf16[2048,1024]{1,0:T(8,128)(2,1)S(1)} %bitcast.117, bf16[64,8,16,128]{3,2,1,0:T(8,128)(2,1)S(1)} %bitcast.118), kind=kOutput, calls=%fused_computation.12 | convolution fusion | flops 2147483648 | bytes 8388608 | tf_op jit(solution)/shard_map/dot_general | solution.py:104
  92.2 2.4 %fusion.6 = f32[512,1024]{1,0:T(8,128)S(1)} fusion(bf16[2048,1024]{1,0:T(8,128)(2,1)S(1)} %bitcast.116, bf16[64,8,16,128]{3,2,1,0:T(8,128)(2,1)S(1)} %bitcast.119), kind=kOutput, calls=%fused_computation.10 | convolution fusion | flops 2147483648 | bytes 8388608 | tf_op jit(solution)/shard_map/dot_general | solution.py:105
  95.1 1.0 convolution_convert_fusion
  96.1 93.8 %all_to_all.10 = bf16[16,48,2048]{2,1,0:T(8,128)(2,1)S(1)} all-to-all(bf16[16,48,2048]{2,1,0:T(8,128)(2,1)S(1)} %bitcast.114), channel_id=1, replica_groups=mesh['chan'=16,'tm'=16] {'chan'}, dimensions={0} | all-to-all | bytes 6291456 | tf_op jit(solution)/shard_map/all_to_all | solution.py:123
  189.8 1.7 copy.81
  (39 shorter events, 4.8 us)
Async XLA Ops:
  0.7 43.0 %collective-permute-start = (bf16[32,192]{1,0:T(8,128)(2,1)S(1)}, bf16[32,192]{1,0:T(8,128)(2,1)S(1)}, u32[]{:S(2)}, u32[]{:S(2)}) collective-permute-start(bf16[32,192]{1,0:T(8,128)(2,1)S(1)} %slice.99), channel_id=1, source_target_pairs={{1,0},{2,1},{3,2},{4,3},{5,4},{6,5},{7,6},{8,7},{9,8},{10,9},{11,1... | collective-permute-start | bytes 36872 | tf_op jit(solution)/shard_map/ppermute | solution.py:18
  64.3 4.7 %copy-start.2 = (s32[1,32,8,1]{1,3,2,0:T(1,128)S(1)}, s32[1,32,8,1]{1,3,2,0:T(1,128)}, u32[]{:S(2)}) copy-start(s32[1,32,8,1]{1,3,2,0:T(1,128)} %param.7) | copy-start | bytes 3076
  64.3 23.0 %all-to-all-start = ((bf16[2,32,8,16,128]{4,2,1,0,3:T(8,128)(2,1)}), bf16[2,32,8,16,128]{4,2,1,0,3:T(8,128)(2,1)S(1)}, u32[]{:S(2)}, u32[]{:S(2)}) async-start(bf16[2,32,8,16,128]{4,2,1,0,3:T(8,128)(2,1)} %maximum_bitcast_fusion), calls=%async_computation | async-start | bytes 4194304 | tf_op jit(solution)/shard_map/all_to_all | solution.py:99
  87.3 2.4 %copy-start.1 = (bf16[64,32,1024]{2,1,0:T(8,128)(2,1)S(1)}, bf16[64,32,1024]{2,1,0:T(8,128)(2,1)}, u32[]{:S(2)}) copy-start(bf16[64,32,1024]{2,1,0:T(8,128)(2,1)} %get-tuple-element.13) | copy-start | bytes 12582916
  89.8 2.4 %copy-start = (bf16[64,32,1024]{2,1,0:T(8,128)(2,1)S(1)}, bf16[64,32,1024]{2,1,0:T(8,128)(2,1)}, u32[]{:S(2)}) copy-start(bf16[64,32,1024]{2,1,0:T(8,128)(2,1)} %get-tuple-element.14) | copy-start | bytes 12582916

commit v2 on v1

--- a/solution.py
+++ b/solution.py
@@ -70,8 +70,11 @@
     ).astype(jnp.bfloat16)
     spectra = spectra.reshape(channels, 2, BANDS, frames_dev)
 
-    bands_all = lax.all_gather(pair_band[0], "tm", axis=1, tiled=False)
-    offsets_all = lax.all_gather(pair_offset[0], "tm", axis=1, tiled=False)
+    local_tables = jnp.stack([pair_band[0], pair_offset[0]], axis=0)
+    spread = jnp.broadcast_to(local_tables[None], (blocks,) + local_tables.shape)
+    tables = lax.all_to_all(spread, "tm", split_axis=0, concat_axis=0, tiled=True)
+    bands_all = tables[:, 0].transpose(1, 0, 2)
+    offsets_all = tables[:, 1].transpose(1, 0, 2)
     pairs = bands_all.shape[2]
     band_first = bands_all.reshape(channels, blocks * pairs)
     offset = offsets_all.reshape(channels, blocks * pairs)
@@ -84,14 +87,17 @@
     imag_part = first[:, :, 1] * second[:, :, 0] - first[:, :, 0] * second[:, :, 1]
 
     moment = lax.axis_index("tm") * frames_dev + jnp.arange(frames_dev, dtype=jnp.int32)
-    shift_bins = (jnp.arange(1, DMAX + 1, dtype=jnp.int32) * (HOP * FRAMES // BANDS) - KEEP // 2) % FRAMES
-    phase_cos, phase_sin = turn_table(shift_bins, moment)
-    cosine = jnp.zeros(offset.shape + (frames_dev,), jnp.float32)
-    sine = jnp.zeros(offset.shape + (frames_dev,), jnp.float32)
-    for index in range(DMAX):
-        chosen = (offset == index + 1)[..., None]
-        cosine = jnp.where(chosen, phase_cos[index], cosine)
-        sine = jnp.where(chosen, phase_sin[index], sine)
+    step = math.gcd(HOP * FRAMES // BANDS, KEEP // 2, FRAMES)
+    levels = FRAMES // step
+    level_cos, level_sin = turn_table(jnp.arange(levels, dtype=jnp.int32), jnp.full((1,), step, jnp.int32))
+    shift_bins = (offset * (HOP * FRAMES // BANDS) - KEEP // 2) % FRAMES
+    level = (shift_bins[..., None] // step) * moment % levels
+    cosine = jnp.full(level.shape, level_cos[0, 0])
+    sine = jnp.full(level.shape, level_sin[0, 0])
+    for index in range(1, levels):
+        chosen = level == index
+        cosine = jnp.where(chosen, level_cos[index, 0], cosine)
+        sine = jnp.where(chosen, level_sin[index, 0], sine)
     demod_re = (real_part * cosine + imag_part * sine).astype(jnp.bfloat16)
     demod_im = (imag_part * cosine - real_part * sine).astype(jnp.bfloat16)
     demod = jnp.stack([demod_re, demod_im], axis=0)

time: 192 us -> 175 us (0.911)
  blocking collectives: 132 us -> 86.6 us
  starting transfers between devices: 5.97 us -> 16.6 us
  matrix products: 10.6 us -> 18.1 us
  waiting for transfers between devices: 10.2 us -> 17.7 us
    all_gather x2 -> x0, blocking collectives: 38.6 us -> none  [the longest x1 22.4 us: on_device(): bands_all = lax.all_gather(pair_band[0], 'tm', axis=1, tiled=False)]
    all_to_all x0 -> x1, starting transfers between devices: none -> 8.47 us  [on_device(): lax.all_to_all(spread, 'tm', split_axis=0, concat_axis=0, tiled=True)]
    all_to_all x1, waiting for transfers between devices: 10.2 us -> 17.7 us  [on_device(): lax.all_to_all(demod, 'tm', split_axis=3, concat_axis=3, tiled=True)]
    all_to_all x1, blocking collectives: 93.8 us -> 86.6 us  [on_device(): lax.all_to_all(outgoing, 'chan', split_axis=0, concat_axis=0, tiled=True)]
    convert_element_type x1 -> x0, other arithmetic: 5.04 us -> none  [on_device(): demod_im = (imag_part * cosine - real_part * sine).astype(jnp.bfloat16)]
    dot_general x1, matrix products: 1.44 us -> 5.31 us  [on_device(): jnp.einsum('crb,cpbm->crpm', pick_first, spectra, preferred_element_type=...]
    add x1, other arithmetic: 1.26 us -> 4.34 us  [on_device(): first[:, :, 0] * second[:, :, 0] + first[:, :, 1] * second[:, :, 1]]
    convert_element_type x1, other arithmetic: 5.04 us -> 7.39 us  [on_device(): demod_re = (real_part * cosine + imag_part * sine).astype(jnp.bfloat16)]
  transfers between devices with their start and end apart: 2 -> 3, of which waited for: 1 -> 1; matrix products, arithmetic and copies ran while one was open for 6% -> 11% of each run, Pallas kernels for 0% -> 0%
where the time goes in v2:
time: 175 us; the launch traced here: 174 us
  blocking collectives  86.6 us (49%)
  other arithmetic  25.3 us (14%)
  matrix products  18.1 us (10%)
  waiting for transfers between devices  17.7 us (10%)
  starting transfers between devices  16.6 us (9%)
  local copies, waits for them, and re-layouts  9.78 us (6%)
    all_to_all x1, blocking collectives, on_device(): lax.all_to_all(outgoing, 'chan', split_axis=0, concat_axis=0, tiled=True)  86.6 us
    all_to_all x1, waiting for transfers between devices, on_device(): lax.all_to_all(demod, 'tm', split_axis=3, concat_axis=3, tiled=True)  17.7 us
    all_to_all x1, starting transfers between devices, on_device(): lax.all_to_all(spread, 'tm', split_axis=0, concat_axis=0, tiled=True)  8.47 us
    convert_element_type x1, other arithmetic, on_device(): demod_re = (real_part * cosine + imag_part * sine).astype(jnp.bfloat16)  7.39 us
    all_to_all x1, starting transfers between devices, on_device(): lax.all_to_all(demod, 'tm', split_axis=3, concat_axis=3, tiled=True)  6.81 us
    dot_general x1, matrix products, on_device(): jnp.einsum('crb,cpbm->crpm', pick_first, spectra, preferred_element_type=...  5.31 us
    convert_element_type x1, other arithmetic, fourier_tables(): cosine.reshape(FRAMES, KEEP).astype(jnp.bfloat16)  5.25 us
    add x1, other arithmetic, on_device(): first[:, :, 0] * second[:, :, 0] + first[:, :, 1] * second[:, :, 1]  4.34 us
  transfers between devices with their start and end apart: 3, of which 1 were waited for; matrix products, arithmetic and copies ran while one was open for 11% of the time, Pallas kernels for 0%

profile of v2, /device:TPU:1, one launch (start us, length us, event | category | flops | bytes accessed | tf_op | source)
XLA Modules:
  0.0 174.2 jit_solution(8002819625001822888)
XLA Ops:
  0.7 1.3 collective-permute-start
  2.7 0.7 reshape.533
  3.5 8.5 %all-to-all-start = ((s32[16,1,512]{2,1,0:T(1,128)}), s32[16,1,512]{2,1,0:T(1,128)S(1)}, u32[]{:S(2)}, u32[]{:S(2)}) async-start(s32[16,1,512]{2,1,0:T(1,128)} %reshape.533), calls=%async_computation | async-start | bytes 65536 | tf_op jit(solution)/shard_map/all_to_all | solution.py:75
  13.3 1.1 multiply_convert_fusion.2
  14.5 1.1 pad_maximum_fusion
  15.6 0.8 reshape.523
  16.4 0.9 fusion.67
  17.3 4.0 %convolution_convert_fusion.1 = bf16[512,32,128]{2,0,1:T(8,128)(2,1)} fusion(bf16[32,128,64]{2,1,0:T(8,128)(2,1)S(1)} %get-tuple-element.12, bf16[32,128,64]{2,1,0:T(8,128)(2,1)S(1)} %get-tuple-element.13, bf16[32,128,64]{2,1,0:T(8,128)(2,1)S(1)} %get-tuple-element.14, bf16[32,128,64]{2,1,0:T(8,128)(2,1)S(1)} %get-tuple-element.11, ...), kind=kOutput, calls=%fused_computation.14 | convolution fusion | flops 1084751872 | bytes 6553600 | tf_op jit(solution)/shard_map/cmn,nk->ckm/dot_general | solution.py:68
  21.8 0.7 reduce.2
  22.9 5.3 %fusion.1 = f32[32,128,2,128]{3,1,2,0:T(8,128)} fusion(bf16[32,2,256,128]{3,2,1,0:T(8,128)(2,1)} %bitcast.92, s32[32,128]{1,0:T(8,128)S(1)} %copy.25), kind=kOutput, calls=%fused_computation.5 | convolution fusion | flops 537919488 | bytes 8404992 | tf_op jit(solution)/shard_map/crb,cpbm->crpm/dot_general | solution.py:84
  28.2 3.0 %fusion.4 = f32[32,128,2,128]{3,1,2,0:T(8,128)} fusion(bf16[32,2,256,128]{3,2,1,0:T(8,128)(2,1)S(1)} %bitcast.93, s32[32,128]{1,0:T(8,128)S(1)} %copy.26), kind=kOutput, calls=%fused_computation.7 | convolution fusion | flops 537919488 | bytes 8404992 | tf_op jit(solution)/shard_map/crb,cpbm->crpm/dot_general | solution.py:85
  31.4 4.3 %add_bitcast_fusion = (f32[1,32,16,8,128]{4,3,2,1,0:T(8,128)S(1)}, f32[1,32,16,8,128]{4,3,2,1,0:T(8,128)S(1)}) fusion(f32[32,128,2,128]{3,1,2,0:T(8,128)} %fusion.4, f32[32,128,2,128]{3,1,2,0:T(8,128)} %fusion.1), kind=kLoop, calls=%fused_computation.33 | loop fusion | flops 3145728 | bytes 12582912 | tf_op jit(solution)/shard_map/add | solution.py:86
  35.7 7.4 %add_convert_fusion = (bf16[1,32,16,8,128]{4,3,1,0,2:T(8,128)(2,1)S(1)}, bf16[1,32,16,8,128]{4,3,1,0,2:T(8,128)(2,1)S(1)}) fusion(f32[1,32,16,8,128]{4,3,2,1,0:T(8,128)S(1)} %get-tuple-element.6, f32[1,32,16,8,128]{4,3,2,1,0:T(8,128)S(1)} %get-tuple-element.5, f32[]{:T(128)} %bitcast.27, f32[]{:T(128)} %bitcast.26, f32[]{:T(128)} %bitcast.25, f32[]{:T(128)} %bitcast.24, ...), kind=kLoop, calls=%fused_computation.29 | loop fusion | flops 15204352 | bytes 6308384 | tf_op jit(solution)/shard_map/convert_element_type | solution.py:101
  43.1 1.5 maximum_bitcast_fusion
  44.6 6.8 %all-to-all-start.1 = ((bf16[2,32,8,16,128]{4,2,1,0,3:T(8,128)(2,1)}), bf16[2,32,8,16,128]{4,2,1,0,3:T(8,128)(2,1)S(1)}, u32[]{:S(2)}, u32[]{:S(2)}) async-start(bf16[2,32,8,16,128]{4,2,1,0,3:T(8,128)(2,1)} %maximum_bitcast_fusion), calls=%async_computation.1 | async-start | bytes 4194304 | tf_op jit(solution)/shard_map/all_to_all | solution.py:105
  53.2 1.1 fusion.48
  54.3 5.2 %multiply_convert_fusion.1 = (bf16[64,32,1024]{2,1,0:T(8,128)(2,1)}, bf16[64,32,1024]{2,1,0:T(8,128)(2,1)}) fusion(f32[32,1024]{1,0:T(8,128)S(1)} %get-tuple-element.27, f32[64,1024]{1,0:T(8,128)S(1)} %get-tuple-element.26, f32[32,1024]{1,0:T(8,128)S(1)} %get-tuple-element.28, f32[64,1024]{1,0:T(8,128)S(1)} %get-tuple-element.25), kind=kLoop, calls=%fused_computation.1 | loop fusion | flops 20971520 | bytes 9175040 | tf_op jit(solution)/shard_map/convert_element_type | solution.py:50
  59.5 17.7 %all-to-all-done.1 = bf16[2,32,8,16,128]{4,2,1,0,3:T(8,128)(2,1)S(1)} async-done(((bf16[2,32,8,16,128]{4,2,1,0,3:T(8,128)(2,1)}), bf16[2,32,8,16,128]{4,2,1,0,3:T(8,128)(2,1)S(1)}, u32[]{:S(2)}, u32[]{:S(2)}) %all-to-all-start.1) | async-done | bytes 2097184 | tf_op jit(solution)/shard_map/all_to_all | solution.py:105
  77.2 2.4 %copy.32 = bf16[2,32,8,16,128]{4,3,2,1,0:T(8,128)(2,1)S(1)} copy(bf16[2,32,8,16,128]{4,2,1,0,3:T(8,128)(2,1)S(1)} %all-to-all-done.1) | data formatting | bytes 4194304 | tf_op jit(solution)/shard_map/all_to_all | solution.py:105
  79.6 2.4 %fusion.9 = f32[512,1024]{1,0:T(8,128)S(1)} fusion(bf16[2048,1024]{1,0:T(8,128)(2,1)S(1)} %bitcast.97, bf16[64,8,16,128]{3,2,1,0:T(8,128)(2,1)S(1)} %bitcast.98), kind=kOutput, calls=%fused_computation.18 | convolution fusion | flops 2147483648 | bytes 8388608 | tf_op jit(solution)/shard_map/dot_general | solution.py:110
  82.0 2.4 %fusion.7 = f32[512,1024]{1,0:T(8,128)S(1)} fusion(bf16[2048,1024]{1,0:T(8,128)(2,1)S(1)} %bitcast.96, bf16[64,8,16,128]{3,2,1,0:T(8,128)(2,1)S(1)} %bitcast.99), kind=kOutput, calls=%fused_computation.16 | convolution fusion | flops 2147483648 | bytes 8388608 | tf_op jit(solution)/shard_map/dot_general | solution.py:111
  84.9 1.0 convolution_convert_fusion
  85.9 86.6 %all_to_all.15 = bf16[16,48,2048]{2,1,0:T(8,128)(2,1)S(1)} all-to-all(bf16[16,48,2048]{2,1,0:T(8,128)(2,1)S(1)} %bitcast.94), channel_id=1, replica_groups=mesh['chan'=16,'tm'=16] {'chan'}, dimensions={0} | all-to-all | bytes 6291456 | tf_op jit(solution)/shard_map/all_to_all | solution.py:129
  172.5 1.7 copy.51
  (41 shorter events, 6.0 us)
Async XLA Ops:
  0.7 13.8 %collective-permute-start = (bf16[32,192]{1,0:T(8,128)(2,1)S(1)}, bf16[32,192]{1,0:T(8,128)(2,1)S(1)}, u32[]{:S(2)}, u32[]{:S(2)}) collective-permute-start(bf16[32,192]{1,0:T(8,128)(2,1)S(1)} %slice.82), channel_id=1, source_target_pairs={{1,0},{2,1},{3,2},{4,3},{5,4},{6,5},{7,6},{8,7},{9,8},{10,9},{11,1... | collective-permute-start | bytes 36872 | tf_op jit(solution)/shard_map/ppermute | solution.py:18
  3.5 17.9 %all-to-all-start = ((s32[16,1,512]{2,1,0:T(1,128)}), s32[16,1,512]{2,1,0:T(1,128)S(1)}, u32[]{:S(2)}, u32[]{:S(2)}) async-start(s32[16,1,512]{2,1,0:T(1,128)} %reshape.533), calls=%async_computation | async-start | bytes 65536 | tf_op jit(solution)/shard_map/all_to_all | solution.py:75
  22.9 5.3 %copy-start = (bf16[512,32,128]{2,0,1:T(8,128)(2,1)S(1)}, bf16[512,32,128]{2,0,1:T(8,128)(2,1)}, u32[]{:S(2)}) copy-start(bf16[512,32,128]{2,0,1:T(8,128)(2,1)} %convolution_convert_fusion.1) | copy-start | bytes 12582916
  44.6 6.8 %copy-start.3 = (s32[1,32,8,1]{1,3,2,0:T(1,128)S(1)}, s32[1,32,8,1]{1,3,2,0:T(1,128)}, u32[]{:S(2)}) copy-start(s32[1,32,8,1]{1,3,2,0:T(1,128)} %param.7) | copy-start | bytes 3076
  44.6 32.6 %all-to-all-start.1 = ((bf16[2,32,8,16,128]{4,2,1,0,3:T(8,128)(2,1)}), bf16[2,32,8,16,128]{4,2,1,0,3:T(8,128)(2,1)S(1)}, u32[]{:S(2)}, u32[]{:S(2)}) async-start(bf16[2,32,8,16,128]{4,2,1,0,3:T(8,128)(2,1)} %maximum_bitcast_fusion), calls=%async_computation.1 | async-start | bytes 4194304 | tf_op jit(solution)/shard_map/all_to_all | solution.py:105
  77.2 2.4 %copy-start.2 = (bf16[64,32,1024]{2,1,0:T(8,128)(2,1)S(1)}, bf16[64,32,1024]{2,1,0:T(8,128)(2,1)}, u32[]{:S(2)}) copy-start(bf16[64,32,1024]{2,1,0:T(8,128)(2,1)} %get-tuple-element.15) | copy-start | bytes 12582916
  79.6 2.4 %copy-start.1 = (bf16[64,32,1024]{2,1,0:T(8,128)(2,1)S(1)}, bf16[64,32,1024]{2,1,0:T(8,128)(2,1)}, u32[]{:S(2)}) copy-start(bf16[64,32,1024]{2,1,0:T(8,128)(2,1)} %get-tuple-element.16) | copy-start | bytes 12582916

commit v3 on v2

--- a/solution.py
+++ b/solution.py
@@ -81,8 +81,14 @@
     positions = jnp.arange(BANDS, dtype=jnp.int32)
     pick_first = (band_first[..., None] == positions).astype(jnp.bfloat16)
     pick_second = ((band_first + offset)[..., None] == positions).astype(jnp.bfloat16)
-    first = jnp.einsum("crb,cpbm->crpm", pick_first, spectra, preferred_element_type=jnp.float32)
-    second = jnp.einsum("crb,cpbm->crpm", pick_second, spectra, preferred_element_type=jnp.float32)
+    picked = jnp.einsum(
+        "crb,cpbm->crpm",
+        jnp.concatenate([pick_first, pick_second], axis=1),
+        spectra,
+        preferred_element_type=jnp.bfloat16,
+    ).astype(jnp.float32)
+    first = picked[:, : blocks * pairs]
+    second = picked[:, blocks * pairs :]
     real_part = first[:, :, 0] * second[:, :, 0] + first[:, :, 1] * second[:, :, 1]
     imag_part = first[:, :, 1] * second[:, :, 0] - first[:, :, 0] * second[:, :, 1]
 

time: 175 us -> 170 us (0.971)
  matrix products: 18.1 us -> 12.8 us
    dot_general x2 -> x1, matrix products: 8.34 us -> 3.08 us  [on_device(): jnp.einsum('crb,cpbm->crpm', jnp.concatenate([pick_first, pick_second], a...]
    add x1, other arithmetic: 4.34 us -> 2.18 us  [on_device(): first[:, :, 0] * second[:, :, 0] + first[:, :, 1] * second[:, :, 1]]
where the time goes in v3:
time: 170 us
  blocking collectives  86.6 us (51%)
  other arithmetic  26 us (15%)
  waiting for transfers between devices  17.7 us (10%)
  starting transfers between devices  16.6 us (10%)
  matrix products  12.8 us (8%)
  local copies, waits for them, and re-layouts  9.77 us (6%)
    all_to_all x1, blocking collectives, on_device(): lax.all_to_all(outgoing, 'chan', split_axis=0, concat_axis=0, tiled=True)  86.6 us
    all_to_all x1, waiting for transfers between devices, on_device(): lax.all_to_all(demod, 'tm', split_axis=3, concat_axis=3, tiled=True)  17.7 us
    convert_element_type x1, other arithmetic, on_device(): demod_re = (real_part * cosine + imag_part * sine).astype(jnp.bfloat16)  8.81 us
    all_to_all x1, starting transfers between devices, on_device(): lax.all_to_all(spread, 'tm', split_axis=0, concat_axis=0, tiled=True)  8.47 us
    all_to_all x1, starting transfers between devices, on_device(): lax.all_to_all(demod, 'tm', split_axis=3, concat_axis=3, tiled=True)  6.8 us
    convert_element_type x1, other arithmetic, fourier_tables(): cosine.reshape(FRAMES, KEEP).astype(jnp.bfloat16)  5.25 us
    dot_general x1, matrix products, on_device(): jnp.einsum('cmn,nk->ckm', framed, bank_table, preferred_element_type=jnp....  3.99 us
  transfers between devices with their start and end apart: 3, of which 1 were waited for; matrix products, arithmetic and copies ran while one was open for 11% of the time, Pallas kernels for 0%

profile of v3, /device:TPU:1, one launch (start us, length us, event | category | flops | bytes accessed | tf_op | source)
XLA Modules:
  0.0 169.6 jit_solution(11270629347416283704)
XLA Ops:
  0.7 1.3 collective-permute-start
  2.7 0.7 reshape.532
  3.5 8.5 %all-to-all-start = ((s32[16,1,512]{2,1,0:T(1,128)}), s32[16,1,512]{2,1,0:T(1,128)S(1)}, u32[]{:S(2)}, u32[]{:S(2)}) async-start(s32[16,1,512]{2,1,0:T(1,128)} %reshape.532), calls=%async_computation | async-start | bytes 65536 | tf_op jit(solution)/shard_map/all_to_all | solution.py:75
  13.3 1.1 multiply_convert_fusion.2
  14.5 1.1 pad_maximum_fusion
  15.6 0.8 reshape.524
  16.4 0.9 fusion.64
  17.3 4.0 %convolution_convert_fusion.1 = bf16[512,32,128]{2,0,1:T(8,128)(2,1)} fusion(bf16[32,128,64]{2,1,0:T(8,128)(2,1)S(1)} %get-tuple-element.12, bf16[32,128,64]{2,1,0:T(8,128)(2,1)S(1)} %get-tuple-element.13, bf16[32,128,64]{2,1,0:T(8,128)(2,1)S(1)} %get-tuple-element.14, bf16[32,128,64]{2,1,0:T(8,128)(2,1)S(1)} %get-tuple-element.11, ...), kind=kOutput, calls=%fused_computation.14 | convolution fusion | flops 1084751872 | bytes 6553600 | tf_op jit(solution)/shard_map/cmn,nk->ckm/dot_general | solution.py:68
  21.8 0.7 reduce.2
  22.9 1.4 iota_compare_fusion
  24.3 3.1 %fusion.3 = f32[32,256,2,128]{3,1,2,0:T(8,128)S(1)} fusion(bf16[32,2,256,128]{3,2,1,0:T(8,128)(2,1)} %bitcast.90, pred[32,128,256]{2,1,0:T(32,128)(4,1)S(1)} %get-tuple-element.31, pred[32,128,256]{2,1,0:T(32,128)(4,1)S(1)} %get-tuple-element.32), kind=kOutput, calls=%fused_computation.15 | convolution fusion | flops 1077936128 | bytes 14680064 | tf_op jit(solution)/shard_map/crb,cpbm->crpm/dot_general | solution.py:84
  27.4 2.2 %add_bitcast_fusion.4 = (f32[1,32,16,8,128]{4,3,2,1,0:T(8,128)S(1)}, f32[1,32,16,8,128]{4,3,2,1,0:T(8,128)}) fusion(f32[32,256,2,128]{3,1,2,0:T(8,128)S(1)} %fusion.3), kind=kLoop, calls=%fused_computation.34 | loop fusion | flops 3145728 | bytes 12582912 | tf_op jit(solution)/shard_map/add | solution.py:92
  29.7 8.8 %add_convert_fusion = (bf16[1,32,16,8,128]{4,3,1,0,2:T(8,128)(2,1)S(1)}, bf16[1,32,16,8,128]{4,3,1,0,2:T(8,128)(2,1)S(1)}) fusion(f32[1,32,16,8,128]{4,3,2,1,0:T(8,128)} %get-tuple-element.6, f32[1,32,16,8,128]{4,3,2,1,0:T(8,128)S(1)} %get-tuple-element.5, f32[]{:T(128)} %bitcast.24, f32[]{:T(128)} %bitcast.23, f32[]{:T(128)} %bitcast.22, f32[]{:T(128)} %bitcast.21, ...), kind=kLoop, calls=%fused_computation.30 | loop fusion | flops 15204352 | bytes 6308384 | tf_op jit(solution)/shard_map/convert_element_type | solution.py:107
  38.5 1.5 maximum_bitcast_fusion
  40.0 6.8 %all-to-all-start.1 = ((bf16[2,32,8,16,128]{4,2,1,0,3:T(8,128)(2,1)}), bf16[2,32,8,16,128]{4,2,1,0,3:T(8,128)(2,1)S(1)}, u32[]{:S(2)}, u32[]{:S(2)}) async-start(bf16[2,32,8,16,128]{4,2,1,0,3:T(8,128)(2,1)} %maximum_bitcast_fusion), calls=%async_computation.1 | async-start | bytes 4194304 | tf_op jit(solution)/shard_map/all_to_all | solution.py:111
  48.6 1.1 fusion.44
  49.7 5.2 %multiply_convert_fusion.1 = (bf16[64,32,1024]{2,1,0:T(8,128)(2,1)}, bf16[64,32,1024]{2,1,0:T(8,128)(2,1)}) fusion(f32[32,1024]{1,0:T(8,128)S(1)} %get-tuple-element.27, f32[64,1024]{1,0:T(8,128)S(1)} %get-tuple-element.26, f32[32,1024]{1,0:T(8,128)S(1)} %get-tuple-element.28, f32[64,1024]{1,0:T(8,128)S(1)} %get-tuple-element.25), kind=kLoop, calls=%fused_computation.1 | loop fusion | flops 20971520 | bytes 9175040 | tf_op jit(solution)/shard_map/convert_element_type | solution.py:50
  54.9 17.7 %all-to-all-done.1 = bf16[2,32,8,16,128]{4,2,1,0,3:T(8,128)(2,1)S(1)} async-done(((bf16[2,32,8,16,128]{4,2,1,0,3:T(8,128)(2,1)}), bf16[2,32,8,16,128]{4,2,1,0,3:T(8,128)(2,1)S(1)}, u32[]{:S(2)}, u32[]{:S(2)}) %all-to-all-start.1) | async-done | bytes 2097184 | tf_op jit(solution)/shard_map/all_to_all | solution.py:111
  72.6 2.4 %copy.32 = bf16[2,32,8,16,128]{4,3,2,1,0:T(8,128)(2,1)S(1)} copy(bf16[2,32,8,16,128]{4,2,1,0,3:T(8,128)(2,1)S(1)} %all-to-all-done.1) | data formatting | bytes 4194304 | tf_op jit(solution)/shard_map/all_to_all | solution.py:111
  75.0 2.4 %fusion.7 = f32[512,1024]{1,0:T(8,128)S(1)} fusion(bf16[2048,1024]{1,0:T(8,128)(2,1)S(1)} %bitcast.92, bf16[64,8,16,128]{3,2,1,0:T(8,128)(2,1)S(1)} %bitcast.93), kind=kOutput, calls=%fused_computation.19 | convolution fusion | flops 2147483648 | bytes 8388608 | tf_op jit(solution)/shard_map/dot_general | solution.py:116
  77.4 2.4 %fusion.5 = f32[512,1024]{1,0:T(8,128)S(1)} fusion(bf16[2048,1024]{1,0:T(8,128)(2,1)S(1)} %bitcast.91, bf16[64,8,16,128]{3,2,1,0:T(8,128)(2,1)S(1)} %bitcast.94), kind=kOutput, calls=%fused_computation.17 | convolution fusion | flops 2147483648 | bytes 8388608 | tf_op jit(solution)/shard_map/dot_general | solution.py:117
  80.3 1.0 convolution_convert_fusion
  81.3 86.6 %all_to_all.15 = bf16[16,48,2048]{2,1,0:T(8,128)(2,1)S(1)} all-to-all(bf16[16,48,2048]{2,1,0:T(8,128)(2,1)S(1)} %bitcast.88), channel_id=1, replica_groups=mesh['chan'=16,'tm'=16] {'chan'}, dimensions={0} | all-to-all | bytes 6291456 | tf_op jit(solution)/shard_map/all_to_all | solution.py:135
  167.9 1.7 copy.54
  (39 shorter events, 6.0 us)
Async XLA Ops:
  0.7 13.8 %collective-permute-start = (bf16[32,192]{1,0:T(8,128)(2,1)S(1)}, bf16[32,192]{1,0:T(8,128)(2,1)S(1)}, u32[]{:S(2)}, u32[]{:S(2)}) collective-permute-start(bf16[32,192]{1,0:T(8,128)(2,1)S(1)} %slice.89), channel_id=1, source_target_pairs={{1,0},{2,1},{3,2},{4,3},{5,4},{6,5},{7,6},{8,7},{9,8},{10,9},{11,1... | collective-permute-start | bytes 36872 | tf_op jit(solution)/shard_map/ppermute | solution.py:18
  3.5 17.8 %all-to-all-start = ((s32[16,1,512]{2,1,0:T(1,128)}), s32[16,1,512]{2,1,0:T(1,128)S(1)}, u32[]{:S(2)}, u32[]{:S(2)}) async-start(s32[16,1,512]{2,1,0:T(1,128)} %reshape.532), calls=%async_computation | async-start | bytes 65536 | tf_op jit(solution)/shard_map/all_to_all | solution.py:75
  40.0 6.8 %copy-start.2 = (s32[1,32,8,1]{1,3,2,0:T(1,128)S(1)}, s32[1,32,8,1]{1,3,2,0:T(1,128)}, u32[]{:S(2)}) copy-start(s32[1,32,8,1]{1,3,2,0:T(1,128)} %param.7) | copy-start | bytes 3076
  40.0 32.6 %all-to-all-start.1 = ((bf16[2,32,8,16,128]{4,2,1,0,3:T(8,128)(2,1)}), bf16[2,32,8,16,128]{4,2,1,0,3:T(8,128)(2,1)S(1)}, u32[]{:S(2)}, u32[]{:S(2)}) async-start(bf16[2,32,8,16,128]{4,2,1,0,3:T(8,128)(2,1)} %maximum_bitcast_fusion), calls=%async_computation.1 | async-start | bytes 4194304 | tf_op jit(solution)/shard_map/all_to_all | solution.py:111
  72.6 2.4 %copy-start.1 = (bf16[64,32,1024]{2,1,0:T(8,128)(2,1)S(1)}, bf16[64,32,1024]{2,1,0:T(8,128)(2,1)}, u32[]{:S(2)}) copy-start(bf16[64,32,1024]{2,1,0:T(8,128)(2,1)} %get-tuple-element.15) | copy-start | bytes 12582916
  75.0 2.4 %copy-start = (bf16[64,32,1024]{2,1,0:T(8,128)(2,1)S(1)}, bf16[64,32,1024]{2,1,0:T(8,128)(2,1)}, u32[]{:S(2)}) copy-start(bf16[64,32,1024]{2,1,0:T(8,128)(2,1)} %get-tuple-element.16) | copy-start | bytes 12582916

commit v4 on v2

--- a/solution.py
+++ b/solution.py
@@ -4,6 +4,7 @@
 import jax.numpy as jnp
 from jax import lax
 from jax.sharding import PartitionSpec as P
+from jax.experimental import pallas as pl
 
 BANDS = 256
 HOP = 64
@@ -52,6 +53,60 @@
     )
 
 
+def demod_kernel(spec_ref, first_ref, second_ref, turn_ref, cos_ref, sin_ref, out_ref):
+    per_block = spec_ref.shape[0]
+    bands = spec_ref.shape[2]
+    rows = first_ref.shape[1]
+    positions = lax.broadcasted_iota(jnp.int32, (rows, bands), 1)
+    for index in range(per_block):
+        spectra = jnp.concatenate([spec_ref[index, 0], spec_ref[index, 1]], axis=1)
+        pick = jnp.concatenate(
+            [
+                (first_ref[index] == positions).astype(jnp.bfloat16),
+                (second_ref[index] == positions).astype(jnp.bfloat16),
+            ],
+            axis=0,
+        )
+        picked = jnp.dot(pick, spectra, preferred_element_type=jnp.float32)
+        frames = spectra.shape[1] // 2
+        a_re = picked[:rows, :frames]
+        a_im = picked[:rows, frames:]
+        b_re = picked[rows:, :frames]
+        b_im = picked[rows:, frames:]
+        real_part = a_re * b_re + a_im * b_im
+        imag_part = a_im * b_re - a_re * b_im
+        turn = turn_ref[index]
+        cosine = jnp.broadcast_to(cos_ref[0:1, :], (rows, frames))
+        sine = jnp.broadcast_to(sin_ref[0:1, :], (rows, frames))
+        for level in range(1, cos_ref.shape[0]):
+            chosen = turn == level
+            cosine = jnp.where(chosen, cos_ref[level : level + 1, :], cosine)
+            sine = jnp.where(chosen, sin_ref[level : level + 1, :], sine)
+        out_ref[0, index] = (real_part * cosine + imag_part * sine).astype(out_ref.dtype)
+        out_ref[1, index] = (imag_part * cosine - real_part * sine).astype(out_ref.dtype)
+
+
+def demodulated(spectra, first, second, turn, cos_table, sin_table, per_block=4, interpret=False):
+    channels, parts, bands, frames = spectra.shape
+    rows = first.shape[1]
+    levels = cos_table.shape[0]
+    return pl.pallas_call(
+        demod_kernel,
+        out_shape=jax.ShapeDtypeStruct((2, channels, rows, frames), jnp.bfloat16),
+        grid=(channels // per_block,),
+        in_specs=[
+            pl.BlockSpec((per_block, parts, bands, frames), lambda i: (i, 0, 0, 0)),
+            pl.BlockSpec((per_block, rows, 1), lambda i: (i, 0, 0)),
+            pl.BlockSpec((per_block, rows, 1), lambda i: (i, 0, 0)),
+            pl.BlockSpec((per_block, rows, 1), lambda i: (i, 0, 0)),
+            pl.BlockSpec((levels, frames), lambda i: (0, 0)),
+            pl.BlockSpec((levels, frames), lambda i: (0, 0)),
+        ],
+        out_specs=pl.BlockSpec((2, per_block, rows, frames), lambda i: (0, i, 0, 0)),
+        interpret=interpret,
+    )(spectra, first[..., None], second[..., None], turn[..., None], cos_table, sin_table)
+
+
 def on_device(signal, pair_band, pair_offset, pair_owner):
     channels = signal.shape[0]
     stride_count = BANDS // HOP
@@ -76,32 +131,17 @@
     bands_all = tables[:, 0].transpose(1, 0, 2)
     offsets_all = tables[:, 1].transpose(1, 0, 2)
     pairs = bands_all.shape[2]
-    band_first = bands_all.reshape(channels, blocks * pairs)
-    offset = offsets_all.reshape(channels, blocks * pairs)
-    positions = jnp.arange(BANDS, dtype=jnp.int32)
-    pick_first = (band_first[..., None] == positions).astype(jnp.bfloat16)
-    pick_second = ((band_first + offset)[..., None] == positions).astype(jnp.bfloat16)
-    first = jnp.einsum("crb,cpbm->crpm", pick_first, spectra, preferred_element_type=jnp.float32)
-    second = jnp.einsum("crb,cpbm->crpm", pick_second, spectra, preferred_element_type=jnp.float32)
-    real_part = first[:, :, 0] * second[:, :, 0] + first[:, :, 1] * second[:, :, 1]
-    imag_part = first[:, :, 1] * second[:, :, 0] - first[:, :, 0] * second[:, :, 1]
-
+    band_first = bands_all.transpose(0, 2, 1).reshape(channels, pairs * blocks)
+    offset = offsets_all.transpose(0, 2, 1).reshape(channels, pairs * blocks)
     moment = lax.axis_index("tm") * frames_dev + jnp.arange(frames_dev, dtype=jnp.int32)
     step = math.gcd(HOP * FRAMES // BANDS, KEEP // 2, FRAMES)
     levels = FRAMES // step
-    level_cos, level_sin = turn_table(jnp.arange(levels, dtype=jnp.int32), jnp.full((1,), step, jnp.int32))
+    cos_table, sin_table = turn_table(jnp.arange(levels, dtype=jnp.int32) * step, moment)
     shift_bins = (offset * (HOP * FRAMES // BANDS) - KEEP // 2) % FRAMES
-    level = (shift_bins[..., None] // step) * moment % levels
-    cosine = jnp.full(level.shape, level_cos[0, 0])
-    sine = jnp.full(level.shape, level_sin[0, 0])
-    for index in range(1, levels):
-        chosen = level == index
-        cosine = jnp.where(chosen, level_cos[index, 0], cosine)
-        sine = jnp.where(chosen, level_sin[index, 0], sine)
-    demod_re = (real_part * cosine + imag_part * sine).astype(jnp.bfloat16)
-    demod_im = (imag_part * cosine - real_part * sine).astype(jnp.bfloat16)
-    demod = jnp.stack([demod_re, demod_im], axis=0)
-    demod = demod.reshape(2, channels, blocks, pairs, frames_dev).transpose(0, 1, 3, 2, 4)
+    demod = demodulated(
+        spectra, band_first, band_first + offset, shift_bins // step, cos_table, sin_table
+    )
+    demod = demod.reshape(2, channels, pairs, blocks, frames_dev)
     arrived = lax.all_to_all(demod, "tm", split_axis=3, concat_axis=3, tiled=True)
     rows = channels * pairs
     arrived = arrived.reshape(2 * rows, blocks * frames_dev)

time: 175 us -> 175 us (level)
  other arithmetic: 25.3 us -> 16 us
  local copies, waits for them, and re-layouts: 9.78 us -> 18.8 us
  Pallas kernels: 0 us -> 8.98 us
  matrix products: 18.1 us -> 9.72 us
    pallas_call x0 -> x1, Pallas kernels: none -> 8.98 us  [demodulated(): pl.pallas_call(demod_kernel, out_shape=jax.ShapeDtypeStruct((2, channels,...]
    dot_general x2 -> x0, matrix products: 8.34 us -> none  [the longest x1 5.31 us: on_device(): jnp.einsum('crb,cpbm->crpm', pick_first, spectra, preferred_element_type=...]
    convert_element_type x1 -> x0, other arithmetic: 7.39 us -> none  [on_device(): demod_re = (real_part * cosine + imag_part * sine).astype(jnp.bfloat16)]
    reshape x0 -> x3, local copies, waits for them, and re-layouts: none -> 5.43 us  [the longest x1 3.45 us: on_device(): demod = demod.reshape(2, channels, pairs, blocks, frames_dev)]
    add x1 -> x0, other arithmetic: 4.34 us -> none  [on_device(): first[:, :, 0] * second[:, :, 0] + first[:, :, 1] * second[:, :, 1]]
    select_n x1, other arithmetic: 0.07 us -> 3.36 us  [on_device(): shift_bins // step]
    another operation x1 -> x6, local copies, waits for them, and re-layouts: 0.01 us -> 3.03 us  [the longest x2 2.99 us: demodulated(): first[..., None]]
    add x1, local copies, waits for them, and re-layouts: 0.07 us -> 1.97 us  [on_device(): band_first + offset]
  transfers between devices with their start and end apart: 3 -> 3, of which waited for: 1 -> 1; matrix products, arithmetic and copies ran while one was open for 11% -> 10% of each run, Pallas kernels for 0% -> 0%
where the time goes in v4:
time: 175 us; the launch traced here: 174 us
  blocking collectives  86.6 us (49%)
  local copies, waits for them, and re-layouts  18.8 us (11%)
  waiting for transfers between devices  17.7 us (10%)
  starting transfers between devices  16.5 us (9%)
  other arithmetic  16 us (9%)
  matrix products  9.72 us (6%)
  Pallas kernels  8.98 us (5%)
    all_to_all x1, blocking collectives, on_device(): lax.all_to_all(outgoing, 'chan', split_axis=0, concat_axis=0, tiled=True)  86.6 us
    all_to_all x1, waiting for transfers between devices, on_device(): lax.all_to_all(demod, 'tm', split_axis=3, concat_axis=3, tiled=True)  17.7 us
    pallas_call x1, Pallas kernels, demodulated(): pl.pallas_call(demod_kernel, out_shape=jax.ShapeDtypeStruct((2, channels,...  8.98 us
    all_to_all x1, starting transfers between devices, on_device(): lax.all_to_all(spread, 'tm', split_axis=0, concat_axis=0, tiled=True)  8.47 us
    all_to_all x1, starting transfers between devices, on_device(): lax.all_to_all(demod, 'tm', split_axis=3, concat_axis=3, tiled=True)  6.78 us
    convert_element_type x1, other arithmetic, fourier_tables(): cosine.reshape(FRAMES, KEEP).astype(jnp.bfloat16)  5.25 us
    dot_general x1, matrix products, on_device(): jnp.einsum('cmn,nk->ckm', framed, bank_table, preferred_element_type=jnp....  4 us
  transfers between devices with their start and end apart: 3, of which 1 were waited for; matrix products, arithmetic and copies ran while one was open for 10% of the time, Pallas kernels for 0%

profile of v4, /device:TPU:1, one launch (start us, length us, event | category | flops | bytes accessed | tf_op | source)
XLA Modules:
  0.0 174.5 jit_solution(8864270484105284102)
XLA Ops:
  0.7 1.3 collective-permute-start
  2.7 0.7 reshape.319
  3.5 8.5 %all-to-all-start = ((s32[16,1,512]{2,1,0:T(1,128)}), s32[16,1,512]{2,1,0:T(1,128)S(1)}, u32[]{:S(2)}, u32[]{:S(2)}) async-start(s32[16,1,512]{2,1,0:T(1,128)} %reshape.319), calls=%async_computation | async-start | bytes 65536 | tf_op jit(solution)/shard_map/all_to_all | solution.py:130
  12.1 1.1 multiply_convert_fusion.2
  13.9 1.1 pad_maximum_fusion
  15.0 0.8 reshape.310
  15.8 0.9 fusion.57
  16.8 4.0 %convolution_convert_fusion.1 = bf16[512,32,128]{2,0,1:T(8,128)(2,1)} fusion(bf16[32,128,64]{2,1,0:T(8,128)(2,1)S(1)} %get-tuple-element.8, bf16[32,128,64]{2,1,0:T(8,128)(2,1)S(1)} %get-tuple-element.9, bf16[32,128,64]{2,1,0:T(8,128)(2,1)S(1)} %get-tuple-element.10, bf16[32,128,64]{2,1,0:T(8,128)(2,1)S(1)} %get-tuple-element.7, ...), kind=kOutput, calls=%fused_computation.10 | convolution fusion | flops 1084751872 | bytes 6553600 | tf_op jit(solution)/shard_map/cmn,nk->ckm/dot_general | solution.py:123
  22.2 1.9 %copy.41 = s32[32,128,1]{2,1,0:T(8,128)S(1)} copy(s32[32,128,1]{0,1,2:T(8,128)S(1)} %bitcast.65) | data formatting | bytes 32768 | tf_op jit(solution)/shard_map/reshape | solution.py:135
  24.2 2.9 %copy.42.first_ref = s32[32,128,1]{2,1,0:T(8,128)} copy(s32[32,128,1]{0,1,2:T(8,128)S(1)} %bitcast.67) | data formatting | bytes 32768 | tf_op jit(solution)/shard_map/broadcast_in_dim;reshape | solution.py:107
  27.1 2.0 %copy.43.second_ref = s32[32,128,1]{2,1,0:T(8,128)} copy(s32[32,128,1]{1,0,2:T(8,128)S(1)} %add.132) | data formatting | bytes 32768 | tf_op jit(solution)/shard_map/add | solution.py:142
  29.1 3.4 %add_select_fusion.turn_ref = s32[32,128,1]{2,1,0:T(8,128)} fusion(s32[32,128,1]{2,1,0:T(8,128)S(1)} %copy.41), kind=kLoop, calls=%fused_computation.3 | loop fusion | flops 114688 | bytes 32768 | tf_op jit(solution)/shard_map/jit(floor_divide)/jit(_where)/select_n | solution.py:142
  32.5 9.0 %shard_map.46 = bf16[2,32,128,128]{3,2,1,0:T(8,128)(2,1)} custom-call(bf16[32,2,256,128]{3,2,1,0:T(8,128)(2,1)} %bitcast.59, s32[32,128,1]{2,1,0:T(8,128)} %copy.42.first_ref, s32[32,128,1]{2,1,0:T(8,128)} %copy.43.second_ref, s32[32,128,1]{2,1,0:T(8,128)} %add_select_fusion.turn_ref, f32[4,128]{1,0:T(4,128)} %get-tuple-element.16.cos_ref, ...), custom_call_target="tpu_custom_call" | custom-call | tf_op jit(solution)/shard_map/pallas_call | solution.py:93
  41.5 3.5 %copy.44 = bf16[2,32,8,16,128]{4,2,1,0,3:T(8,128)(2,1)} copy(bf16[2,32,8,16,128]{4,3,2,1,0:T(8,128)(2,1)} %bitcast.58) | data formatting | bytes 4194304 | tf_op jit(solution)/shard_map/reshape | solution.py:144
  44.9 6.8 %all-to-all-start.1 = ((bf16[2,32,8,16,128]{4,2,1,0,3:T(8,128)(2,1)}), bf16[2,32,8,16,128]{4,2,1,0,3:T(8,128)(2,1)S(1)}, u32[]{:S(2)}, u32[]{:S(2)}) async-start(bf16[2,32,8,16,128]{4,2,1,0,3:T(8,128)(2,1)} %copy.44), calls=%async_computation.1 | async-start | bytes 4194304 | tf_op jit(solution)/shard_map/all_to_all | solution.py:145
  53.4 1.1 fusion.42
  54.5 5.3 %multiply_convert_fusion.1 = (bf16[64,32,1024]{2,1,0:T(8,128)(2,1)}, bf16[64,32,1024]{2,1,0:T(8,128)(2,1)}) fusion(f32[32,1024]{1,0:T(8,128)S(1)} %get-tuple-element.19, f32[64,1024]{1,0:T(8,128)S(1)} %get-tuple-element.18, f32[32,1024]{1,0:T(8,128)S(1)} %get-tuple-element.20, f32[64,1024]{1,0:T(8,128)S(1)} %get-tuple-element.17), kind=kLoop, calls=%fused_computation.1 | loop fusion | flops 20971520 | bytes 9175040 | tf_op jit(solution)/shard_map/convert_element_type | solution.py:51
  59.8 17.7 %all-to-all-done.1 = bf16[2,32,8,16,128]{4,2,1,0,3:T(8,128)(2,1)S(1)} async-done(((bf16[2,32,8,16,128]{4,2,1,0,3:T(8,128)(2,1)}), bf16[2,32,8,16,128]{4,2,1,0,3:T(8,128)(2,1)S(1)}, u32[]{:S(2)}, u32[]{:S(2)}) %all-to-all-start.1) | async-done | bytes 2097184 | tf_op jit(solution)/shard_map/all_to_all | solution.py:145
  77.5 2.4 %copy.45 = bf16[2,32,8,16,128]{4,3,2,1,0:T(8,128)(2,1)S(1)} copy(bf16[2,32,8,16,128]{4,2,1,0,3:T(8,128)(2,1)S(1)} %all-to-all-done.1) | data formatting | bytes 4194304 | tf_op jit(solution)/shard_map/all_to_all | solution.py:145
  79.9 2.4 %fusion.4 = f32[512,1024]{1,0:T(8,128)S(1)} fusion(bf16[2048,1024]{1,0:T(8,128)(2,1)S(1)} %bitcast.61, bf16[64,8,16,128]{3,2,1,0:T(8,128)(2,1)S(1)} %bitcast.62), kind=kOutput, calls=%fused_computation.15 | convolution fusion | flops 2147483648 | bytes 8388608 | tf_op jit(solution)/shard_map/dot_general | solution.py:150
  82.3 2.4 %fusion.2 = f32[512,1024]{1,0:T(8,128)S(1)} fusion(bf16[2048,1024]{1,0:T(8,128)(2,1)S(1)} %bitcast.60, bf16[64,8,16,128]{3,2,1,0:T(8,128)(2,1)S(1)} %bitcast.63), kind=kOutput, calls=%fused_computation.13 | convolution fusion | flops 2147483648 | bytes 8388608 | tf_op jit(solution)/shard_map/dot_general | solution.py:151
  85.2 1.0 convolution_convert_fusion
  86.2 86.6 %all_to_all.15 = bf16[16,48,2048]{2,1,0:T(8,128)(2,1)S(1)} all-to-all(bf16[16,48,2048]{2,1,0:T(8,128)(2,1)S(1)} %bitcast.56), channel_id=1, replica_groups=mesh['chan'=16,'tm'=16] {'chan'}, dimensions={0} | all-to-all | bytes 6291456 | tf_op jit(solution)/shard_map/all_to_all | solution.py:169
  172.8 1.7 copy.58
  (38 shorter events, 6.0 us)
Async XLA Ops:
  0.7 13.2 %collective-permute-start = (bf16[32,192]{1,0:T(8,128)(2,1)S(1)}, bf16[32,192]{1,0:T(8,128)(2,1)S(1)}, u32[]{:S(2)}, u32[]{:S(2)}) collective-permute-start(bf16[32,192]{1,0:T(8,128)(2,1)S(1)} %slice.41), channel_id=1, source_target_pairs={{1,0},{2,1},{3,2},{4,3},{5,4},{6,5},{7,6},{8,7},{9,8},{10,9},{11,1... | collective-permute-start | bytes 36872 | tf_op jit(solution)/shard_map/ppermute | solution.py:19
  3.5 17.3 %all-to-all-start = ((s32[16,1,512]{2,1,0:T(1,128)}), s32[16,1,512]{2,1,0:T(1,128)S(1)}, u32[]{:S(2)}, u32[]{:S(2)}) async-start(s32[16,1,512]{2,1,0:T(1,128)} %reshape.319), calls=%async_computation | async-start | bytes 65536 | tf_op jit(solution)/shard_map/all_to_all | solution.py:130
  44.9 6.8 %copy-start.2 = (s32[1,32,8,1]{1,3,2,0:T(1,128)S(1)}, s32[1,32,8,1]{1,3,2,0:T(1,128)}, u32[]{:S(2)}) copy-start(s32[1,32,8,1]{1,3,2,0:T(1,128)} %param.7) | copy-start | bytes 3076
  44.9 32.5 %all-to-all-start.1 = ((bf16[2,32,8,16,128]{4,2,1,0,3:T(8,128)(2,1)}), bf16[2,32,8,16,128]{4,2,1,0,3:T(8,128)(2,1)S(1)}, u32[]{:S(2)}, u32[]{:S(2)}) async-start(bf16[2,32,8,16,128]{4,2,1,0,3:T(8,128)(2,1)} %copy.44), calls=%async_computation.1 | async-start | bytes 4194304 | tf_op jit(solution)/shard_map/all_to_all | solution.py:145
  77.5 2.4 %copy-start.1 = (bf16[64,32,1024]{2,1,0:T(8,128)(2,1)S(1)}, bf16[64,32,1024]{2,1,0:T(8,128)(2,1)}, u32[]{:S(2)}) copy-start(bf16[64,32,1024]{2,1,0:T(8,128)(2,1)} %get-tuple-element.11) | copy-start | bytes 12582916
  79.9 2.4 %copy-start = (bf16[64,32,1024]{2,1,0:T(8,128)(2,1)S(1)}, bf16[64,32,1024]{2,1,0:T(8,128)(2,1)}, u32[]{:S(2)}) copy-start(bf16[64,32,1024]{2,1,0:T(8,128)(2,1)} %get-tuple-element.12) | copy-start | bytes 12582916

commit v5 on v4

--- a/solution.py
+++ b/solution.py
@@ -56,55 +56,64 @@
 def demod_kernel(spec_ref, first_ref, second_ref, turn_ref, cos_ref, sin_ref, out_ref):
     per_block = spec_ref.shape[0]
     bands = spec_ref.shape[2]
+    frames = spec_ref.shape[3]
     rows = first_ref.shape[1]
+    blocks = out_ref.shape[0]
+    pairs = out_ref.shape[3]
     positions = lax.broadcasted_iota(jnp.int32, (rows, bands), 1)
+    first_all = first_ref[...].T
+    second_all = second_ref[...].T
+    turn_all = turn_ref[...].T
     for index in range(per_block):
         spectra = jnp.concatenate([spec_ref[index, 0], spec_ref[index, 1]], axis=1)
         pick = jnp.concatenate(
             [
-                (first_ref[index] == positions).astype(jnp.bfloat16),
-                (second_ref[index] == positions).astype(jnp.bfloat16),
+                (first_all[:, index : index + 1] == positions).astype(jnp.bfloat16),
+                (second_all[:, index : index + 1] == positions).astype(jnp.bfloat16),
             ],
             axis=0,
         )
         picked = jnp.dot(pick, spectra, preferred_element_type=jnp.float32)
-        frames = spectra.shape[1] // 2
         a_re = picked[:rows, :frames]
         a_im = picked[:rows, frames:]
         b_re = picked[rows:, :frames]
         b_im = picked[rows:, frames:]
         real_part = a_re * b_re + a_im * b_im
         imag_part = a_im * b_re - a_re * b_im
-        turn = turn_ref[index]
+        turn = turn_all[:, index : index + 1]
         cosine = jnp.broadcast_to(cos_ref[0:1, :], (rows, frames))
         sine = jnp.broadcast_to(sin_ref[0:1, :], (rows, frames))
         for level in range(1, cos_ref.shape[0]):
             chosen = turn == level
             cosine = jnp.where(chosen, cos_ref[level : level + 1, :], cosine)
             sine = jnp.where(chosen, sin_ref[level : level + 1, :], sine)
-        out_ref[0, index] = (real_part * cosine + imag_part * sine).astype(out_ref.dtype)
-        out_ref[1, index] = (imag_part * cosine - real_part * sine).astype(out_ref.dtype)
+        demod_re = (real_part * cosine + imag_part * sine).astype(out_ref.dtype)
+        demod_im = (imag_part * cosine - real_part * sine).astype(out_ref.dtype)
+        for block in range(blocks):
+            out_ref[block, 0, index] = demod_re[block * pairs : (block + 1) * pairs]
+            out_ref[block, 1, index] = demod_im[block * pairs : (block + 1) * pairs]
 
 
-def demodulated(spectra, first, second, turn, cos_table, sin_table, per_block=4, interpret=False):
+def demodulated(spectra, first, second, turn, cos_table, sin_table, blocks, per_block=8, interpret=False):
     channels, parts, bands, frames = spectra.shape
     rows = first.shape[1]
+    pairs = rows // blocks
     levels = cos_table.shape[0]
     return pl.pallas_call(
         demod_kernel,
-        out_shape=jax.ShapeDtypeStruct((2, channels, rows, frames), jnp.bfloat16),
+        out_shape=jax.ShapeDtypeStruct((blocks, 2, channels, pairs, frames), jnp.bfloat16),
         grid=(channels // per_block,),
         in_specs=[
             pl.BlockSpec((per_block, parts, bands, frames), lambda i: (i, 0, 0, 0)),
-            pl.BlockSpec((per_block, rows, 1), lambda i: (i, 0, 0)),
-            pl.BlockSpec((per_block, rows, 1), lambda i: (i, 0, 0)),
-            pl.BlockSpec((per_block, rows, 1), lambda i: (i, 0, 0)),
+            pl.BlockSpec((per_block, rows), lambda i: (i, 0)),
+            pl.BlockSpec((per_block, rows), lambda i: (i, 0)),
+            pl.BlockSpec((per_block, rows), lambda i: (i, 0)),
             pl.BlockSpec((levels, frames), lambda i: (0, 0)),
             pl.BlockSpec((levels, frames), lambda i: (0, 0)),
         ],
-        out_specs=pl.BlockSpec((2, per_block, rows, frames), lambda i: (0, i, 0, 0)),
+        out_specs=pl.BlockSpec((blocks, 2, per_block, pairs, frames), lambda i: (0, 0, i, 0, 0)),
         interpret=interpret,
-    )(spectra, first[..., None], second[..., None], turn[..., None], cos_table, sin_table)
+    )(spectra, first, second, turn, cos_table, sin_table)
 
 
 def on_device(signal, pair_band, pair_offset, pair_owner):
@@ -131,18 +140,18 @@
     bands_all = tables[:, 0].transpose(1, 0, 2)
     offsets_all = tables[:, 1].transpose(1, 0, 2)
     pairs = bands_all.shape[2]
-    band_first = bands_all.transpose(0, 2, 1).reshape(channels, pairs * blocks)
-    offset = offsets_all.transpose(0, 2, 1).reshape(channels, pairs * blocks)
+    band_first = bands_all.reshape(channels, blocks * pairs)
+    offset = offsets_all.reshape(channels, blocks * pairs)
     moment = lax.axis_index("tm") * frames_dev + jnp.arange(frames_dev, dtype=jnp.int32)
     step = math.gcd(HOP * FRAMES // BANDS, KEEP // 2, FRAMES)
     levels = FRAMES // step
     cos_table, sin_table = turn_table(jnp.arange(levels, dtype=jnp.int32) * step, moment)
     shift_bins = (offset * (HOP * FRAMES // BANDS) - KEEP // 2) % FRAMES
     demod = demodulated(
-        spectra, band_first, band_first + offset, shift_bins // step, cos_table, sin_table
+        spectra, band_first, band_first + offset, shift_bins // step, cos_table, sin_table, blocks
     )
-    demod = demod.reshape(2, channels, pairs, blocks, frames_dev)
-    arrived = lax.all_to_all(demod, "tm", split_axis=3, concat_axis=3, tiled=True)
+    arrived = lax.all_to_all(demod, "tm", split_axis=0, concat_axis=0, tiled=True)
+    arrived = arrived.transpose(1, 2, 3, 0, 4)
     rows = channels * pairs
     arrived = arrived.reshape(2 * rows, blocks * frames_dev)
 

time: 175 us -> 160 us (0.914)
  local copies, waits for them, and re-layouts: 18.8 us -> 8.49 us
  other arithmetic: 16 us -> 13.2 us
  Pallas kernels: 8.98 us -> 6.69 us
    reshape x3, local copies, waits for them, and re-layouts: 5.43 us -> 0.14 us  [the longest x2 0.08 us: on_device(): offset = offsets_all.reshape(channels, blocks * pairs)]
    another operation x6 -> x1, local copies, waits for them, and re-layouts: 3.03 us -> 0.01 us  [the longest x2 2.99 us: demodulated(): first[..., None]]
    select_n x1, other arithmetic: 3.36 us -> 0.65 us  [on_device(): shift_bins // step]
    all_to_all x1 -> x0, local copies, waits for them, and re-layouts: 2.43 us -> none  [on_device(): lax.all_to_all(demod, 'tm', split_axis=3, concat_axis=3, tiled=True)]
    transpose x0 -> x1, local copies, waits for them, and re-layouts: none -> 2.43 us  [on_device(): arrived = arrived.transpose(1, 2, 3, 0, 4)]
    pallas_call x1, Pallas kernels: 8.98 us -> 6.69 us  [demodulated(): pl.pallas_call(demod_kernel, out_shape=jax.ShapeDtypeStruct((blocks, 2, c...]
    add x1 -> x0, local copies, waits for them, and re-layouts: 1.97 us -> none  [on_device(): band_first + offset]
  transfers between devices with their start and end apart: 3 -> 3, of which waited for: 1 -> 1; matrix products, arithmetic and copies ran while one was open for 10% -> 11% of each run, Pallas kernels for 0% -> 0%
where the time goes in v5:
time: 160 us; the launch traced here: 159 us
  blocking collectives  86.6 us (54%)
  waiting for transfers between devices  17.7 us (11%)
  starting transfers between devices  16.6 us (10%)
  other arithmetic  13.2 us (8%)
  matrix products  9.7 us (6%)
  local copies, waits for them, and re-layouts  8.49 us (5%)
  Pallas kernels  6.69 us (4%)
    all_to_all x1, blocking collectives, on_device(): lax.all_to_all(outgoing, 'chan', split_axis=0, concat_axis=0, tiled=True)  86.6 us
    all_to_all x1, waiting for transfers between devices, on_device(): lax.all_to_all(demod, 'tm', split_axis=0, concat_axis=0, tiled=True)  17.7 us
    all_to_all x1, starting transfers between devices, on_device(): lax.all_to_all(spread, 'tm', split_axis=0, concat_axis=0, tiled=True)  8.47 us
    all_to_all x1, starting transfers between devices, on_device(): lax.all_to_all(demod, 'tm', split_axis=0, concat_axis=0, tiled=True)  6.81 us
    pallas_call x1, Pallas kernels, demodulated(): pl.pallas_call(demod_kernel, out_shape=jax.ShapeDtypeStruct((blocks, 2, c...  6.69 us
    convert_element_type x1, other arithmetic, fourier_tables(): cosine.reshape(FRAMES, KEEP).astype(jnp.bfloat16)  5.25 us
    dot_general x1, matrix products, on_device(): jnp.einsum('cmn,nk->ckm', framed, bank_table, preferred_element_type=jnp....  3.99 us
  transfers between devices with their start and end apart: 3, of which 1 were waited for; matrix products, arithmetic and copies ran while one was open for 11% of the time, Pallas kernels for 0%

profile of v5, /device:TPU:1, one launch (start us, length us, event | category | flops | bytes accessed | tf_op | source)
XLA Modules:
  0.0 159.1 jit_solution(6903737837652089789)
XLA Ops:
  0.0 0.7 slice.41
  0.7 1.3 collective-permute-start
  2.0 0.7 pad_add_fusion
  2.7 0.7 reshape.210
  3.5 8.5 %all-to-all-start = ((s32[16,1,512]{2,1,0:T(1,128)}), s32[16,1,512]{2,1,0:T(1,128)S(1)}, u32[]{:S(2)}, u32[]{:S(2)}) async-start(s32[16,1,512]{2,1,0:T(1,128)} %reshape.210), calls=%async_computation | async-start | bytes 65536 | tf_op jit(solution)/shard_map/all_to_all | solution.py:139
  12.1 1.1 multiply_convert_fusion.2
  13.2 0.7 fusion.52
  13.9 1.1 pad_maximum_fusion
  15.0 0.8 reshape.201
  15.8 0.9 fusion.57
  16.8 4.0 %convolution_convert_fusion.1 = bf16[512,32,128]{2,0,1:T(8,128)(2,1)} fusion(bf16[32,128,64]{2,1,0:T(8,128)(2,1)S(1)} %get-tuple-element.8, bf16[32,128,64]{2,1,0:T(8,128)(2,1)S(1)} %get-tuple-element.9, bf16[32,128,64]{2,1,0:T(8,128)(2,1)S(1)} %get-tuple-element.10, bf16[32,128,64]{2,1,0:T(8,128)(2,1)S(1)} %get-tuple-element.7, ...), kind=kOutput, calls=%fused_computation.3 | convolution fusion | flops 1084751872 | bytes 6553600 | tf_op jit(solution)/shard_map/cmn,nk->ckm/dot_general | solution.py:132
  21.3 0.7 reduce.2
  22.2 0.6 add_select_fusion.3
  22.9 6.7 %shard_map.46 = bf16[16,2,32,8,128]{4,3,2,1,0:T(8,128)(2,1)} custom-call(bf16[32,2,256,128]{3,2,1,0:T(8,128)(2,1)} %bitcast.61, s32[32,128]{1,0:T(8,128)} %copy-done.2, s32[32,128]{1,0:T(8,128)} %get-tuple-element.16.second_ref, s32[32,128]{1,0:T(8,128)} %get-tuple-element.15.turn_ref, f32[4,128]{1,0:T(4,128)} %get-tuple-element.18.cos_ref, ...), custom_call_target="tpu_custom_call" | custom-call | tf_op jit(solution)/shard_map/pallas_call | solution.py:102
  29.6 6.8 %all-to-all-start.1 = ((bf16[16,2,32,8,128]{4,3,2,1,0:T(8,128)(2,1)}), bf16[16,2,32,8,128]{4,3,2,1,0:T(8,128)(2,1)S(1)}, u32[]{:S(2)}, u32[]{:S(2)}) async-start(bf16[16,2,32,8,128]{4,3,2,1,0:T(8,128)(2,1)} %shard_map.46), calls=%async_computation.1 | async-start | bytes 4194304 | tf_op jit(solution)/shard_map/all_to_all | solution.py:153
  38.1 1.1 fusion.39
  39.2 5.3 %multiply_convert_fusion.1 = (bf16[64,32,1024]{2,1,0:T(8,128)(2,1)}, bf16[64,32,1024]{2,1,0:T(8,128)(2,1)}) fusion(f32[32,1024]{1,0:T(8,128)S(1)} %get-tuple-element.21, f32[64,1024]{1,0:T(8,128)S(1)} %get-tuple-element.20, f32[32,1024]{1,0:T(8,128)S(1)} %get-tuple-element.22, f32[64,1024]{1,0:T(8,128)S(1)} %get-tuple-element.19), kind=kLoop, calls=%fused_computation.1 | loop fusion | flops 20971520 | bytes 9175040 | tf_op jit(solution)/shard_map/convert_element_type | solution.py:51
  44.5 17.7 %all-to-all-done.1 = bf16[16,2,32,8,128]{4,3,2,1,0:T(8,128)(2,1)S(1)} async-done(((bf16[16,2,32,8,128]{4,3,2,1,0:T(8,128)(2,1)}), bf16[16,2,32,8,128]{4,3,2,1,0:T(8,128)(2,1)S(1)}, u32[]{:S(2)}, u32[]{:S(2)}) %all-to-all-start.1) | async-done | bytes 2097184 | tf_op jit(solution)/shard_map/all_to_all | solution.py:153
  62.1 2.4 %copy.21 = bf16[2,32,8,16,128]{4,3,2,1,0:T(8,128)(2,1)S(1)} copy(bf16[2,32,8,16,128]{4,2,1,0,3:T(8,128)(2,1)S(1)} %bitcast.60) | data formatting | bytes 4194304 | tf_op jit(solution)/shard_map/transpose | solution.py:154
  64.6 2.4 %fusion.2 = f32[512,1024]{1,0:T(8,128)S(1)} fusion(bf16[2048,1024]{1,0:T(8,128)(2,1)S(1)} %bitcast.63, bf16[64,8,16,128]{3,2,1,0:T(8,128)(2,1)S(1)} %bitcast.64), kind=kOutput, calls=%fused_computation.6 | convolution fusion | flops 2147483648 | bytes 8388608 | tf_op jit(solution)/shard_map/dot_general | solution.py:159
  67.0 2.4 %fusion = f32[512,1024]{1,0:T(8,128)S(1)} fusion(bf16[2048,1024]{1,0:T(8,128)(2,1)S(1)} %bitcast.62, bf16[64,8,16,128]{3,2,1,0:T(8,128)(2,1)S(1)} %bitcast.65), kind=kOutput, calls=%fused_computation.4 | convolution fusion | flops 2147483648 | bytes 8388608 | tf_op jit(solution)/shard_map/dot_general | solution.py:160
  69.9 1.0 convolution_convert_fusion
  70.9 86.6 %all_to_all.15 = bf16[16,48,2048]{2,1,0:T(8,128)(2,1)S(1)} all-to-all(bf16[16,48,2048]{2,1,0:T(8,128)(2,1)S(1)} %bitcast.58), channel_id=1, replica_groups=mesh['chan'=16,'tm'=16] {'chan'}, dimensions={0} | all-to-all | bytes 6291456 | tf_op jit(solution)/shard_map/all_to_all | solution.py:178
  157.5 1.7 %copy.34 = bf16[1,1,16,48,2048]{4,3,2,1,0:T(8,128)(2,1)} copy(bf16[1,1,16,48,2048]{4,3,2,1,0:T(8,128)(2,1)S(1)} %bitcast.59) | data formatting | bytes 6291456
  (33 shorter events, 3.1 us)
Async XLA Ops:
  0.7 13.2 %collective-permute-start = (bf16[32,192]{1,0:T(8,128)(2,1)S(1)}, bf16[32,192]{1,0:T(8,128)(2,1)S(1)}, u32[]{:S(2)}, u32[]{:S(2)}) collective-permute-start(bf16[32,192]{1,0:T(8,128)(2,1)S(1)} %slice.41), channel_id=1, source_target_pairs={{1,0},{2,1},{3,2},{4,3},{5,4},{6,5},{7,6},{8,7},{9,8},{10,9},{11,1... | collective-permute-start | bytes 36872 | tf_op jit(solution)/shard_map/ppermute | solution.py:19
  3.5 17.3 %all-to-all-start = ((s32[16,1,512]{2,1,0:T(1,128)}), s32[16,1,512]{2,1,0:T(1,128)S(1)}, u32[]{:S(2)}, u32[]{:S(2)}) async-start(s32[16,1,512]{2,1,0:T(1,128)} %reshape.210), calls=%async_computation | async-start | bytes 65536 | tf_op jit(solution)/shard_map/all_to_all | solution.py:139
  22.1 0.7 copy-start.2
  29.6 6.8 %copy-start.3 = (s32[1,32,8,1]{1,3,2,0:T(1,128)S(1)}, s32[1,32,8,1]{1,3,2,0:T(1,128)}, u32[]{:S(2)}) copy-start(s32[1,32,8,1]{1,3,2,0:T(1,128)} %param.7) | copy-start | bytes 3076
  29.6 32.6 %all-to-all-start.1 = ((bf16[16,2,32,8,128]{4,3,2,1,0:T(8,128)(2,1)}), bf16[16,2,32,8,128]{4,3,2,1,0:T(8,128)(2,1)S(1)}, u32[]{:S(2)}, u32[]{:S(2)}) async-start(bf16[16,2,32,8,128]{4,3,2,1,0:T(8,128)(2,1)} %shard_map.46), calls=%async_computation.1 | async-start | bytes 4194304 | tf_op jit(solution)/shard_map/all_to_all | solution.py:153
  62.1 2.4 %copy-start.1 = (bf16[64,32,1024]{2,1,0:T(8,128)(2,1)S(1)}, bf16[64,32,1024]{2,1,0:T(8,128)(2,1)}, u32[]{:S(2)}) copy-start(bf16[64,32,1024]{2,1,0:T(8,128)(2,1)} %get-tuple-element.11) | copy-start | bytes 12582916
  64.6 2.4 %copy-start = (bf16[64,32,1024]{2,1,0:T(8,128)(2,1)S(1)}, bf16[64,32,1024]{2,1,0:T(8,128)(2,1)}, u32[]{:S(2)}) copy-start(bf16[64,32,1024]{2,1,0:T(8,128)(2,1)} %get-tuple-element.12) | copy-start | bytes 12582916

commit v6 on v5

--- a/solution.py
+++ b/solution.py
@@ -53,10 +53,10 @@
     )
 
 
-def demod_kernel(spec_ref, first_ref, second_ref, turn_ref, cos_ref, sin_ref, out_ref):
-    per_block = spec_ref.shape[0]
-    bands = spec_ref.shape[2]
-    frames = spec_ref.shape[3]
+def demod_kernel(framed_ref, bank_ref, first_ref, second_ref, turn_ref, cos_ref, sin_ref, out_ref):
+    per_block = framed_ref.shape[0]
+    frames = framed_ref.shape[1]
+    bands = bank_ref.shape[0] // 2
     rows = first_ref.shape[1]
     blocks = out_ref.shape[0]
     pairs = out_ref.shape[3]
@@ -65,7 +65,11 @@
     second_all = second_ref[...].T
     turn_all = turn_ref[...].T
     for index in range(per_block):
-        spectra = jnp.concatenate([spec_ref[index, 0], spec_ref[index, 1]], axis=1)
+        spectra = lax.dot_general(
+            bank_ref[...], framed_ref[index], (((1,), (1,)), ((), ())),
+            preferred_element_type=jnp.float32,
+        ).astype(jnp.bfloat16)
+        spectra = jnp.concatenate([spectra[:bands], spectra[bands:]], axis=1)
         pick = jnp.concatenate(
             [
                 (first_all[:, index : index + 1] == positions).astype(jnp.bfloat16),
@@ -94,8 +98,8 @@
             out_ref[block, 1, index] = demod_im[block * pairs : (block + 1) * pairs]
 
 
-def demodulated(spectra, first, second, turn, cos_table, sin_table, blocks, per_block=8, interpret=False):
-    channels, parts, bands, frames = spectra.shape
+def demodulated(framed, bank, first, second, turn, cos_table, sin_table, blocks, per_block=8, interpret=False):
+    channels, frames, window = framed.shape
     rows = first.shape[1]
     pairs = rows // blocks
     levels = cos_table.shape[0]
@@ -104,7 +108,8 @@
         out_shape=jax.ShapeDtypeStruct((blocks, 2, channels, pairs, frames), jnp.bfloat16),
         grid=(channels // per_block,),
         in_specs=[
-            pl.BlockSpec((per_block, parts, bands, frames), lambda i: (i, 0, 0, 0)),
+            pl.BlockSpec((per_block, frames, window), lambda i: (i, 0, 0)),
+            pl.BlockSpec(bank.shape, lambda i: (0, 0)),
             pl.BlockSpec((per_block, rows), lambda i: (i, 0)),
             pl.BlockSpec((per_block, rows), lambda i: (i, 0)),
             pl.BlockSpec((per_block, rows), lambda i: (i, 0)),
@@ -113,7 +118,7 @@
         ],
         out_specs=pl.BlockSpec((blocks, 2, per_block, pairs, frames), lambda i: (0, 0, i, 0, 0)),
         interpret=interpret,
-    )(spectra, first, second, turn, cos_table, sin_table)
+    )(framed, bank, first, second, turn, cos_table, sin_table)
 
 
 def on_device(signal, pair_band, pair_offset, pair_owner):
@@ -129,10 +134,6 @@
         [pieces[:, part_index : part_index + frames_dev, :] for part_index in range(stride_count)],
         axis=2,
     )
-    spectra = jnp.einsum(
-        "cmn,nk->ckm", framed, bank_table, preferred_element_type=jnp.float32
-    ).astype(jnp.bfloat16)
-    spectra = spectra.reshape(channels, 2, BANDS, frames_dev)
 
     local_tables = jnp.stack([pair_band[0], pair_offset[0]], axis=0)
     spread = jnp.broadcast_to(local_tables[None], (blocks,) + local_tables.shape)
@@ -148,7 +149,8 @@
     cos_table, sin_table = turn_table(jnp.arange(levels, dtype=jnp.int32) * step, moment)
     shift_bins = (offset * (HOP * FRAMES // BANDS) - KEEP // 2) % FRAMES
     demod = demodulated(
-        spectra, band_first, band_first + offset, shift_bins // step, cos_table, sin_table, blocks
+        framed, bank_table.T, band_first, band_first + offset, shift_bins // step,
+        cos_table, sin_table, blocks,
     )
     arrived = lax.all_to_all(demod, "tm", split_axis=0, concat_axis=0, tiled=True)
     arrived = arrived.transpose(1, 2, 3, 0, 4)

time: 160 us -> 166 us (1.038)
  Pallas kernels: 6.69 us -> 13.3 us
  matrix products: 9.7 us -> 5.71 us
  other arithmetic: 13.2 us -> 16.7 us
    pallas_call x1, Pallas kernels: 6.69 us -> 13.3 us  [demodulated(): pl.pallas_call(demod_kernel, out_shape=jax.ShapeDtypeStruct((blocks, 2, c...]
    dot_general x1 -> x0, matrix products: 3.99 us -> none  [on_device(): jnp.einsum('cmn,nk->ckm', framed, bank_table, preferred_element_type=jnp....]
    concatenate x0 -> x1, other arithmetic: none -> 2.7 us  [on_device(): jnp.concatenate([pieces[:, part_index:part_index + frames_dev, :] for par...]
where the time goes in v6:
time: 166 us; the launch traced here: 165 us
  blocking collectives  86.6 us (52%)
  waiting for transfers between devices  17.7 us (11%)
  other arithmetic  16.7 us (10%)
  starting transfers between devices  16.6 us (10%)
  Pallas kernels  13.3 us (8%)
  local copies, waits for them, and re-layouts  8.57 us (5%)
  matrix products  5.71 us (3%)
    all_to_all x1, blocking collectives, on_device(): lax.all_to_all(outgoing, 'chan', split_axis=0, concat_axis=0, tiled=True)  86.6 us
    all_to_all x1, waiting for transfers between devices, on_device(): lax.all_to_all(demod, 'tm', split_axis=0, concat_axis=0, tiled=True)  17.7 us
    pallas_call x1, Pallas kernels, demodulated(): pl.pallas_call(demod_kernel, out_shape=jax.ShapeDtypeStruct((blocks, 2, c...  13.3 us
    all_to_all x1, starting transfers between devices, on_device(): lax.all_to_all(spread, 'tm', split_axis=0, concat_axis=0, tiled=True)  8.47 us
    all_to_all x1, starting transfers between devices, on_device(): lax.all_to_all(demod, 'tm', split_axis=0, concat_axis=0, tiled=True)  6.8 us
    convert_element_type x1, other arithmetic, fourier_tables(): cosine.reshape(FRAMES, KEEP).astype(jnp.bfloat16)  5.25 us
  transfers between devices with their start and end apart: 3, of which 1 were waited for; matrix products, arithmetic and copies ran while one was open for 11% of the time, Pallas kernels for 0%

profile of v6, /device:TPU:1, one launch (start us, length us, event | category | flops | bytes accessed | tf_op | source)
XLA Modules:
  0.0 165.2 jit_solution(10435967105370882224)
XLA Ops:
  0.0 0.7 slice.41
  0.7 1.3 collective-permute-start
  2.0 0.7 pad_add_fusion
  2.7 0.7 reshape.205
  3.5 8.5 %all-to-all-start = ((s32[16,1,512]{2,1,0:T(1,128)}), s32[16,1,512]{2,1,0:T(1,128)S(1)}, u32[]{:S(2)}, u32[]{:S(2)}) async-start(s32[16,1,512]{2,1,0:T(1,128)} %reshape.205), calls=%async_computation | async-start | bytes 65536 | tf_op jit(solution)/shard_map/all_to_all | solution.py:140
  12.1 1.1 multiply_convert_fusion.2
  13.2 0.7 fusion.43
  13.9 0.7 maximum_bitcast_fusion.bank_ref
  14.6 1.1 pad_maximum_fusion.1
  15.7 0.8 reshape.198
  16.5 0.9 fusion.47
  17.5 2.7 %pad_maximum_fusion.framed_ref = bf16[32,128,256]{2,1,0:T(8,128)(2,1)} fusion(bf16[32,128,64]{2,1,0:T(8,128)(2,1)S(1)} %get-tuple-element.8, bf16[32,128,64]{2,1,0:T(8,128)(2,1)S(1)} %get-tuple-element.9, bf16[32,128,64]{2,1,0:T(8,128)(2,1)S(1)} %get-tuple-element.10, bf16[32,128,64]{2,1,0:T(8,128)(2,1)S(1)} %get-tuple-element.7), kind=kLoop, calls=%fused_computation.7 | loop fusion | flops 8388608 | bytes 4194304 | tf_op jit(solution)/shard_map/concatenate | solution.py:133
  20.8 0.8 reduce.2
  22.4 13.3 %shard_map.46 = bf16[16,2,32,8,128]{4,3,2,1,0:T(8,128)(2,1)} custom-call(bf16[32,128,256]{2,1,0:T(8,128)(2,1)} %pad_maximum_fusion.framed_ref, bf16[512,256]{1,0:T(8,128)(2,1)} %maximum_bitcast_fusion.bank_ref, s32[32,128]{1,0:T(8,128)} %copy-done.2, s32[32,128]{1,0:T(8,128)} %get-tuple-element.16.second_ref, s32[32,128]{1,0:T(8,128)} %get-tuple-element.15.turn_ref, ...), custom_call_target="tpu_custom_call" | custom-call | tf_op jit(solution)/shard_map/pallas_call | solution.py:106
  35.7 6.8 %all-to-all-start.1 = ((bf16[16,2,32,8,128]{4,3,2,1,0:T(8,128)(2,1)}), bf16[16,2,32,8,128]{4,3,2,1,0:T(8,128)(2,1)S(1)}, u32[]{:S(2)}, u32[]{:S(2)}) async-start(bf16[16,2,32,8,128]{4,3,2,1,0:T(8,128)(2,1)} %shard_map.46), calls=%async_computation.1 | async-start | bytes 4194304 | tf_op jit(solution)/shard_map/all_to_all | solution.py:155
  44.2 1.1 fusion.30
  45.3 5.3 %multiply_convert_fusion.1 = (bf16[64,32,1024]{2,1,0:T(8,128)(2,1)}, bf16[64,32,1024]{2,1,0:T(8,128)(2,1)}) fusion(f32[32,1024]{1,0:T(8,128)S(1)} %get-tuple-element.21, f32[64,1024]{1,0:T(8,128)S(1)} %get-tuple-element.20, f32[32,1024]{1,0:T(8,128)S(1)} %get-tuple-element.22, f32[64,1024]{1,0:T(8,128)S(1)} %get-tuple-element.19), kind=kLoop, calls=%fused_computation.1 | loop fusion | flops 20971520 | bytes 9175040 | tf_op jit(solution)/shard_map/convert_element_type | solution.py:51
  50.6 17.7 %all-to-all-done.1 = bf16[16,2,32,8,128]{4,3,2,1,0:T(8,128)(2,1)S(1)} async-done(((bf16[16,2,32,8,128]{4,3,2,1,0:T(8,128)(2,1)}), bf16[16,2,32,8,128]{4,3,2,1,0:T(8,128)(2,1)S(1)}, u32[]{:S(2)}, u32[]{:S(2)}) %all-to-all-start.1) | async-done | bytes 2097184 | tf_op jit(solution)/shard_map/all_to_all | solution.py:155
  68.2 2.4 %copy.21 = bf16[2,32,8,16,128]{4,3,2,1,0:T(8,128)(2,1)S(1)} copy(bf16[2,32,8,16,128]{4,2,1,0,3:T(8,128)(2,1)S(1)} %bitcast.56) | data formatting | bytes 4194304 | tf_op jit(solution)/shard_map/transpose | solution.py:156
  70.7 2.4 %fusion.2 = f32[512,1024]{1,0:T(8,128)S(1)} fusion(bf16[2048,1024]{1,0:T(8,128)(2,1)S(1)} %bitcast.58, bf16[64,8,16,128]{3,2,1,0:T(8,128)(2,1)S(1)} %bitcast.59), kind=kOutput, calls=%fused_computation.5 | convolution fusion | flops 2147483648 | bytes 8388608 | tf_op jit(solution)/shard_map/dot_general | solution.py:161
  73.1 2.4 %fusion = f32[512,1024]{1,0:T(8,128)S(1)} fusion(bf16[2048,1024]{1,0:T(8,128)(2,1)S(1)} %bitcast.57, bf16[64,8,16,128]{3,2,1,0:T(8,128)(2,1)S(1)} %bitcast.60), kind=kOutput, calls=%fused_computation.3 | convolution fusion | flops 2147483648 | bytes 8388608 | tf_op jit(solution)/shard_map/dot_general | solution.py:162
  76.0 1.0 convolution_convert_fusion
  77.0 86.6 %all_to_all.15 = bf16[16,48,2048]{2,1,0:T(8,128)(2,1)S(1)} all-to-all(bf16[16,48,2048]{2,1,0:T(8,128)(2,1)S(1)} %bitcast.54), channel_id=1, replica_groups=mesh['chan'=16,'tm'=16] {'chan'}, dimensions={0} | all-to-all | bytes 6291456 | tf_op jit(solution)/shard_map/all_to_all | solution.py:180
  163.6 1.7 %copy.34 = bf16[1,1,16,48,2048]{4,3,2,1,0:T(8,128)(2,1)} copy(bf16[1,1,16,48,2048]{4,3,2,1,0:T(8,128)(2,1)S(1)} %bitcast.55) | data formatting | bytes 6291456
  (34 shorter events, 3.8 us)
Async XLA Ops:
  0.7 13.9 %collective-permute-start = (bf16[32,192]{1,0:T(8,128)(2,1)S(1)}, bf16[32,192]{1,0:T(8,128)(2,1)S(1)}, u32[]{:S(2)}, u32[]{:S(2)}) collective-permute-start(bf16[32,192]{1,0:T(8,128)(2,1)S(1)} %slice.41), channel_id=1, source_target_pairs={{1,0},{2,1},{3,2},{4,3},{5,4},{6,5},{7,6},{8,7},{9,8},{10,9},{11,1... | collective-permute-start | bytes 36872 | tf_op jit(solution)/shard_map/ppermute | solution.py:19
  3.5 16.7 %all-to-all-start = ((s32[16,1,512]{2,1,0:T(1,128)}), s32[16,1,512]{2,1,0:T(1,128)S(1)}, u32[]{:S(2)}, u32[]{:S(2)}) async-start(s32[16,1,512]{2,1,0:T(1,128)} %reshape.205), calls=%async_computation | async-start | bytes 65536 | tf_op jit(solution)/shard_map/all_to_all | solution.py:140
  21.7 0.7 copy-start.2
  35.7 6.8 %copy-start.3 = (s32[1,32,8,1]{1,3,2,0:T(1,128)S(1)}, s32[1,32,8,1]{1,3,2,0:T(1,128)}, u32[]{:S(2)}) copy-start(s32[1,32,8,1]{1,3,2,0:T(1,128)} %param.7) | copy-start | bytes 3076
  35.7 32.6 %all-to-all-start.1 = ((bf16[16,2,32,8,128]{4,3,2,1,0:T(8,128)(2,1)}), bf16[16,2,32,8,128]{4,3,2,1,0:T(8,128)(2,1)S(1)}, u32[]{:S(2)}, u32[]{:S(2)}) async-start(bf16[16,2,32,8,128]{4,3,2,1,0:T(8,128)(2,1)} %shard_map.46), calls=%async_computation.1 | async-start | bytes 4194304 | tf_op jit(solution)/shard_map/all_to_all | solution.py:155
  68.2 2.4 %copy-start.1 = (bf16[64,32,1024]{2,1,0:T(8,128)(2,1)S(1)}, bf16[64,32,1024]{2,1,0:T(8,128)(2,1)}, u32[]{:S(2)}) copy-start(bf16[64,32,1024]{2,1,0:T(8,128)(2,1)} %get-tuple-element.11) | copy-start | bytes 12582916
  70.7 2.4 %copy-start = (bf16[64,32,1024]{2,1,0:T(8,128)(2,1)S(1)}, bf16[64,32,1024]{2,1,0:T(8,128)(2,1)}, u32[]{:S(2)}) copy-start(bf16[64,32,1024]{2,1,0:T(8,128)(2,1)} %get-tuple-element.12) | copy-start | bytes 12582916

commit v7 on v5

--- a/solution.py
+++ b/solution.py
@@ -135,6 +135,7 @@
     spectra = spectra.reshape(channels, 2, BANDS, frames_dev)
 
     local_tables = jnp.stack([pair_band[0], pair_offset[0]], axis=0)
+    spectra, local_tables = lax.optimization_barrier((spectra, local_tables))
     spread = jnp.broadcast_to(local_tables[None], (blocks,) + local_tables.shape)
     tables = lax.all_to_all(spread, "tm", split_axis=0, concat_axis=0, tiled=True)
     bands_all = tables[:, 0].transpose(1, 0, 2)

time: 160 us -> 165 us (1.031)
  waiting for transfers between devices: 17.7 us -> 24.8 us
  starting transfers between devices: 16.6 us -> 14.1 us
    all_to_all x1, waiting for transfers between devices: 0.01 us -> 5.77 us  [on_device(): lax.all_to_all(spread, 'tm', split_axis=0, concat_axis=0, tiled=True)]
    all_to_all x1, starting transfers between devices: 6.81 us -> 4.03 us  [on_device(): lax.all_to_all(demod, 'tm', split_axis=0, concat_axis=0, tiled=True)]
    ppermute x1, waiting for transfers between devices: 0.01 us -> 1.87 us  [passed_along(): return lax.ppermute(array, axis, pairs)]
  transfers between devices with their start and end apart: 3 -> 3, of which waited for: 1 -> 3; matrix products, arithmetic and copies ran while one was open for 11% -> 7% of each run, Pallas kernels for 0% -> 0%
where the time goes in v7:
time: 165 us; the launch traced here: 164 us
  blocking collectives  87.2 us (53%)
  waiting for transfers between devices  24.8 us (15%)
  starting transfers between devices  14.1 us (9%)
  other arithmetic  13.2 us (8%)
  matrix products  9.72 us (6%)
  local copies, waits for them, and re-layouts  8.48 us (5%)
  Pallas kernels  6.7 us (4%)
    all_to_all x1, blocking collectives, on_device(): lax.all_to_all(outgoing, 'chan', split_axis=0, concat_axis=0, tiled=True)  87.2 us
    all_to_all x1, waiting for transfers between devices, on_device(): lax.all_to_all(demod, 'tm', split_axis=0, concat_axis=0, tiled=True)  17.1 us
    all_to_all x1, starting transfers between devices, on_device(): lax.all_to_all(spread, 'tm', split_axis=0, concat_axis=0, tiled=True)  8.83 us
    pallas_call x1, Pallas kernels, demodulated(): pl.pallas_call(demod_kernel, out_shape=jax.ShapeDtypeStruct((blocks, 2, c...  6.7 us
    all_to_all x1, waiting for transfers between devices, on_device(): lax.all_to_all(spread, 'tm', split_axis=0, concat_axis=0, tiled=True)  5.77 us
    convert_element_type x1, other arithmetic, fourier_tables(): cosine.reshape(FRAMES, KEEP).astype(jnp.bfloat16)  5.25 us
    all_to_all x1, starting transfers between devices, on_device(): lax.all_to_all(demod, 'tm', split_axis=0, concat_axis=0, tiled=True)  4.03 us
    dot_general x1, matrix products, on_device(): jnp.einsum('cmn,nk->ckm', framed, bank_table, preferred_element_type=jnp....  4.01 us
  transfers between devices with their start and end apart: 3, of which 3 were waited for; matrix products, arithmetic and copies ran while one was open for 7% of the time, Pallas kernels for 0%

profile of v7, /device:TPU:1, one launch (start us, length us, event | category | flops | bytes accessed | tf_op | source)
XLA Modules:
  0.0 164.4 jit_solution(16446631786242703155)
XLA Ops:
  0.0 0.7 slice.41
  0.7 1.3 collective-permute-start
  2.1 1.1 multiply_convert_fusion.2
  3.3 0.7 pad_add_fusion
  4.0 1.9 %collective-permute-done = bf16[32,192]{1,0:T(8,128)(2,1)S(1)} collective-permute-done((bf16[32,192]{1,0:T(8,128)(2,1)S(1)}, bf16[32,192]{1,0:T(8,128)(2,1)S(1)}, u32[]{:S(2)}, u32[]{:S(2)}) %collective-permute-start) | collective-permute-done | bytes 12320 | tf_op jit(solution)/shard_map/ppermute | solution.py:19
  5.9 1.1 pad_maximum_fusion
  6.9 0.8 reshape.201
  7.7 0.9 fusion.57
  8.7 4.0 %convolution_convert_fusion.1 = bf16[512,32,128]{2,0,1:T(8,128)(2,1)} fusion(bf16[32,128,64]{2,1,0:T(8,128)(2,1)S(1)} %get-tuple-element.12, bf16[32,128,64]{2,1,0:T(8,128)(2,1)S(1)} %get-tuple-element.13, bf16[32,128,64]{2,1,0:T(8,128)(2,1)S(1)} %get-tuple-element.14, bf16[32,128,64]{2,1,0:T(8,128)(2,1)S(1)} %get-tuple-element.11, ...), kind=kOutput, calls=%fused_computation.3 | convolution fusion | flops 1084751872 | bytes 6553600 | tf_op jit(solution)/shard_map/cmn,nk->ckm/dot_general | solution.py:132
  12.7 0.7 reshape.210
  13.4 8.8 %all-to-all-start = ((s32[16,1,512]{2,1,0:T(1,128)}), s32[16,1,512]{2,1,0:T(1,128)S(1)}, u32[]{:S(2)}, u32[]{:S(2)}) async-start(s32[16,1,512]{2,1,0:T(1,128)} %reshape.210), calls=%async_computation | async-start | bytes 65536 | tf_op jit(solution)/shard_map/all_to_all | solution.py:140
  23.0 5.8 %all-to-all-done = s32[16,1,512]{2,1,0:T(1,128)S(1)} async-done(((s32[16,1,512]{2,1,0:T(1,128)}), s32[16,1,512]{2,1,0:T(1,128)S(1)}, u32[]{:S(2)}, u32[]{:S(2)}) %all-to-all-start) | async-done | bytes 32800 | tf_op jit(solution)/shard_map/all_to_all | solution.py:140
  29.3 0.7 reduce.2
  30.9 6.7 %shard_map.46 = bf16[16,2,32,8,128]{4,3,2,1,0:T(8,128)(2,1)} custom-call(bf16[32,2,256,128]{3,2,1,0:T(8,128)(2,1)} %bitcast.61, s32[32,128]{1,0:T(8,128)} %copy-done.2, s32[32,128]{1,0:T(8,128)} %get-tuple-element.20.second_ref, s32[32,128]{1,0:T(8,128)} %get-tuple-element.19.turn_ref, f32[4,128]{1,0:T(4,128)} %get-tuple-element.22.cos_ref, ...), custom_call_target="tpu_custom_call" | custom-call | tf_op jit(solution)/shard_map/pallas_call | solution.py:102
  37.6 4.0 %all-to-all-start.1 = ((bf16[16,2,32,8,128]{4,3,2,1,0:T(8,128)(2,1)}), bf16[16,2,32,8,128]{4,3,2,1,0:T(8,128)(2,1)S(1)}, u32[]{:S(2)}, u32[]{:S(2)}) async-start(bf16[16,2,32,8,128]{4,3,2,1,0:T(8,128)(2,1)} %shard_map.46), calls=%async_computation.1 | async-start | bytes 4194304 | tf_op jit(solution)/shard_map/all_to_all | solution.py:154
  43.4 1.1 fusion.39
  44.5 5.3 %multiply_convert_fusion.1 = (bf16[64,32,1024]{2,1,0:T(8,128)(2,1)}, bf16[64,32,1024]{2,1,0:T(8,128)(2,1)}) fusion(f32[32,1024]{1,0:T(8,128)S(1)} %get-tuple-element.27, f32[64,1024]{1,0:T(8,128)S(1)} %get-tuple-element.24, f32[32,1024]{1,0:T(8,128)S(1)} %get-tuple-element.28, f32[64,1024]{1,0:T(8,128)S(1)} %get-tuple-element.23), kind=kLoop, calls=%fused_computation.1 | loop fusion | flops 20971520 | bytes 9175040 | tf_op jit(solution)/shard_map/convert_element_type | solution.py:51
  49.7 17.1 %all-to-all-done.1 = bf16[16,2,32,8,128]{4,3,2,1,0:T(8,128)(2,1)S(1)} async-done(((bf16[16,2,32,8,128]{4,3,2,1,0:T(8,128)(2,1)}), bf16[16,2,32,8,128]{4,3,2,1,0:T(8,128)(2,1)S(1)}, u32[]{:S(2)}, u32[]{:S(2)}) %all-to-all-start.1) | async-done | bytes 2097184 | tf_op jit(solution)/shard_map/all_to_all | solution.py:154
  66.9 2.4 %copy.21 = bf16[2,32,8,16,128]{4,3,2,1,0:T(8,128)(2,1)S(1)} copy(bf16[2,32,8,16,128]{4,2,1,0,3:T(8,128)(2,1)S(1)} %bitcast.60) | data formatting | bytes 4194304 | tf_op jit(solution)/shard_map/transpose | solution.py:155
  69.3 2.4 %fusion.2 = f32[512,1024]{1,0:T(8,128)S(1)} fusion(bf16[2048,1024]{1,0:T(8,128)(2,1)S(1)} %bitcast.63, bf16[64,8,16,128]{3,2,1,0:T(8,128)(2,1)S(1)} %bitcast.64), kind=kOutput, calls=%fused_computation.6 | convolution fusion | flops 2147483648 | bytes 8388608 | tf_op jit(solution)/shard_map/dot_general | solution.py:160
  71.7 2.4 %fusion = f32[512,1024]{1,0:T(8,128)S(1)} fusion(bf16[2048,1024]{1,0:T(8,128)(2,1)S(1)} %bitcast.62, bf16[64,8,16,128]{3,2,1,0:T(8,128)(2,1)S(1)} %bitcast.65), kind=kOutput, calls=%fused_computation.4 | convolution fusion | flops 2147483648 | bytes 8388608 | tf_op jit(solution)/shard_map/dot_general | solution.py:161
  74.6 1.0 convolution_convert_fusion
  75.6 87.2 %all_to_all.15 = bf16[16,48,2048]{2,1,0:T(8,128)(2,1)S(1)} all-to-all(bf16[16,48,2048]{2,1,0:T(8,128)(2,1)S(1)} %bitcast.58), channel_id=1, replica_groups=mesh['chan'=16,'tm'=16] {'chan'}, dimensions={0} | all-to-all | bytes 6291456 | tf_op jit(solution)/shard_map/all_to_all | solution.py:179
  162.8 1.7 %copy.34 = bf16[1,1,16,48,2048]{4,3,2,1,0:T(8,128)(2,1)} copy(bf16[1,1,16,48,2048]{4,3,2,1,0:T(8,128)(2,1)S(1)} %bitcast.59) | data formatting | bytes 6291456
  (33 shorter events, 4.4 us)
Async XLA Ops:
  0.7 5.1 %collective-permute-start = (bf16[32,192]{1,0:T(8,128)(2,1)S(1)}, bf16[32,192]{1,0:T(8,128)(2,1)S(1)}, u32[]{:S(2)}, u32[]{:S(2)}) collective-permute-start(bf16[32,192]{1,0:T(8,128)(2,1)S(1)} %slice.41), channel_id=1, source_target_pairs={{1,0},{2,1},{3,2},{4,3},{5,4},{6,5},{7,6},{8,7},{9,8},{10,9},{11,1... | collective-permute-start | bytes 36872 | tf_op jit(solution)/shard_map/ppermute | solution.py:19
  13.4 15.3 %all-to-all-start = ((s32[16,1,512]{2,1,0:T(1,128)}), s32[16,1,512]{2,1,0:T(1,128)S(1)}, u32[]{:S(2)}, u32[]{:S(2)}) async-start(s32[16,1,512]{2,1,0:T(1,128)} %reshape.210), calls=%async_computation | async-start | bytes 65536 | tf_op jit(solution)/shard_map/all_to_all | solution.py:140
  30.2 0.7 copy-start.2
  37.6 4.0 %copy-start.3 = (s32[1,32,8,1]{1,3,2,0:T(1,128)S(1)}, s32[1,32,8,1]{1,3,2,0:T(1,128)}, u32[]{:S(2)}) copy-start(s32[1,32,8,1]{1,3,2,0:T(1,128)} %param.7) | copy-start | bytes 3076
  37.6 29.3 %all-to-all-start.1 = ((bf16[16,2,32,8,128]{4,3,2,1,0:T(8,128)(2,1)}), bf16[16,2,32,8,128]{4,3,2,1,0:T(8,128)(2,1)S(1)}, u32[]{:S(2)}, u32[]{:S(2)}) async-start(bf16[16,2,32,8,128]{4,3,2,1,0:T(8,128)(2,1)} %shard_map.46), calls=%async_computation.1 | async-start | bytes 4194304 | tf_op jit(solution)/shard_map/all_to_all | solution.py:154
  66.9 2.4 %copy-start.1 = (bf16[64,32,1024]{2,1,0:T(8,128)(2,1)S(1)}, bf16[64,32,1024]{2,1,0:T(8,128)(2,1)}, u32[]{:S(2)}) copy-start(bf16[64,32,1024]{2,1,0:T(8,128)(2,1)} %get-tuple-element.15) | copy-start | bytes 12582916
  69.3 2.4 %copy-start = (bf16[64,32,1024]{2,1,0:T(8,128)(2,1)S(1)}, bf16[64,32,1024]{2,1,0:T(8,128)(2,1)}, u32[]{:S(2)}) copy-start(bf16[64,32,1024]{2,1,0:T(8,128)(2,1)} %get-tuple-element.16) | copy-start | bytes 12582916

commit v8 on v5

--- a/solution.py
+++ b/solution.py
@@ -151,16 +151,18 @@
         spectra, band_first, band_first + offset, shift_bins // step, cos_table, sin_table, blocks
     )
     arrived = lax.all_to_all(demod, "tm", split_axis=0, concat_axis=0, tiled=True)
-    arrived = arrived.transpose(1, 2, 3, 0, 4)
     rows = channels * pairs
-    arrived = arrived.reshape(2 * rows, blocks * frames_dev)
-
     cosine_table, sine_table = fourier_tables()
-    with_cos = jnp.dot(arrived, cosine_table, preferred_element_type=jnp.float32)
-    with_sin = jnp.dot(arrived, sine_table, preferred_element_type=jnp.float32)
-    corr_re = with_cos[:rows] + with_sin[rows:]
-    corr_im = with_cos[rows:] - with_sin[:rows]
-    correlation = jnp.concatenate([corr_re, corr_im], axis=1).astype(jnp.bfloat16)
+    dft_table = jnp.stack(
+        [
+            jnp.concatenate([cosine_table, -sine_table], axis=1),
+            jnp.concatenate([sine_table, cosine_table], axis=1),
+        ],
+        axis=0,
+    ).reshape(2, blocks, frames_dev, 2 * KEEP)
+    correlation = jnp.einsum(
+        "tpcqm,ptmf->cqf", arrived, dft_table, preferred_element_type=jnp.float32
+    ).astype(jnp.bfloat16).reshape(rows, 2 * KEEP)
 
     owner = pair_owner[0, :, :, 0].reshape(-1)
     groups = lax.axis_size("chan")

time: 160 us -> 165 us (1.031)
  matrix products: 9.7 us -> 16.6 us
  waiting for transfers between devices: 17.7 us -> 15.2 us
  other arithmetic: 13.2 us -> 15.2 us
    dot_general x1, matrix products: 0.99 us -> 12.6 us  [on_device(): jnp.dot(placing, correlation, preferred_element_type=jnp.float32)]
    dot_general x2 -> x0, matrix products: 4.72 us -> none  [the longest x1 2.36 us: on_device(): jnp.dot(arrived, cosine_table, preferred_element_type=jnp.float32)]
    neg x0 -> x1, other arithmetic: none -> 3.27 us  [on_device(): -sine_table]
    all_to_all x1, waiting for transfers between devices: 17.7 us -> 15.2 us  [on_device(): lax.all_to_all(demod, 'tm', split_axis=0, concat_axis=0, tiled=True)]
    transpose x1 -> x0, local copies, waits for them, and re-layouts: 2.43 us -> none  [on_device(): arrived = arrived.transpose(1, 2, 3, 0, 4)]
    unnamed x13 -> x15, local copies, waits for them, and re-layouts: 2.59 us -> 3.91 us
  transfers between devices with their start and end apart: 3 -> 3, of which waited for: 1 -> 1; matrix products, arithmetic and copies ran while one was open for 11% -> 13% of each run, Pallas kernels for 0% -> 0%
where the time goes in v8:
time: 165 us; the launch traced here: 164 us
  blocking collectives  86.6 us (52%)
  matrix products  16.6 us (10%)
  starting transfers between devices  16.4 us (10%)
  other arithmetic  15.2 us (9%)
  waiting for transfers between devices  15.2 us (9%)
  local copies, waits for them, and re-layouts  7.37 us (4%)
  Pallas kernels  6.69 us (4%)
    all_to_all x1, blocking collectives, on_device(): lax.all_to_all(outgoing, 'chan', split_axis=0, concat_axis=0, tiled=True)  86.6 us
    all_to_all x1, waiting for transfers between devices, on_device(): lax.all_to_all(demod, 'tm', split_axis=0, concat_axis=0, tiled=True)  15.2 us
    dot_general x1, matrix products, on_device(): jnp.dot(placing, correlation, preferred_element_type=jnp.float32)  12.6 us
    all_to_all x1, starting transfers between devices, on_device(): lax.all_to_all(spread, 'tm', split_axis=0, concat_axis=0, tiled=True)  8.47 us
    pallas_call x1, Pallas kernels, demodulated(): pl.pallas_call(demod_kernel, out_shape=jax.ShapeDtypeStruct((blocks, 2, c...  6.69 us
    all_to_all x1, starting transfers between devices, on_device(): lax.all_to_all(demod, 'tm', split_axis=0, concat_axis=0, tiled=True)  6.67 us
    convert_element_type x1, other arithmetic, fourier_tables(): sine.reshape(FRAMES, KEEP).astype(jnp.bfloat16)  4.48 us
    dot_general x1, matrix products, on_device(): jnp.einsum('cmn,nk->ckm', framed, bank_table, preferred_element_type=jnp....  3.98 us
  transfers between devices with their start and end apart: 3, of which 1 were waited for; matrix products, arithmetic and copies ran while one was open for 13% of the time, Pallas kernels for 0%

profile of v8, /device:TPU:1, one launch (start us, length us, event | category | flops | bytes accessed | tf_op | source)
XLA Modules:
  0.0 164.2 jit_solution(9130762420048388927)
XLA Ops:
  0.0 0.7 slice.29
  0.7 1.3 collective-permute-start
  2.0 0.7 pad_add_fusion
  2.7 0.7 reshape.279
  3.5 8.5 %all-to-all-start = ((s32[16,1,512]{2,1,0:T(1,128)}), s32[16,1,512]{2,1,0:T(1,128)S(1)}, u32[]{:S(2)}, u32[]{:S(2)}) async-start(s32[16,1,512]{2,1,0:T(1,128)} %reshape.279), calls=%async_computation | async-start | bytes 65536 | tf_op jit(solution)/shard_map/all_to_all | solution.py:139
  12.1 1.1 multiply_convert_fusion.2
  13.2 0.7 fusion.48
  13.9 1.1 pad_maximum_fusion
  15.0 0.8 reshape.268
  15.8 0.9 fusion.54
  16.8 4.0 %convolution_convert_fusion.1 = bf16[512,32,128]{2,0,1:T(8,128)(2,1)} fusion(bf16[32,128,64]{2,1,0:T(8,128)(2,1)S(1)} %get-tuple-element.6, bf16[32,128,64]{2,1,0:T(8,128)(2,1)S(1)} %get-tuple-element.7, bf16[32,128,64]{2,1,0:T(8,128)(2,1)S(1)} %get-tuple-element.8, bf16[32,128,64]{2,1,0:T(8,128)(2,1)S(1)} %get-tuple-element.5, ...), kind=kOutput, calls=%fused_computation.6 | convolution fusion | flops 1084751872 | bytes 6553600 | tf_op jit(solution)/shard_map/cmn,nk->ckm/dot_general | solution.py:132
  21.3 0.7 reduce.2
  22.2 0.6 add_select_fusion.3
  22.9 6.7 %shard_map.46 = bf16[16,2,32,8,128]{4,3,2,1,0:T(8,128)(2,1)} custom-call(bf16[32,2,256,128]{3,2,1,0:T(8,128)(2,1)} %bitcast.78, s32[32,128]{1,0:T(8,128)} %copy-done.2, s32[32,128]{1,0:T(8,128)} %get-tuple-element.14.second_ref, s32[32,128]{1,0:T(8,128)} %get-tuple-element.13.turn_ref, f32[4,128]{1,0:T(4,128)} %get-tuple-element.16.cos_ref, ...), custom_call_target="tpu_custom_call" | custom-call | tf_op jit(solution)/shard_map/pallas_call | solution.py:102
  29.6 6.7 %all-to-all-start.1 = ((bf16[16,2,32,8,128]{4,3,2,1,0:T(8,128)(2,1)}), bf16[16,2,32,8,128]{4,3,2,1,0:T(8,128)(2,1)S(1)}, u32[]{:S(2)}, u32[]{:S(2)}) async-start(bf16[16,2,32,8,128]{4,3,2,1,0:T(8,128)(2,1)} %shard_map.46), calls=%async_computation.1 | async-start | bytes 4194304 | tf_op jit(solution)/shard_map/all_to_all | solution.py:153
  36.5 0.6 reduce-window.6
  37.9 1.1 fusion.35
  39.0 4.5 %multiply_convert_fusion = (bf16[64,32,1024]{2,1,0:T(8,128)(2,1)S(1)}, bf16[64,32,1024]{2,1,0:T(8,128)(2,1)}) fusion(f32[32,1024]{1,0:T(8,128)S(1)} %get-tuple-element.19, f32[64,1024]{1,0:T(8,128)S(1)} %get-tuple-element.18, f32[32,1024]{1,0:T(8,128)S(1)} %get-tuple-element.20, f32[64,1024]{1,0:T(8,128)S(1)} %get-tuple-element.17), kind=kLoop, calls=%fused_computation.2 | loop fusion | flops 20971520 | bytes 9175040 | tf_op jit(solution)/shard_map/convert_element_type | solution.py:52
  43.5 3.3 %neg.17 = bf16[1,16,128,1024]{3,2,1,0:T(8,128)(2,1)} negate(bf16[1,16,128,1024]{3,2,1,0:T(8,128)(2,1)S(1)} %bitcast.75) | non-fusion elementwise | flops 2097152 | bytes 8388608 | tf_op jit(solution)/shard_map/neg | solution.py:158
  46.8 15.2 %all-to-all-done.1 = bf16[16,2,32,8,128]{4,3,2,1,0:T(8,128)(2,1)S(1)} async-done(((bf16[16,2,32,8,128]{4,3,2,1,0:T(8,128)(2,1)}), bf16[16,2,32,8,128]{4,3,2,1,0:T(8,128)(2,1)S(1)}, u32[]{:S(2)}, u32[]{:S(2)}) %all-to-all-start.1) | async-done | bytes 2097184 | tf_op jit(solution)/shard_map/all_to_all | solution.py:153
  62.0 1.3 copy-done.1
  63.3 12.6 %convolution_convert_fusion = bf16[768,2048]{1,0:T(8,128)(2,1)S(1)} fusion(s32[256]{0:T(256)S(1)} %multiply_add_fusion, bf16[1,16,128,1024]{3,2,1,0:T(8,128)(2,1)} %bitcast.79, bf16[1,16,128,1024]{3,2,1,0:T(8,128)(2,1)} %bitcast.76, bf16[1,16,128,1024]{3,2,1,0:T(8,128)(2,1)} %neg.17, bf16[16,2,32,8,128]{4,3,2,1,0:T(8,128)(2,1)} %copy-done.1), kind=kOutput, calls=%fused_computation.4 | convolution fusion | flops 5169676288 | bytes 17826816 | tf_op jit(solution)/shard_map/dot_general | solution.py:176
  75.9 86.6 %all_to_all.15 = bf16[16,48,2048]{2,1,0:T(8,128)(2,1)S(1)} all-to-all(bf16[16,48,2048]{2,1,0:T(8,128)(2,1)S(1)} %bitcast.80), channel_id=1, replica_groups=mesh['chan'=16,'tm'=16] {'chan'}, dimensions={0} | all-to-all | bytes 6291456 | tf_op jit(solution)/shard_map/all_to_all | solution.py:180
  162.5 1.7 %copy.32 = bf16[1,1,16,48,2048]{4,3,2,1,0:T(8,128)(2,1)} copy(bf16[1,1,16,48,2048]{4,3,2,1,0:T(8,128)(2,1)S(1)} %bitcast.77) | data formatting | bytes 6291456
  (33 shorter events, 2.0 us)
Async XLA Ops:
  0.7 13.2 %collective-permute-start = (bf16[32,192]{1,0:T(8,128)(2,1)S(1)}, bf16[32,192]{1,0:T(8,128)(2,1)S(1)}, u32[]{:S(2)}, u32[]{:S(2)}) collective-permute-start(bf16[32,192]{1,0:T(8,128)(2,1)S(1)} %slice.29), channel_id=1, source_target_pairs={{1,0},{2,1},{3,2},{4,3},{5,4},{6,5},{7,6},{8,7},{9,8},{10,9},{11,1... | collective-permute-start | bytes 36872 | tf_op jit(solution)/shard_map/ppermute | solution.py:19
  3.5 17.3 %all-to-all-start = ((s32[16,1,512]{2,1,0:T(1,128)}), s32[16,1,512]{2,1,0:T(1,128)S(1)}, u32[]{:S(2)}, u32[]{:S(2)}) async-start(s32[16,1,512]{2,1,0:T(1,128)} %reshape.279), calls=%async_computation | async-start | bytes 65536 | tf_op jit(solution)/shard_map/all_to_all | solution.py:139
  22.2 0.7 copy-start.2
  22.9 13.4 %copy-start.4 = (s32[1,32,8,1]{1,3,2,0:T(1,128)S(1)}, s32[1,32,8,1]{1,3,2,0:T(1,128)}, u32[]{:S(2)}) copy-start(s32[1,32,8,1]{1,3,2,0:T(1,128)} %param.7) | copy-start | bytes 3076
  29.6 32.4 %all-to-all-start.1 = ((bf16[16,2,32,8,128]{4,3,2,1,0:T(8,128)(2,1)}), bf16[16,2,32,8,128]{4,3,2,1,0:T(8,128)(2,1)S(1)}, u32[]{:S(2)}, u32[]{:S(2)}) async-start(bf16[16,2,32,8,128]{4,3,2,1,0:T(8,128)(2,1)} %shard_map.46), calls=%async_computation.1 | async-start | bytes 4194304 | tf_op jit(solution)/shard_map/all_to_all | solution.py:153
  37.3 6.1 %copy-start.3 = (s32[16,3]{0,1:T(4,128)}, s32[16,3]{0,1:T(4,128)S(1)}, u32[]{:S(2)}) copy-start(s32[16,3]{0,1:T(4,128)S(1)} %reduce-window.9) | copy-start | bytes 580
  43.5 3.3 %copy-start = (bf16[64,32,1024]{2,1,0:T(8,128)(2,1)}, bf16[64,32,1024]{2,1,0:T(8,128)(2,1)S(1)}, u32[]{:S(2)}) copy-start(bf16[64,32,1024]{2,1,0:T(8,128)(2,1)S(1)} %get-tuple-element.9) | copy-start | bytes 12582916
  43.5 3.3 %slice-start = ((s32[16,3]{0,1:T(4,128)}), s32[16,2]{0,1:T(2,128)S(1)}, s32[]{:S(2)}) async-start(s32[16,3]{0,1:T(4,128)} %copy-done.3), calls=%async_computation.3 | async-start | bytes 2048 | tf_op jit(solution)/shard_map/slice.1
  62.0 1.3 copy-start.1

commit v9 on v5

--- a/solution.py
+++ b/solution.py
@@ -36,17 +36,22 @@
     return jnp.cos(angle), jnp.sin(angle)
 
 
-def fourier_tables():
+def fourier_tables(frames_dev):
+    devices = FRAMES // frames_dev
+    fine = 32
+    coarse_count = FRAMES // fine
     cycles = jnp.arange(KEEP, dtype=jnp.int32)
-    coarse_cos, coarse_sin = turn_table(32 * jnp.arange(FRAMES // 32, dtype=jnp.int32), cycles)
-    fine_cos, fine_sin = turn_table(jnp.arange(32, dtype=jnp.int32), cycles)
+    coarse_cos, coarse_sin = turn_table(fine * jnp.arange(coarse_count, dtype=jnp.int32), cycles)
+    fine_cos, fine_sin = turn_table(jnp.arange(fine, dtype=jnp.int32), cycles)
+    outer = (devices, 1, coarse_count // devices, 1, KEEP)
+    inner = (1, 2, 1, fine // 2, KEEP)
+    coarse_cos = coarse_cos.reshape(outer)
+    coarse_sin = coarse_sin.reshape(outer)
+    fine_cos = fine_cos.reshape(fine // 2, 2, KEEP).transpose(1, 0, 2).reshape(inner)
+    fine_sin = fine_sin.reshape(fine // 2, 2, KEEP).transpose(1, 0, 2).reshape(inner)
     scale = 1.0 / math.sqrt(FRAMES)
-    cosine = (
-        coarse_cos[:, None, :] * fine_cos[None, :, :] - coarse_sin[:, None, :] * fine_sin[None, :, :]
-    ) * scale
-    sine = (
-        coarse_sin[:, None, :] * fine_cos[None, :, :] + coarse_cos[:, None, :] * fine_sin[None, :, :]
-    ) * scale
+    cosine = (coarse_cos * fine_cos - coarse_sin * fine_sin) * scale
+    sine = (coarse_sin * fine_cos + coarse_cos * fine_sin) * scale
     return (
         cosine.reshape(FRAMES, KEEP).astype(jnp.bfloat16),
         sine.reshape(FRAMES, KEEP).astype(jnp.bfloat16),
@@ -123,15 +128,28 @@
     blocks = lax.axis_size("tm")
     bank_table = bank_matrix(BANDS)
     sample_tail = passed_along(signal[:, : BANDS - HOP], "tm", -1)
-    records = jnp.concatenate([signal, sample_tail], axis=1)
-    pieces = records.reshape(channels, frames_dev + stride_count - 1, HOP)
-    framed = jnp.concatenate(
-        [pieces[:, part_index : part_index + frames_dev, :] for part_index in range(stride_count)],
-        axis=2,
-    )
-    spectra = jnp.einsum(
-        "cmn,nk->ckm", framed, bank_table, preferred_element_type=jnp.float32
+    half = frames_dev // 2
+    span = 2 * HOP
+    row_count = half + BANDS // span
+    records = jnp.concatenate(
+        [signal, sample_tail, jnp.zeros((channels, row_count * span - signal.shape[1] - BANDS + HOP), signal.dtype)],
+        axis=1,
+    ).reshape(channels, row_count, span)
+    even_windows = jnp.concatenate(
+        [records[:, j : j + half] for j in range(BANDS // span)], axis=2
+    )
+    odd_windows = jnp.concatenate(
+        [records[:, j : j + half] for j in range(BANDS // span + 1)], axis=2
+    )
+    edge = jnp.zeros((HOP, 2 * BANDS), bank_table.dtype)
+    odd_bank = jnp.concatenate([edge, bank_table, edge], axis=0)
+    even_spectra = jnp.einsum(
+        "cin,nk->cki", even_windows, bank_table, preferred_element_type=jnp.float32
     ).astype(jnp.bfloat16)
+    odd_spectra = jnp.einsum(
+        "cin,nk->cki", odd_windows, odd_bank, preferred_element_type=jnp.float32
+    ).astype(jnp.bfloat16)
+    spectra = jnp.concatenate([even_spectra, odd_spectra], axis=2)
     spectra = spectra.reshape(channels, 2, BANDS, frames_dev)
 
     local_tables = jnp.stack([pair_band[0], pair_offset[0]], axis=0)
@@ -142,7 +160,8 @@
     pairs = bands_all.shape[2]
     band_first = bands_all.reshape(channels, blocks * pairs)
     offset = offsets_all.reshape(channels, blocks * pairs)
-    moment = lax.axis_index("tm") * frames_dev + jnp.arange(frames_dev, dtype=jnp.int32)
+    local = jnp.arange(frames_dev, dtype=jnp.int32)
+    moment = lax.axis_index("tm") * frames_dev + 2 * (local % half) + local // half
     step = math.gcd(HOP * FRAMES // BANDS, KEEP // 2, FRAMES)
     levels = FRAMES // step
     cos_table, sin_table = turn_table(jnp.arange(levels, dtype=jnp.int32) * step, moment)
@@ -155,7 +174,7 @@
     rows = channels * pairs
     arrived = arrived.reshape(2 * rows, blocks * frames_dev)
 
-    cosine_table, sine_table = fourier_tables()
+    cosine_table, sine_table = fourier_tables(frames_dev)
     with_cos = jnp.dot(arrived, cosine_table, preferred_element_type=jnp.float32)
     with_sin = jnp.dot(arrived, sine_table, preferred_element_type=jnp.float32)
     corr_re = with_cos[:rows] + with_sin[rows:]

time: 160 us -> 166 us (1.038)
  local copies, waits for them, and re-layouts: 8.49 us -> 15.7 us
  other arithmetic: 13.2 us -> 15.9 us
  matrix products: 9.7 us -> 7.69 us
    concatenate x0 -> x2, local copies, waits for them, and re-layouts: none -> 7.59 us  [the longest x1 6.47 us: on_device(): spectra = jnp.concatenate([even_spectra, odd_spectra], axis=2)]
    dot_general x1 -> x2, matrix products: 3.99 us -> 1.98 us  [the longest x1 1.26 us: on_device(): jnp.einsum('cin,nk->cki', odd_windows, odd_bank, preferred_element_type=j...]
    cos x1 -> x2, other arithmetic: 1.09 us -> 3.02 us  [turn_table(): return (jnp.cos(angle), jnp.sin(angle))]
  transfers between devices with their start and end apart: 3 -> 3, of which waited for: 1 -> 1; matrix products, arithmetic and copies ran while one was open for 11% -> 16% of each run, Pallas kernels for 0% -> 0%
where the time goes in v9:
time: 166 us
  blocking collectives  86.6 us (52%)
  waiting for transfers between devices  16.5 us (10%)
  starting transfers between devices  16.4 us (10%)
  other arithmetic  15.9 us (10%)
  local copies, waits for them, and re-layouts  15.7 us (9%)
  matrix products  7.69 us (5%)
  Pallas kernels  6.69 us (4%)
    all_to_all x1, blocking collectives, on_device(): lax.all_to_all(outgoing, 'chan', split_axis=0, concat_axis=0, tiled=True)  86.6 us
    all_to_all x1, waiting for transfers between devices, on_device(): lax.all_to_all(demod, 'tm', split_axis=0, concat_axis=0, tiled=True)  16.5 us
    all_to_all x1, starting transfers between devices, on_device(): lax.all_to_all(spread, 'tm', split_axis=0, concat_axis=0, tiled=True)  8.47 us
    pallas_call x1, Pallas kernels, demodulated(): pl.pallas_call(demod_kernel, out_shape=jax.ShapeDtypeStruct((blocks, 2, c...  6.69 us
    all_to_all x1, starting transfers between devices, on_device(): lax.all_to_all(demod, 'tm', split_axis=0, concat_axis=0, tiled=True)  6.66 us
    concatenate x1, local copies, waits for them, and re-layouts, on_device(): spectra = jnp.concatenate([even_spectra, odd_spectra], axis=2)  6.47 us
    convert_element_type x1, other arithmetic, fourier_tables(): cosine.reshape(FRAMES, KEEP).astype(jnp.bfloat16)  5.14 us
  transfers between devices with their start and end apart: 3, of which 1 were waited for; matrix products, arithmetic and copies ran while one was open for 16% of the time, Pallas kernels for 0%

profile of v9, /device:TPU:1, one launch (start us, length us, event | category | flops | bytes accessed | tf_op | source)
XLA Modules:
  0.0 165.8 jit_solution(5883738023781813140)
XLA Ops:
  0.0 0.7 slice.40
  0.7 1.3 collective-permute-start
  2.7 0.7 reshape.212
  3.5 8.5 %all-to-all-start = ((s32[16,1,512]{2,1,0:T(1,128)}), s32[16,1,512]{2,1,0:T(1,128)S(1)}, u32[]{:S(2)}, u32[]{:S(2)}) async-start(s32[16,1,512]{2,1,0:T(1,128)} %reshape.212), calls=%async_computation | async-start | bytes 65536 | tf_op jit(solution)/shard_map/all_to_all | solution.py:157
  12.1 1.2 multiply_convert_fusion.2
  13.3 0.7 fusion.56
  14.0 0.8 copy.16
  14.8 1.1 concatenate.24
  16.6 0.7 convert_bitcast_fusion.1
  17.3 1.3 convert_bitcast_fusion
  18.6 2.4 %pad_maximum_fusion = bf16[32,512,128]{1,2,0:T(8,128)(2,1)} fusion(bf16[32,512,64]{1,2,0:T(8,128)(2,1)S(1)} %convert_bitcast_fusion, bf16[32,512,64]{1,2,0:T(8,128)(2,1)S(1)} %convert_bitcast_fusion.1), kind=kLoop, calls=%fused_computation.2 | loop fusion | flops 8388608 | bytes 8388608 | tf_op jit(solution)/shard_map/concatenate | solution.py:152
  21.0 6.5 %copy.19 = bf16[32,512,128]{2,1,0:T(8,128)(2,1)} copy(bf16[32,512,128]{1,2,0:T(8,128)(2,1)} %pad_maximum_fusion) | data formatting | bytes 8388608 | tf_op jit(solution)/shard_map/concatenate | solution.py:152
  28.0 0.7 reduce.2
  29.6 6.7 %shard_map.46 = bf16[16,2,32,8,128]{4,3,2,1,0:T(8,128)(2,1)} custom-call(bf16[32,2,256,128]{3,2,1,0:T(8,128)(2,1)} %bitcast.64, s32[32,128]{1,0:T(8,128)} %copy-done.2, s32[32,128]{1,0:T(8,128)} %get-tuple-element.15.second_ref, s32[32,128]{1,0:T(8,128)} %get-tuple-element.14.turn_ref, f32[4,128]{1,0:T(4,128)} %get-tuple-element.19.cos_ref, ...), custom_call_target="tpu_custom_call" | custom-call | tf_op jit(solution)/shard_map/pallas_call | solution.py:107
  36.3 6.7 %all-to-all-start.1 = ((bf16[16,2,32,8,128]{4,3,2,1,0:T(8,128)(2,1)}), bf16[16,2,32,8,128]{4,3,2,1,0:T(8,128)(2,1)S(1)}, u32[]{:S(2)}, u32[]{:S(2)}) async-start(bf16[16,2,32,8,128]{4,3,2,1,0:T(8,128)(2,1)} %shard_map.46), calls=%async_computation.1 | async-start | bytes 4194304 | tf_op jit(solution)/shard_map/all_to_all | solution.py:172
  44.6 2.4 %fusion.43 = (f32[16,4,1024]{2,1,0:T(4,128)S(1)}, f32[16,4,1024]{2,1,0:T(4,128)S(1)}) fusion(s32[16,4]{1,0:T(8,128)S(1)} %add_multiply_fusion), kind=kLoop, calls=%fused_computation.65 | loop fusion | flops 917504 | bytes 524544 | tf_op jit(solution)/shard_map/cos | solution.py:36
  47.1 5.1 %multiply_convert_fusion.1 = (bf16[16,2,4,16,1024]{4,3,2,1,0:T(8,128)(2,1)}, bf16[16,2,4,16,1024]{4,3,2,1,0:T(8,128)(2,1)}) fusion(f32[2,16,1024]{2,1,0:T(8,128)S(1)} %get-tuple-element.21, f32[16,4,1024]{2,1,0:T(4,128)S(1)} %get-tuple-element.17, f32[2,16,1024]{2,1,0:T(8,128)S(1)} %get-tuple-element.20, f32[16,4,1024]{2,1,0:T(4,128)S(1)} %get-tuple-element.16), kind=kLoop, calls=%fused_computation.1 | loop fusion | flops 20971520 | bytes 9175040 | tf_op jit(solution)/shard_map/convert_element_type | solution.py:56
  52.2 16.5 %all-to-all-done.1 = bf16[16,2,32,8,128]{4,3,2,1,0:T(8,128)(2,1)S(1)} async-done(((bf16[16,2,32,8,128]{4,3,2,1,0:T(8,128)(2,1)}), bf16[16,2,32,8,128]{4,3,2,1,0:T(8,128)(2,1)S(1)}, u32[]{:S(2)}, u32[]{:S(2)}) %all-to-all-start.1) | async-done | bytes 2097184 | tf_op jit(solution)/shard_map/all_to_all | solution.py:172
  68.7 2.4 %copy.24 = bf16[2,32,8,16,128]{4,3,2,1,0:T(8,128)(2,1)S(1)} copy(bf16[2,32,8,16,128]{4,2,1,0,3:T(8,128)(2,1)S(1)} %bitcast.66) | data formatting | bytes 4194304 | tf_op jit(solution)/shard_map/transpose | solution.py:173
  71.2 2.4 %fusion.2 = f32[512,1024]{1,0:T(8,128)S(1)} fusion(bf16[2048,1024]{1,0:T(8,128)(2,1)S(1)} %bitcast.68, bf16[64,8,16,128]{3,2,1,0:T(8,128)(2,1)S(1)} %bitcast.69), kind=kOutput, calls=%fused_computation.6 | convolution fusion | flops 2147483648 | bytes 8388608 | tf_op jit(solution)/shard_map/dot_general | solution.py:178
  73.6 2.4 %fusion = f32[512,1024]{1,0:T(8,128)S(1)} fusion(bf16[2048,1024]{1,0:T(8,128)(2,1)S(1)} %bitcast.67, bf16[64,8,16,128]{3,2,1,0:T(8,128)(2,1)S(1)} %bitcast.70), kind=kOutput, calls=%fused_computation.4 | convolution fusion | flops 2147483648 | bytes 8388608 | tf_op jit(solution)/shard_map/dot_general | solution.py:179
  76.5 1.0 convolution_convert_fusion
  77.5 86.6 %all_to_all.15 = bf16[16,48,2048]{2,1,0:T(8,128)(2,1)S(1)} all-to-all(bf16[16,48,2048]{2,1,0:T(8,128)(2,1)S(1)} %bitcast.63), channel_id=1, replica_groups=mesh['chan'=16,'tm'=16] {'chan'}, dimensions={0} | all-to-all | bytes 6291456 | tf_op jit(solution)/shard_map/all_to_all | solution.py:197
  164.1 1.7 %copy.37 = bf16[1,1,16,48,2048]{4,3,2,1,0:T(8,128)(2,1)} copy(bf16[1,1,16,48,2048]{4,3,2,1,0:T(8,128)(2,1)S(1)} %bitcast.65) | data formatting | bytes 6291456
  (37 shorter events, 5.1 us)
Async XLA Ops:
  0.7 14.1 %collective-permute-start = (bf16[32,192]{1,0:T(8,128)(2,1)S(1)}, bf16[32,192]{1,0:T(8,128)(2,1)S(1)}, u32[]{:S(2)}, u32[]{:S(2)}) collective-permute-start(bf16[32,192]{1,0:T(8,128)(2,1)S(1)} %slice.40), channel_id=1, source_target_pairs={{1,0},{2,1},{3,2},{4,3},{5,4},{6,5},{7,6},{8,7},{9,8},{10,9},{11,1... | collective-permute-start | bytes 36872 | tf_op jit(solution)/shard_map/ppermute | solution.py:19
  3.5 24.0 %all-to-all-start = ((s32[16,1,512]{2,1,0:T(1,128)}), s32[16,1,512]{2,1,0:T(1,128)S(1)}, u32[]{:S(2)}, u32[]{:S(2)}) async-start(s32[16,1,512]{2,1,0:T(1,128)} %reshape.212), calls=%async_computation | async-start | bytes 65536 | tf_op jit(solution)/shard_map/all_to_all | solution.py:157
  28.9 0.7 copy-start.2
  36.3 32.4 %all-to-all-start.1 = ((bf16[16,2,32,8,128]{4,3,2,1,0:T(8,128)(2,1)}), bf16[16,2,32,8,128]{4,3,2,1,0:T(8,128)(2,1)S(1)}, u32[]{:S(2)}, u32[]{:S(2)}) async-start(bf16[16,2,32,8,128]{4,3,2,1,0:T(8,128)(2,1)} %shard_map.46), calls=%async_computation.1 | async-start | bytes 4194304 | tf_op jit(solution)/shard_map/all_to_all | solution.py:172
  68.7 2.4 %copy-start.1 = (bf16[16,2,4,16,1024]{4,3,2,1,0:T(8,128)(2,1)S(1)}, bf16[16,2,4,16,1024]{4,3,2,1,0:T(8,128)(2,1)}, u32[]{:S(2)}) copy-start(bf16[16,2,4,16,1024]{4,3,2,1,0:T(8,128)(2,1)} %get-tuple-element.7) | copy-start | bytes 12582916
  71.2 2.4 %copy-start = (bf16[16,2,4,16,1024]{4,3,2,1,0:T(8,128)(2,1)S(1)}, bf16[16,2,4,16,1024]{4,3,2,1,0:T(8,128)(2,1)}, u32[]{:S(2)}) copy-start(bf16[16,2,4,16,1024]{4,3,2,1,0:T(8,128)(2,1)} %get-tuple-element.8) | copy-start | bytes 12582916

commit v10 on v5

--- a/solution.py
+++ b/solution.py
@@ -1,6 +1,7 @@
 import math
 
 import jax
+import numpy as np
 import jax.numpy as jnp
 from jax import lax
 from jax.sharding import PartitionSpec as P
@@ -20,13 +21,15 @@
 
 
 def bank_matrix(bands):
-    index = jnp.arange(bands, dtype=jnp.int32)
-    angle = (index[:, None] * index[None, :] % bands).astype(jnp.float32) * (2.0 * math.pi / bands)
-    window = 0.5 - 0.5 * jnp.cos((index.astype(jnp.float32) + 0.5) * (2.0 * math.pi / bands))
-    scaled = window / math.sqrt(3.0 * bands / 8.0)
-    return jnp.concatenate(
-        [scaled[:, None] * jnp.cos(angle), -scaled[:, None] * jnp.sin(angle)], axis=1
-    ).astype(jnp.bfloat16)
+    index = np.arange(bands, dtype=np.int32)
+    step = np.float32(2.0 * math.pi / bands)
+    angle = (index[:, None] * index[None, :] % bands).astype(np.float32) * step
+    window = np.float32(0.5) - np.float32(0.5) * np.cos((index.astype(np.float32) + np.float32(0.5)) * step)
+    scaled = window / np.float32(math.sqrt(3.0 * bands / 8.0))
+    table = np.concatenate(
+        [scaled[:, None] * np.cos(angle), -scaled[:, None] * np.sin(angle)], axis=1
+    ).astype(np.float32)
+    return jnp.asarray(table, dtype=jnp.bfloat16)
 
 
 def turn_table(moments, cycles):

time: 160 us -> 165 us (1.031)
  local copies, waits for them, and re-layouts: 8.49 us -> 14.9 us
    convert_element_type x0 -> x1, local copies, waits for them, and re-layouts: none -> 6.44 us  [on_device(): spectra = jnp.einsum('cmn,nk->ckm', framed, bank_table, preferred_element...]
  transfers between devices with their start and end apart: 3 -> 3, of which waited for: 1 -> 1; matrix products, arithmetic and copies ran while one was open for 11% -> 14% of each run, Pallas kernels for 0% -> 0%
where the time goes in v10:
time: 165 us; the launch traced here: 164 us
  blocking collectives  86.6 us (52%)
  waiting for transfers between devices  17.7 us (11%)
  starting transfers between devices  16.4 us (10%)
  local copies, waits for them, and re-layouts  14.9 us (9%)
  other arithmetic  12 us (7%)
  matrix products  9.33 us (6%)
  Pallas kernels  6.69 us (4%)
    all_to_all x1, blocking collectives, on_device(): lax.all_to_all(outgoing, 'chan', split_axis=0, concat_axis=0, tiled=True)  86.6 us
    all_to_all x1, waiting for transfers between devices, on_device(): lax.all_to_all(demod, 'tm', split_axis=0, concat_axis=0, tiled=True)  17.7 us
    all_to_all x1, starting transfers between devices, on_device(): lax.all_to_all(spread, 'tm', split_axis=0, concat_axis=0, tiled=True)  8.47 us
    pallas_call x1, Pallas kernels, demodulated(): pl.pallas_call(demod_kernel, out_shape=jax.ShapeDtypeStruct((blocks, 2, c...  6.69 us
    all_to_all x1, starting transfers between devices, on_device(): lax.all_to_all(demod, 'tm', split_axis=0, concat_axis=0, tiled=True)  6.66 us
    convert_element_type x1, local copies, waits for them, and re-layouts, on_device(): spectra = jnp.einsum('cmn,nk->ckm', framed, bank_table, preferred_element...  6.44 us
    convert_element_type x1, other arithmetic, fourier_tables(): cosine.reshape(FRAMES, KEEP).astype(jnp.bfloat16)  5.25 us
    dot_general x1, matrix products, on_device(): jnp.einsum('cmn,nk->ckm', framed, bank_table, preferred_element_type=jnp....  3.62 us
  transfers between devices with their start and end apart: 3, of which 1 were waited for; matrix products, arithmetic and copies ran while one was open for 14% of the time, Pallas kernels for 0%

profile of v10, /device:TPU:1, one launch (start us, length us, event | category | flops | bytes accessed | tf_op | source)
XLA Modules:
  0.0 163.9 jit_solution(12166268193892468782)
XLA Ops:
  0.0 0.7 slice.41
  0.7 1.3 collective-permute-start
  2.0 0.7 pad_add_fusion
  2.7 0.7 reshape.196
  3.5 8.5 %all-to-all-start = ((s32[16,1,512]{2,1,0:T(1,128)}), s32[16,1,512]{2,1,0:T(1,128)S(1)}, u32[]{:S(2)}, u32[]{:S(2)}) async-start(s32[16,1,512]{2,1,0:T(1,128)} %reshape.196), calls=%async_computation | async-start | bytes 65536 | tf_op jit(solution)/shard_map/all_to_all | solution.py:142
  12.0 0.7 fusion.44
  12.7 1.1 pad_maximum_fusion
  13.8 0.8 reshape.187
  14.6 0.9 fusion.48
  15.6 3.6 %convert_bitcast_fusion = bf16[32,512,128]{1,2,0:T(8,128)(2,1)} fusion(bf16[256,512,1]{1,0,2:T(8,128)(2,1)S(1)} %copy-done.4, bf16[32,128,64]{2,1,0:T(8,128)(2,1)S(1)} %get-tuple-element.8, bf16[32,128,64]{2,1,0:T(8,128)(2,1)S(1)} %get-tuple-element.9, bf16[32,128,64]{2,1,0:T(8,128)(2,1)S(1)} %get-tuple-element.10, bf16[32,128,64]{2,1,0:T(8,128)(2,1)S(1)} %get-tuple-element.7), kind=kOutput, calls=%fused_computation.2 | convolution fusion | flops 1084227584 | bytes 6553600 | tf_op jit(solution)/shard_map/cmn,nk->ckm/dot_general | solution.py:135
  19.2 6.4 %copy.20 = bf16[32,512,128]{2,1,0:T(8,128)(2,1)} copy(bf16[32,512,128]{1,2,0:T(8,128)(2,1)} %convert_bitcast_fusion) | data formatting | bytes 8388608 | tf_op jit(solution)/shard_map/convert_element_type | solution.py:137
  26.1 0.7 reduce.2
  27.1 0.6 add_select_fusion.2
  27.8 6.7 %shard_map.55 = bf16[16,2,32,8,128]{4,3,2,1,0:T(8,128)(2,1)} custom-call(bf16[32,2,256,128]{3,2,1,0:T(8,128)(2,1)} %bitcast.58, s32[32,128]{1,0:T(8,128)} %copy-done.2, s32[32,128]{1,0:T(8,128)} %get-tuple-element.16.second_ref, s32[32,128]{1,0:T(8,128)} %get-tuple-element.15.turn_ref, f32[4,128]{1,0:T(4,128)} %get-tuple-element.18.cos_ref, ...), custom_call_target="tpu_custom_call" | custom-call | tf_op jit(solution)/shard_map/pallas_call | solution.py:105
  34.5 6.7 %all-to-all-start.1 = ((bf16[16,2,32,8,128]{4,3,2,1,0:T(8,128)(2,1)}), bf16[16,2,32,8,128]{4,3,2,1,0:T(8,128)(2,1)S(1)}, u32[]{:S(2)}, u32[]{:S(2)}) async-start(bf16[16,2,32,8,128]{4,3,2,1,0:T(8,128)(2,1)} %shard_map.55), calls=%async_computation.1 | async-start | bytes 4194304 | tf_op jit(solution)/shard_map/all_to_all | solution.py:156
  42.9 1.1 fusion.31
  44.0 5.3 %multiply_convert_fusion.1 = (bf16[64,32,1024]{2,1,0:T(8,128)(2,1)}, bf16[64,32,1024]{2,1,0:T(8,128)(2,1)}) fusion(f32[32,1024]{1,0:T(8,128)S(1)} %get-tuple-element.21, f32[64,1024]{1,0:T(8,128)S(1)} %get-tuple-element.20, f32[32,1024]{1,0:T(8,128)S(1)} %get-tuple-element.22, f32[64,1024]{1,0:T(8,128)S(1)} %get-tuple-element.19), kind=kLoop, calls=%fused_computation.1 | loop fusion | flops 20971520 | bytes 9175040 | tf_op jit(solution)/shard_map/convert_element_type | solution.py:54
  49.2 17.7 %all-to-all-done.1 = bf16[16,2,32,8,128]{4,3,2,1,0:T(8,128)(2,1)S(1)} async-done(((bf16[16,2,32,8,128]{4,3,2,1,0:T(8,128)(2,1)}), bf16[16,2,32,8,128]{4,3,2,1,0:T(8,128)(2,1)S(1)}, u32[]{:S(2)}, u32[]{:S(2)}) %all-to-all-start.1) | async-done | bytes 2097184 | tf_op jit(solution)/shard_map/all_to_all | solution.py:156
  66.9 2.4 %copy.25 = bf16[2,32,8,16,128]{4,3,2,1,0:T(8,128)(2,1)S(1)} copy(bf16[2,32,8,16,128]{4,2,1,0,3:T(8,128)(2,1)S(1)} %bitcast.60) | data formatting | bytes 4194304 | tf_op jit(solution)/shard_map/transpose | solution.py:157
  69.3 2.4 %fusion.2 = f32[512,1024]{1,0:T(8,128)S(1)} fusion(bf16[2048,1024]{1,0:T(8,128)(2,1)S(1)} %bitcast.62, bf16[64,8,16,128]{3,2,1,0:T(8,128)(2,1)S(1)} %bitcast.63), kind=kOutput, calls=%fused_computation.6 | convolution fusion | flops 2147483648 | bytes 8388608 | tf_op jit(solution)/shard_map/dot_general | solution.py:162
  71.7 2.4 %fusion = f32[512,1024]{1,0:T(8,128)S(1)} fusion(bf16[2048,1024]{1,0:T(8,128)(2,1)S(1)} %bitcast.61, bf16[64,8,16,128]{3,2,1,0:T(8,128)(2,1)S(1)} %bitcast.64), kind=kOutput, calls=%fused_computation.4 | convolution fusion | flops 2147483648 | bytes 8388608 | tf_op jit(solution)/shard_map/dot_general | solution.py:163
  74.6 1.0 convolution_convert_fusion
  75.6 86.6 %all_to_all.15 = bf16[16,48,2048]{2,1,0:T(8,128)(2,1)S(1)} all-to-all(bf16[16,48,2048]{2,1,0:T(8,128)(2,1)S(1)} %bitcast.57), channel_id=1, replica_groups=mesh['chan'=16,'tm'=16] {'chan'}, dimensions={0} | all-to-all | bytes 6291456 | tf_op jit(solution)/shard_map/all_to_all | solution.py:181
  162.2 1.7 %copy.38 = bf16[1,1,16,48,2048]{4,3,2,1,0:T(8,128)(2,1)} copy(bf16[1,1,16,48,2048]{4,3,2,1,0:T(8,128)(2,1)S(1)} %bitcast.59) | data formatting | bytes 6291456
  (33 shorter events, 3.0 us)
Async XLA Ops:
  0.7 12.0 %collective-permute-start = (bf16[32,192]{1,0:T(8,128)(2,1)S(1)}, bf16[32,192]{1,0:T(8,128)(2,1)S(1)}, u32[]{:S(2)}, u32[]{:S(2)}) collective-permute-start(bf16[32,192]{1,0:T(8,128)(2,1)S(1)} %slice.41), channel_id=1, source_target_pairs={{1,0},{2,1},{3,2},{4,3},{5,4},{6,5},{7,6},{8,7},{9,8},{10,9},{11,1... | collective-permute-start | bytes 36872 | tf_op jit(solution)/shard_map/ppermute | solution.py:20
  3.5 22.2 %all-to-all-start = ((s32[16,1,512]{2,1,0:T(1,128)}), s32[16,1,512]{2,1,0:T(1,128)S(1)}, u32[]{:S(2)}, u32[]{:S(2)}) async-start(s32[16,1,512]{2,1,0:T(1,128)} %reshape.196), calls=%async_computation | async-start | bytes 65536 | tf_op jit(solution)/shard_map/all_to_all | solution.py:142
  14.6 1.0 copy-start.4
  27.0 0.7 copy-start.2
  27.8 13.4 %copy-start.3 = (s32[1,32,8,1]{1,3,2,0:T(1,128)S(1)}, s32[1,32,8,1]{1,3,2,0:T(1,128)}, u32[]{:S(2)}) copy-start(s32[1,32,8,1]{1,3,2,0:T(1,128)} %param.8) | copy-start | bytes 3076
  34.5 32.4 %all-to-all-start.1 = ((bf16[16,2,32,8,128]{4,3,2,1,0:T(8,128)(2,1)}), bf16[16,2,32,8,128]{4,3,2,1,0:T(8,128)(2,1)S(1)}, u32[]{:S(2)}, u32[]{:S(2)}) async-start(bf16[16,2,32,8,128]{4,3,2,1,0:T(8,128)(2,1)} %shard_map.55), calls=%async_computation.1 | async-start | bytes 4194304 | tf_op jit(solution)/shard_map/all_to_all | solution.py:156
  66.9 2.4 %copy-start.1 = (bf16[64,32,1024]{2,1,0:T(8,128)(2,1)S(1)}, bf16[64,32,1024]{2,1,0:T(8,128)(2,1)}, u32[]{:S(2)}) copy-start(bf16[64,32,1024]{2,1,0:T(8,128)(2,1)} %get-tuple-element.11) | copy-start | bytes 12582916
  69.3 2.4 %copy-start = (bf16[64,32,1024]{2,1,0:T(8,128)(2,1)S(1)}, bf16[64,32,1024]{2,1,0:T(8,128)(2,1)}, u32[]{:S(2)}) copy-start(bf16[64,32,1024]{2,1,0:T(8,128)(2,1)} %get-tuple-element.12) | copy-start | bytes 12582916

commit v11 on v5

--- a/solution.py
+++ b/solution.py
@@ -151,15 +151,16 @@
         spectra, band_first, band_first + offset, shift_bins // step, cos_table, sin_table, blocks
     )
     arrived = lax.all_to_all(demod, "tm", split_axis=0, concat_axis=0, tiled=True)
-    arrived = arrived.transpose(1, 2, 3, 0, 4)
     rows = channels * pairs
-    arrived = arrived.reshape(2 * rows, blocks * frames_dev)
-
     cosine_table, sine_table = fourier_tables()
-    with_cos = jnp.dot(arrived, cosine_table, preferred_element_type=jnp.float32)
-    with_sin = jnp.dot(arrived, sine_table, preferred_element_type=jnp.float32)
-    corr_re = with_cos[:rows] + with_sin[rows:]
-    corr_im = with_cos[rows:] - with_sin[:rows]
+    both_tables = jnp.concatenate([cosine_table, sine_table], axis=1).reshape(
+        blocks, frames_dev, 2 * KEEP
+    )
+    with_both = jnp.einsum(
+        "tpcqm,tmf->pcqf", arrived, both_tables, preferred_element_type=jnp.float32
+    ).reshape(2, rows, 2 * KEEP)
+    corr_re = with_both[0, :, :KEEP] + with_both[1, :, KEEP:]
+    corr_im = with_both[1, :, :KEEP] - with_both[0, :, KEEP:]
     correlation = jnp.concatenate([corr_re, corr_im], axis=1).astype(jnp.bfloat16)
 
     owner = pair_owner[0, :, :, 0].reshape(-1)

time: 160 us -> 159 us (level)
  matrix products: 9.7 us -> 12.2 us
  local copies, waits for them, and re-layouts: 8.49 us -> 6.05 us
    dot_general x2 -> x1, matrix products: 4.72 us -> 7.26 us  [on_device(): jnp.einsum('tpcqm,tmf->pcqf', arrived, both_tables, preferred_element_typ...]
    transpose x1 -> x0, local copies, waits for them, and re-layouts: 2.43 us -> none  [on_device(): arrived = arrived.transpose(1, 2, 3, 0, 4)]
where the time goes in v11:
time: 159 us
  blocking collectives  86.6 us (54%)
  waiting for transfers between devices  17.7 us (11%)
  starting transfers between devices  16.4 us (10%)
  other arithmetic  13.1 us (8%)
  matrix products  12.2 us (8%)
  Pallas kernels  6.69 us (4%)
  local copies, waits for them, and re-layouts  6.05 us (4%)
    all_to_all x1, blocking collectives, on_device(): lax.all_to_all(outgoing, 'chan', split_axis=0, concat_axis=0, tiled=True)  86.6 us
    all_to_all x1, waiting for transfers between devices, on_device(): lax.all_to_all(demod, 'tm', split_axis=0, concat_axis=0, tiled=True)  17.7 us
    all_to_all x1, starting transfers between devices, on_device(): lax.all_to_all(spread, 'tm', split_axis=0, concat_axis=0, tiled=True)  8.47 us
    dot_general x1, matrix products, on_device(): jnp.einsum('tpcqm,tmf->pcqf', arrived, both_tables, preferred_element_typ...  7.26 us
    pallas_call x1, Pallas kernels, demodulated(): pl.pallas_call(demod_kernel, out_shape=jax.ShapeDtypeStruct((blocks, 2, c...  6.69 us
    all_to_all x1, starting transfers between devices, on_device(): lax.all_to_all(demod, 'tm', split_axis=0, concat_axis=0, tiled=True)  6.68 us
    convert_element_type x1, other arithmetic, fourier_tables(): cosine.reshape(FRAMES, KEEP).astype(jnp.bfloat16)  5.25 us
    dot_general x1, matrix products, on_device(): jnp.einsum('cmn,nk->ckm', framed, bank_table, preferred_element_type=jnp....  3.99 us
  transfers between devices with their start and end apart: 3, of which 1 were waited for; matrix products, arithmetic and copies ran while one was open for 11% of the time, Pallas kernels for 0%

profile of v11, /device:TPU:1, one launch (start us, length us, event | category | flops | bytes accessed | tf_op | source)
XLA Modules:
  0.0 158.9 jit_solution(8547269896105043626)
XLA Ops:
  0.0 0.7 slice.41
  0.7 1.3 collective-permute-start
  2.0 0.7 pad_add_fusion
  2.7 0.7 reshape.205
  3.5 8.5 %all-to-all-start = ((s32[16,1,512]{2,1,0:T(1,128)}), s32[16,1,512]{2,1,0:T(1,128)S(1)}, u32[]{:S(2)}, u32[]{:S(2)}) async-start(s32[16,1,512]{2,1,0:T(1,128)} %reshape.205), calls=%async_computation | async-start | bytes 65536 | tf_op jit(solution)/shard_map/all_to_all | solution.py:139
  12.1 1.1 multiply_convert_fusion.2
  13.2 0.7 fusion.53
  13.9 1.1 pad_maximum_fusion
  15.0 0.8 reshape.195
  15.8 0.9 fusion.59
  16.8 4.0 %convolution_convert_fusion.1 = bf16[512,32,128]{2,0,1:T(8,128)(2,1)} fusion(bf16[32,128,64]{2,1,0:T(8,128)(2,1)S(1)} %get-tuple-element.8, bf16[32,128,64]{2,1,0:T(8,128)(2,1)S(1)} %get-tuple-element.9, bf16[32,128,64]{2,1,0:T(8,128)(2,1)S(1)} %get-tuple-element.10, bf16[32,128,64]{2,1,0:T(8,128)(2,1)S(1)} %get-tuple-element.7, ...), kind=kOutput, calls=%fused_computation.8 | convolution fusion | flops 1084751872 | bytes 6553600 | tf_op jit(solution)/shard_map/cmn,nk->ckm/dot_general | solution.py:132
  21.3 0.7 reduce.2
  22.2 0.7 add_select_fusion.3
  22.9 6.7 %shard_map.46 = bf16[16,2,32,8,128]{4,3,2,1,0:T(8,128)(2,1)} custom-call(bf16[32,2,256,128]{3,2,1,0:T(8,128)(2,1)} %bitcast.68, s32[32,128]{1,0:T(8,128)} %copy-done, s32[32,128]{1,0:T(8,128)} %get-tuple-element.16.second_ref, s32[32,128]{1,0:T(8,128)} %get-tuple-element.15.turn_ref, f32[4,128]{1,0:T(4,128)} %get-tuple-element.18.cos_ref, ...), custom_call_target="tpu_custom_call" | custom-call | tf_op jit(solution)/shard_map/pallas_call | solution.py:102
  29.6 6.7 %all-to-all-start.1 = ((bf16[16,2,32,8,128]{4,3,2,1,0:T(8,128)(2,1)}), bf16[16,2,32,8,128]{4,3,2,1,0:T(8,128)(2,1)S(1)}, u32[]{:S(2)}, u32[]{:S(2)}) async-start(bf16[16,2,32,8,128]{4,3,2,1,0:T(8,128)(2,1)} %shard_map.46), calls=%async_computation.1 | async-start | bytes 4194304 | tf_op jit(solution)/shard_map/all_to_all | solution.py:153
  36.6 0.6 reduce-window.6
  37.5 0.5 fusion.42
  38.0 1.1 fusion.40
  39.1 5.3 %multiply_convert_fusion.1 = (bf16[64,32,1024]{2,1,0:T(8,128)(2,1)}, bf16[64,32,1024]{2,1,0:T(8,128)(2,1)}) fusion(f32[32,1024]{1,0:T(8,128)S(1)} %get-tuple-element.21, f32[64,1024]{1,0:T(8,128)S(1)} %get-tuple-element.20, f32[32,1024]{1,0:T(8,128)S(1)} %get-tuple-element.22, f32[64,1024]{1,0:T(8,128)S(1)} %get-tuple-element.19), kind=kLoop, calls=%fused_computation.5 | loop fusion | flops 20971520 | bytes 9175040 | tf_op jit(solution)/shard_map/convert_element_type | solution.py:51
  44.4 17.7 %all-to-all-done.1 = bf16[16,2,32,8,128]{4,3,2,1,0:T(8,128)(2,1)S(1)} async-done(((bf16[16,2,32,8,128]{4,3,2,1,0:T(8,128)(2,1)}), bf16[16,2,32,8,128]{4,3,2,1,0:T(8,128)(2,1)S(1)}, u32[]{:S(2)}, u32[]{:S(2)}) %all-to-all-start.1) | async-done | bytes 2097184 | tf_op jit(solution)/shard_map/all_to_all | solution.py:153
  62.0 7.3 %fusion.3 = f32[2,256,2048]{2,1,0:T(8,128)S(1)} fusion(bf16[16,128,1024]{2,1,0:T(8,128)(2,1)} %bitcast.70, bf16[16,128,1024]{2,1,0:T(8,128)(2,1)} %bitcast.69, bf16[16,2,32,8,128]{4,3,2,1,0:T(8,128)(2,1)S(1)} %all-to-all-done.1), kind=kOutput, calls=%fused_computation.7 | convolution fusion | flops 4311744512 | bytes 14680064 | tf_op jit(solution)/shard_map/tpcqm,tmf->pcqf/dot_general | solution.py:159
  69.6 1.0 convolution_convert_fusion
  70.6 86.6 %all_to_all.15 = bf16[16,48,2048]{2,1,0:T(8,128)(2,1)S(1)} all-to-all(bf16[16,48,2048]{2,1,0:T(8,128)(2,1)S(1)} %bitcast.66), channel_id=1, replica_groups=mesh['chan'=16,'tm'=16] {'chan'}, dimensions={0} | all-to-all | bytes 6291456 | tf_op jit(solution)/shard_map/all_to_all | solution.py:179
  157.2 1.7 %copy.26 = bf16[1,1,16,48,2048]{4,3,2,1,0:T(8,128)(2,1)} copy(bf16[1,1,16,48,2048]{4,3,2,1,0:T(8,128)(2,1)S(1)} %bitcast.67) | data formatting | bytes 6291456
  (27 shorter events, 1.8 us)
Async XLA Ops:
  0.7 13.2 %collective-permute-start = (bf16[32,192]{1,0:T(8,128)(2,1)S(1)}, bf16[32,192]{1,0:T(8,128)(2,1)S(1)}, u32[]{:S(2)}, u32[]{:S(2)}) collective-permute-start(bf16[32,192]{1,0:T(8,128)(2,1)S(1)} %slice.41), channel_id=1, source_target_pairs={{1,0},{2,1},{3,2},{4,3},{5,4},{6,5},{7,6},{8,7},{9,8},{10,9},{11,1... | collective-permute-start | bytes 36872 | tf_op jit(solution)/shard_map/ppermute | solution.py:19
  3.5 17.3 %all-to-all-start = ((s32[16,1,512]{2,1,0:T(1,128)}), s32[16,1,512]{2,1,0:T(1,128)S(1)}, u32[]{:S(2)}, u32[]{:S(2)}) async-start(s32[16,1,512]{2,1,0:T(1,128)} %reshape.205), calls=%async_computation | async-start | bytes 65536 | tf_op jit(solution)/shard_map/all_to_all | solution.py:139
  22.2 0.7 copy-start
  22.9 13.4 %copy-start.1 = (s32[1,32,8,1]{1,3,2,0:T(1,128)S(1)}, s32[1,32,8,1]{1,3,2,0:T(1,128)}, u32[]{:S(2)}) copy-start(s32[1,32,8,1]{1,3,2,0:T(1,128)} %param.7) | copy-start | bytes 3076
  29.6 32.4 %all-to-all-start.1 = ((bf16[16,2,32,8,128]{4,3,2,1,0:T(8,128)(2,1)}), bf16[16,2,32,8,128]{4,3,2,1,0:T(8,128)(2,1)S(1)}, u32[]{:S(2)}, u32[]{:S(2)}) async-start(bf16[16,2,32,8,128]{4,3,2,1,0:T(8,128)(2,1)} %shard_map.46), calls=%async_computation.1 | async-start | bytes 4194304 | tf_op jit(solution)/shard_map/all_to_all | solution.py:153

commit v12 on v8

--- a/solution.py
+++ b/solution.py
@@ -160,9 +160,11 @@
         ],
         axis=0,
     ).reshape(2, blocks, frames_dev, 2 * KEEP)
+    dft_table = lax.optimization_barrier(dft_table)
     correlation = jnp.einsum(
         "tpcqm,ptmf->cqf", arrived, dft_table, preferred_element_type=jnp.float32
     ).astype(jnp.bfloat16).reshape(rows, 2 * KEEP)
+
 
     owner = pair_owner[0, :, :, 0].reshape(-1)
     groups = lax.axis_size("chan")

time: 165 us -> 171 us (1.036)
  other arithmetic: 15.2 us -> 30.5 us
  waiting for transfers between devices: 15.2 us -> 11.3 us
  matrix products: 16.6 us -> 13.1 us
    another operation x3 -> x4, other arithmetic: 1.76 us -> 15.3 us  [the longest x1 13.5 us: on_device(): jnp.stack([jnp.concatenate([cosine_table, -sine_table], axis=1), jnp.conc...]
    dot_general x1, matrix products: 12.6 us -> 0.99 us  [on_device(): jnp.dot(placing, correlation, preferred_element_type=jnp.float32)]
    dot_general x0 -> x1, matrix products: none -> 8.12 us  [on_device(): jnp.einsum('tpcqm,ptmf->cqf', arrived, dft_table, preferred_element_type=...]
    all_to_all x1, waiting for transfers between devices: 15.2 us -> 11.3 us  [on_device(): lax.all_to_all(demod, 'tm', split_axis=0, concat_axis=0, tiled=True)]
    neg x1, other arithmetic: 3.27 us -> 5.42 us  [on_device(): -sine_table]
    unnamed x15 -> x11, local copies, waits for them, and re-layouts: 3.91 us -> 2.59 us
  transfers between devices with their start and end apart: 3 -> 3, of which waited for: 1 -> 1; matrix products, arithmetic and copies ran while one was open for 13% -> 21% of each run, Pallas kernels for 0% -> 0%
where the time goes in v12:
time: 171 us
  blocking collectives  86.6 us (51%)
  other arithmetic  30.5 us (18%)
  starting transfers between devices  16.4 us (10%)
  matrix products  13.1 us (8%)
  waiting for transfers between devices  11.3 us (7%)
  Pallas kernels  6.69 us (4%)
  local copies, waits for them, and re-layouts  6.06 us (4%)
    all_to_all x1, blocking collectives, on_device(): lax.all_to_all(outgoing, 'chan', split_axis=0, concat_axis=0, tiled=True)  86.6 us
    another operation x1, other arithmetic, on_device(): jnp.stack([jnp.concatenate([cosine_table, -sine_table], axis=1), jnp.conc...  13.5 us
    all_to_all x1, waiting for transfers between devices, on_device(): lax.all_to_all(demod, 'tm', split_axis=0, concat_axis=0, tiled=True)  11.3 us
    all_to_all x1, starting transfers between devices, on_device(): lax.all_to_all(spread, 'tm', split_axis=0, concat_axis=0, tiled=True)  8.47 us
    dot_general x1, matrix products, on_device(): jnp.einsum('tpcqm,ptmf->cqf', arrived, dft_table, preferred_element_type=...  8.12 us
    pallas_call x1, Pallas kernels, demodulated(): pl.pallas_call(demod_kernel, out_shape=jax.ShapeDtypeStruct((blocks, 2, c...  6.69 us
    all_to_all x1, starting transfers between devices, on_device(): lax.all_to_all(demod, 'tm', split_axis=0, concat_axis=0, tiled=True)  6.68 us
    neg x1, other arithmetic, on_device(): -sine_table  5.42 us
  transfers between devices with their start and end apart: 3, of which 1 were waited for; matrix products, arithmetic and copies ran while one was open for 21% of the time, Pallas kernels for 0%

profile of v12, /device:TPU:1, one launch (start us, length us, event | category | flops | bytes accessed | tf_op | source)
XLA Modules:
  0.0 170.8 jit_solution(6870330726459928990)
XLA Ops:
  0.0 0.7 slice.29
  0.7 1.3 collective-permute-start
  2.0 0.7 pad_add_fusion
  2.7 0.7 reshape.279
  3.5 8.5 %all-to-all-start = ((s32[16,1,512]{2,1,0:T(1,128)}), s32[16,1,512]{2,1,0:T(1,128)S(1)}, u32[]{:S(2)}, u32[]{:S(2)}) async-start(s32[16,1,512]{2,1,0:T(1,128)} %reshape.279), calls=%async_computation | async-start | bytes 65536 | tf_op jit(solution)/shard_map/all_to_all | solution.py:139
  12.6 1.1 fusion.40
  13.7 1.1 multiply_convert_fusion.2
  14.9 5.1 %multiply_convert_fusion = (bf16[64,32,1024]{2,1,0:T(8,128)(2,1)}, bf16[64,32,1024]{2,1,0:T(8,128)(2,1)}) fusion(f32[32,1024]{1,0:T(8,128)S(1)} %get-tuple-element.19, f32[64,1024]{1,0:T(8,128)S(1)} %get-tuple-element.18, f32[32,1024]{1,0:T(8,128)S(1)} %get-tuple-element.20, f32[64,1024]{1,0:T(8,128)S(1)} %get-tuple-element.17), kind=kLoop, calls=%fused_computation.3 | loop fusion | flops 20971520 | bytes 9175040 | tf_op jit(solution)/shard_map/convert_element_type | solution.py:52
  19.9 0.7 fusion.53
  20.9 5.4 %neg.17 = bf16[1,16,128,1024]{3,2,1,0:T(8,128)(2,1)} negate(bf16[1,16,128,1024]{3,2,1,0:T(8,128)(2,1)} %bitcast.70) | non-fusion elementwise | flops 2097152 | bytes 8388608 | tf_op jit(solution)/shard_map/neg | solution.py:158
  26.4 0.8 reshape.268
  27.2 0.9 fusion.57
  28.1 4.0 %convolution_convert_fusion.1 = bf16[512,32,128]{2,0,1:T(8,128)(2,1)} fusion(bf16[32,128,64]{2,1,0:T(8,128)(2,1)S(1)} %get-tuple-element.6, bf16[32,128,64]{2,1,0:T(8,128)(2,1)S(1)} %get-tuple-element.7, bf16[32,128,64]{2,1,0:T(8,128)(2,1)S(1)} %get-tuple-element.8, bf16[32,128,64]{2,1,0:T(8,128)(2,1)S(1)} %get-tuple-element.5, ...), kind=kOutput, calls=%fused_computation.7 | convolution fusion | flops 1084751872 | bytes 6553600 | tf_op jit(solution)/shard_map/cmn,nk->ckm/dot_general | solution.py:132
  32.6 0.7 reduce.2
  33.6 0.7 add_select_fusion.3
  34.3 6.7 %shard_map.46 = bf16[16,2,32,8,128]{4,3,2,1,0:T(8,128)(2,1)} custom-call(bf16[32,2,256,128]{3,2,1,0:T(8,128)(2,1)} %bitcast.75, s32[32,128]{1,0:T(8,128)} %copy-done.1, s32[32,128]{1,0:T(8,128)} %get-tuple-element.14.second_ref, s32[32,128]{1,0:T(8,128)} %get-tuple-element.13.turn_ref, f32[4,128]{1,0:T(4,128)} %get-tuple-element.16.cos_ref, ...), custom_call_target="tpu_custom_call" | custom-call | tf_op jit(solution)/shard_map/pallas_call | solution.py:102
  41.0 6.7 %all-to-all-start.1 = ((bf16[16,2,32,8,128]{4,3,2,1,0:T(8,128)(2,1)}), bf16[16,2,32,8,128]{4,3,2,1,0:T(8,128)(2,1)S(1)}, u32[]{:S(2)}, u32[]{:S(2)}) async-start(bf16[16,2,32,8,128]{4,3,2,1,0:T(8,128)(2,1)} %shard_map.46), calls=%async_computation.1 | async-start | bytes 4194304 | tf_op jit(solution)/shard_map/all_to_all | solution.py:153
  47.6 13.5 %maximum_maximum_fusion = bf16[2,16,128,2048]{3,2,1,0:T(8,128)(2,1)} fusion(bf16[1,16,128,1024]{3,2,1,0:T(8,128)(2,1)} %bitcast.73, bf16[1,16,128,1024]{3,2,1,0:T(8,128)(2,1)} %bitcast.71, bf16[1,16,128,1024]{3,2,1,0:T(8,128)(2,1)} %neg.17), kind=kLoop, calls=%fused_computation | loop fusion | flops 67108864 | bytes 29360128 | tf_op jit(solution)/shard_map/stack | solution.py:156
  61.2 0.6 reduce-window.6
  62.1 11.3 %all-to-all-done.1 = bf16[16,2,32,8,128]{4,3,2,1,0:T(8,128)(2,1)S(1)} async-done(((bf16[16,2,32,8,128]{4,3,2,1,0:T(8,128)(2,1)}), bf16[16,2,32,8,128]{4,3,2,1,0:T(8,128)(2,1)S(1)}, u32[]{:S(2)}, u32[]{:S(2)}) %all-to-all-start.1) | async-done | bytes 2097184 | tf_op jit(solution)/shard_map/all_to_all | solution.py:153
  73.4 8.1 %fusion.8 = bf16[256,2048]{1,0:T(8,128)(2,1)S(1)} fusion(bf16[2,16,128,2048]{3,2,1,0:T(8,128)(2,1)} %maximum_maximum_fusion, bf16[16,2,32,8,128]{4,3,2,1,0:T(8,128)(2,1)S(1)} %all-to-all-done.1), kind=kOutput, calls=%fused_computation.9 | convolution fusion | flops 4295491584 | bytes 19922944 | tf_op jit(solution)/shard_map/tpcqm,ptmf->cqf/dot_general | solution.py:164
  81.5 1.0 convolution_convert_fusion
  82.5 86.6 %all_to_all.15 = bf16[16,48,2048]{2,1,0:T(8,128)(2,1)S(1)} all-to-all(bf16[16,48,2048]{2,1,0:T(8,128)(2,1)S(1)} %bitcast.72), channel_id=1, replica_groups=mesh['chan'=16,'tm'=16] {'chan'}, dimensions={0} | all-to-all | bytes 6291456 | tf_op jit(solution)/shard_map/all_to_all | solution.py:182
  169.1 1.7 copy.30
  (30 shorter events, 2.0 us)
Async XLA Ops:
  0.7 25.6 %collective-permute-start = (bf16[32,192]{1,0:T(8,128)(2,1)S(1)}, bf16[32,192]{1,0:T(8,128)(2,1)S(1)}, u32[]{:S(2)}, u32[]{:S(2)}) collective-permute-start(bf16[32,192]{1,0:T(8,128)(2,1)S(1)} %slice.29), channel_id=1, source_target_pairs={{1,0},{2,1},{3,2},{4,3},{5,4},{6,5},{7,6},{8,7},{9,8},{10,9},{11,1... | collective-permute-start | bytes 36872 | tf_op jit(solution)/shard_map/ppermute | solution.py:19
  3.5 28.7 %all-to-all-start = ((s32[16,1,512]{2,1,0:T(1,128)}), s32[16,1,512]{2,1,0:T(1,128)S(1)}, u32[]{:S(2)}, u32[]{:S(2)}) async-start(s32[16,1,512]{2,1,0:T(1,128)} %reshape.279), calls=%async_computation | async-start | bytes 65536 | tf_op jit(solution)/shard_map/all_to_all | solution.py:139
  14.9 5.8 %copy-start.2 = (s32[1,32,8,1]{1,3,2,0:T(1,128)S(1)}, s32[1,32,8,1]{1,3,2,0:T(1,128)}, u32[]{:S(2)}) copy-start(s32[1,32,8,1]{1,3,2,0:T(1,128)} %param.7) | copy-start | bytes 3076
  20.9 5.4 %copy-start = (bf16[32,8192]{1,0:T(8,128)(2,1)S(1)}, bf16[32,8192]{1,0:T(8,128)(2,1)}, u32[]{:S(2)}) copy-start(bf16[32,8192]{1,0:T(8,128)(2,1)} %param.4) | copy-start | bytes 1572868
  33.5 0.7 copy-start.1
  41.0 32.4 %all-to-all-start.1 = ((bf16[16,2,32,8,128]{4,3,2,1,0:T(8,128)(2,1)}), bf16[16,2,32,8,128]{4,3,2,1,0:T(8,128)(2,1)S(1)}, u32[]{:S(2)}, u32[]{:S(2)}) async-start(bf16[16,2,32,8,128]{4,3,2,1,0:T(8,128)(2,1)} %shard_map.46), calls=%async_computation.1 | async-start | bytes 4194304 | tf_op jit(solution)/shard_map/all_to_all | solution.py:153

commit v13 on v11

--- a/solution.py
+++ b/solution.py
@@ -134,21 +134,21 @@
     ).astype(jnp.bfloat16)
     spectra = spectra.reshape(channels, 2, BANDS, frames_dev)
 
-    local_tables = jnp.stack([pair_band[0], pair_offset[0]], axis=0)
-    spread = jnp.broadcast_to(local_tables[None], (blocks,) + local_tables.shape)
-    tables = lax.all_to_all(spread, "tm", split_axis=0, concat_axis=0, tiled=True)
-    bands_all = tables[:, 0].transpose(1, 0, 2)
-    offsets_all = tables[:, 1].transpose(1, 0, 2)
-    pairs = bands_all.shape[2]
-    band_first = bands_all.reshape(channels, blocks * pairs)
-    offset = offsets_all.reshape(channels, blocks * pairs)
-    moment = lax.axis_index("tm") * frames_dev + jnp.arange(frames_dev, dtype=jnp.int32)
     step = math.gcd(HOP * FRAMES // BANDS, KEEP // 2, FRAMES)
     levels = FRAMES // step
+    band = pair_band[0]
+    shift_bins = (pair_offset[0] * (HOP * FRAMES // BANDS) - KEEP // 2) % FRAMES
+    local_tables = jnp.stack([band, band + pair_offset[0], shift_bins // step], axis=0)
+    pairs = band.shape[1]
+    spread = jnp.broadcast_to(
+        local_tables[:, :, None, :], (3, channels, blocks, pairs)
+    )
+    tables = lax.all_to_all(spread, "tm", split_axis=2, concat_axis=2, tiled=True)
+    tables = tables.reshape(3, channels, blocks * pairs)
+    moment = lax.axis_index("tm") * frames_dev + jnp.arange(frames_dev, dtype=jnp.int32)
     cos_table, sin_table = turn_table(jnp.arange(levels, dtype=jnp.int32) * step, moment)
-    shift_bins = (offset * (HOP * FRAMES // BANDS) - KEEP // 2) % FRAMES
     demod = demodulated(
-        spectra, band_first, band_first + offset, shift_bins // step, cos_table, sin_table, blocks
+        spectra, tables[0], tables[1], tables[2], cos_table, sin_table, blocks
     )
     arrived = lax.all_to_all(demod, "tm", split_axis=0, concat_axis=0, tiled=True)
     rows = channels * pairs

time: 159 us -> 161 us (1.013)
  local copies, waits for them, and re-layouts: 6.05 us -> 8 us
    squeeze x0 -> x4, local copies, waits for them, and re-layouts: none -> 2.05 us  [the longest x2 0.69 us: on_device(): tables[2]]
  transfers between devices with their start and end apart: 3 -> 3, of which waited for: 1 -> 1; matrix products, arithmetic and copies ran while one was open for 11% -> 12% of each run, Pallas kernels for 0% -> 0%
where the time goes in v13:
time: 161 us
  blocking collectives  86.6 us (54%)
  waiting for transfers between devices  17.7 us (11%)
  starting transfers between devices  16.4 us (10%)
  other arithmetic  13.1 us (8%)
  matrix products  12.2 us (8%)
  local copies, waits for them, and re-layouts  8 us (5%)
  Pallas kernels  6.69 us (4%)
    all_to_all x1, blocking collectives, on_device(): lax.all_to_all(outgoing, 'chan', split_axis=0, concat_axis=0, tiled=True)  86.6 us
    all_to_all x1, waiting for transfers between devices, on_device(): lax.all_to_all(demod, 'tm', split_axis=0, concat_axis=0, tiled=True)  17.7 us
    all_to_all x1, starting transfers between devices, on_device(): lax.all_to_all(spread, 'tm', split_axis=2, concat_axis=2, tiled=True)  8.47 us
    dot_general x1, matrix products, on_device(): jnp.einsum('tpcqm,tmf->pcqf', arrived, both_tables, preferred_element_typ...  7.26 us
    pallas_call x1, Pallas kernels, demodulated(): pl.pallas_call(demod_kernel, out_shape=jax.ShapeDtypeStruct((blocks, 2, c...  6.69 us
    all_to_all x1, starting transfers between devices, on_device(): lax.all_to_all(demod, 'tm', split_axis=0, concat_axis=0, tiled=True)  6.68 us
    convert_element_type x1, other arithmetic, fourier_tables(): cosine.reshape(FRAMES, KEEP).astype(jnp.bfloat16)  5.24 us
    dot_general x1, matrix products, on_device(): jnp.einsum('cmn,nk->ckm', framed, bank_table, preferred_element_type=jnp....  3.98 us
  transfers between devices with their start and end apart: 3, of which 1 were waited for; matrix products, arithmetic and copies ran while one was open for 12% of the time, Pallas kernels for 0%

profile of v13, /device:TPU:1, one launch (start us, length us, event | category | flops | bytes accessed | tf_op | source)
XLA Modules:
  0.0 160.9 jit_solution(13998132980600792888)
XLA Ops:
  0.0 0.7 slice.47
  0.7 1.3 collective-permute-start
  2.0 0.7 fusion.60
  2.7 0.7 pad_add_fusion
  3.4 0.8 reshape.204
  4.2 8.5 %all-to-all-start = ((s32[16,1,768]{2,1,0:T(1,128)}), s32[16,1,768]{2,1,0:T(1,128)S(1)}, u32[]{:S(2)}, u32[]{:S(2)}) async-start(s32[16,1,768]{2,1,0:T(1,128)} %reshape.204), calls=%async_computation | async-start | bytes 98304 | tf_op jit(solution)/shard_map/all_to_all | solution.py:146
  12.8 1.1 multiply_convert_fusion.2
  14.0 0.7 fusion.53
  14.7 1.1 pad_maximum_fusion
  15.8 0.8 reshape.196
  16.6 0.9 fusion.59
  17.5 4.0 %convolution_convert_fusion.1 = bf16[512,32,128]{2,0,1:T(8,128)(2,1)} fusion(bf16[32,128,64]{2,1,0:T(8,128)(2,1)S(1)} %get-tuple-element.8, bf16[32,128,64]{2,1,0:T(8,128)(2,1)S(1)} %get-tuple-element.9, bf16[32,128,64]{2,1,0:T(8,128)(2,1)S(1)} %get-tuple-element.10, bf16[32,128,64]{2,1,0:T(8,128)(2,1)S(1)} %get-tuple-element.7, ...), kind=kOutput, calls=%fused_computation.8 | convolution fusion | flops 1084751872 | bytes 6553600 | tf_op jit(solution)/shard_map/cmn,nk->ckm/dot_general | solution.py:132
  22.0 0.8 reduce.2
  22.9 0.7 copy.17.first_ref
  23.6 0.7 copy.18.second_ref
  24.9 6.7 %shard_map.46 = bf16[16,2,32,8,128]{4,3,2,1,0:T(8,128)(2,1)} custom-call(bf16[32,2,256,128]{3,2,1,0:T(8,128)(2,1)} %bitcast.62, s32[32,128]{1,0:T(8,128)} %copy.17.first_ref, s32[32,128]{1,0:T(8,128)} %copy.18.second_ref, s32[32,128]{1,0:T(8,128)} %copy.19.turn_ref, f32[4,128]{1,0:T(4,128)} %get-tuple-element.19.cos_ref, f32[4,128]{1,0:T(4,128)} %get-tuple-element.18.sin_ref), custom_call_target="tpu_custom_call" | custom-call | tf_op jit(solution)/shard_map/pallas_call | solution.py:102
  31.6 6.7 %all-to-all-start.1 = ((bf16[16,2,32,8,128]{4,3,2,1,0:T(8,128)(2,1)}), bf16[16,2,32,8,128]{4,3,2,1,0:T(8,128)(2,1)S(1)}, u32[]{:S(2)}, u32[]{:S(2)}) async-start(bf16[16,2,32,8,128]{4,3,2,1,0:T(8,128)(2,1)} %shard_map.46), calls=%async_computation.1 | async-start | bytes 4194304 | tf_op jit(solution)/shard_map/all_to_all | solution.py:153
  40.1 1.1 fusion.40
  41.2 5.2 %multiply_convert_fusion.1 = (bf16[64,32,1024]{2,1,0:T(8,128)(2,1)}, bf16[64,32,1024]{2,1,0:T(8,128)(2,1)}) fusion(f32[32,1024]{1,0:T(8,128)S(1)} %get-tuple-element.22, f32[64,1024]{1,0:T(8,128)S(1)} %get-tuple-element.21, f32[32,1024]{1,0:T(8,128)S(1)} %get-tuple-element.23, f32[64,1024]{1,0:T(8,128)S(1)} %get-tuple-element.20), kind=kLoop, calls=%fused_computation.5 | loop fusion | flops 20971520 | bytes 9175040 | tf_op jit(solution)/shard_map/convert_element_type | solution.py:51
  46.4 17.7 %all-to-all-done.1 = bf16[16,2,32,8,128]{4,3,2,1,0:T(8,128)(2,1)S(1)} async-done(((bf16[16,2,32,8,128]{4,3,2,1,0:T(8,128)(2,1)}), bf16[16,2,32,8,128]{4,3,2,1,0:T(8,128)(2,1)S(1)}, u32[]{:S(2)}, u32[]{:S(2)}) %all-to-all-start.1) | async-done | bytes 2097184 | tf_op jit(solution)/shard_map/all_to_all | solution.py:153
  64.1 7.3 %fusion.3 = f32[2,256,2048]{2,1,0:T(8,128)S(1)} fusion(bf16[16,128,1024]{2,1,0:T(8,128)(2,1)} %bitcast.64, bf16[16,128,1024]{2,1,0:T(8,128)(2,1)} %bitcast.63, bf16[16,2,32,8,128]{4,3,2,1,0:T(8,128)(2,1)S(1)} %all-to-all-done.1), kind=kOutput, calls=%fused_computation.7 | convolution fusion | flops 4311744512 | bytes 14680064 | tf_op jit(solution)/shard_map/tpcqm,tmf->pcqf/dot_general | solution.py:159
  71.7 1.0 convolution_convert_fusion
  72.7 86.6 %all_to_all.15 = bf16[16,48,2048]{2,1,0:T(8,128)(2,1)S(1)} all-to-all(bf16[16,48,2048]{2,1,0:T(8,128)(2,1)S(1)} %bitcast.60), channel_id=1, replica_groups=mesh['chan'=16,'tm'=16] {'chan'}, dimensions={0} | all-to-all | bytes 6291456 | tf_op jit(solution)/shard_map/all_to_all | solution.py:179
  159.3 1.7 %copy.24 = bf16[1,1,16,48,2048]{4,3,2,1,0:T(8,128)(2,1)} copy(bf16[1,1,16,48,2048]{4,3,2,1,0:T(8,128)(2,1)S(1)} %bitcast.61) | data formatting | bytes 6291456
  (26 shorter events, 3.5 us)
Async XLA Ops:
  0.7 14.0 %collective-permute-start = (bf16[32,192]{1,0:T(8,128)(2,1)S(1)}, bf16[32,192]{1,0:T(8,128)(2,1)S(1)}, u32[]{:S(2)}, u32[]{:S(2)}) collective-permute-start(bf16[32,192]{1,0:T(8,128)(2,1)S(1)} %slice.47), channel_id=1, source_target_pairs={{1,0},{2,1},{3,2},{4,3},{5,4},{6,5},{7,6},{8,7},{9,8},{10,9},{11,1... | collective-permute-start | bytes 36872 | tf_op jit(solution)/shard_map/ppermute | solution.py:19
  4.2 17.3 %all-to-all-start = ((s32[16,1,768]{2,1,0:T(1,128)}), s32[16,1,768]{2,1,0:T(1,128)S(1)}, u32[]{:S(2)}, u32[]{:S(2)}) async-start(s32[16,1,768]{2,1,0:T(1,128)} %reshape.204), calls=%async_computation | async-start | bytes 98304 | tf_op jit(solution)/shard_map/all_to_all | solution.py:146
  24.9 13.4 %copy-start = (s32[1,32,8,1]{1,3,2,0:T(1,128)S(1)}, s32[1,32,8,1]{1,3,2,0:T(1,128)}, u32[]{:S(2)}) copy-start(s32[1,32,8,1]{1,3,2,0:T(1,128)} %param.7) | copy-start | bytes 3076
  31.6 32.4 %all-to-all-start.1 = ((bf16[16,2,32,8,128]{4,3,2,1,0:T(8,128)(2,1)}), bf16[16,2,32,8,128]{4,3,2,1,0:T(8,128)(2,1)S(1)}, u32[]{:S(2)}, u32[]{:S(2)}) async-start(bf16[16,2,32,8,128]{4,3,2,1,0:T(8,128)(2,1)} %shard_map.46), calls=%async_computation.1 | async-start | bytes 4194304 | tf_op jit(solution)/shard_map/all_to_all | solution.py:153

commit v14 on v11

--- a/solution.py
+++ b/solution.py
@@ -87,11 +87,12 @@
             chosen = turn == level
             cosine = jnp.where(chosen, cos_ref[level : level + 1, :], cosine)
             sine = jnp.where(chosen, sin_ref[level : level + 1, :], sine)
-        demod_re = (real_part * cosine + imag_part * sine).astype(out_ref.dtype)
-        demod_im = (imag_part * cosine - real_part * sine).astype(out_ref.dtype)
+        demod_re = real_part * cosine + imag_part * sine
+        demod_im = imag_part * cosine - real_part * sine
         for block in range(blocks):
-            out_ref[block, 0, index] = demod_re[block * pairs : (block + 1) * pairs]
-            out_ref[block, 1, index] = demod_im[block * pairs : (block + 1) * pairs]
+            rows_of = slice(block * pairs, (block + 1) * pairs)
+            out_ref[block, 0, index] = demod_re[rows_of].astype(out_ref.dtype)
+            out_ref[block, 1, index] = demod_im[rows_of].astype(out_ref.dtype)
 
 
 def demodulated(spectra, first, second, turn, cos_table, sin_table, blocks, per_block=8, interpret=False):

time: 159 us -> 159 us (level)
  no operation moved by 1% of the time
where the time goes in v14:
time: 159 us
  blocking collectives  86.6 us (54%)
  waiting for transfers between devices  17.7 us (11%)
  starting transfers between devices  16.4 us (10%)
  other arithmetic  13.1 us (8%)
  matrix products  12.2 us (8%)
  Pallas kernels  6.69 us (4%)
  local copies, waits for them, and re-layouts  6.05 us (4%)
    all_to_all x1, blocking collectives, on_device(): lax.all_to_all(outgoing, 'chan', split_axis=0, concat_axis=0, tiled=True)  86.6 us
    all_to_all x1, waiting for transfers between devices, on_device(): lax.all_to_all(demod, 'tm', split_axis=0, concat_axis=0, tiled=True)  17.7 us
    all_to_all x1, starting transfers between devices, on_device(): lax.all_to_all(spread, 'tm', split_axis=0, concat_axis=0, tiled=True)  8.47 us
    dot_general x1, matrix products, on_device(): jnp.einsum('tpcqm,tmf->pcqf', arrived, both_tables, preferred_element_typ...  7.26 us
    pallas_call x1, Pallas kernels, demodulated(): pl.pallas_call(demod_kernel, out_shape=jax.ShapeDtypeStruct((blocks, 2, c...  6.69 us
    all_to_all x1, starting transfers between devices, on_device(): lax.all_to_all(demod, 'tm', split_axis=0, concat_axis=0, tiled=True)  6.68 us
    convert_element_type x1, other arithmetic, fourier_tables(): cosine.reshape(FRAMES, KEEP).astype(jnp.bfloat16)  5.25 us
    dot_general x1, matrix products, on_device(): jnp.einsum('cmn,nk->ckm', framed, bank_table, preferred_element_type=jnp....  3.99 us
  transfers between devices with their start and end apart: 3, of which 1 were waited for; matrix products, arithmetic and copies ran while one was open for 11% of the time, Pallas kernels for 0%

profile of v14, /device:TPU:1, one launch (start us, length us, event | category | flops | bytes accessed | tf_op | source)
XLA Modules:
  0.0 158.9 jit_solution(18335873313835424074)
XLA Ops:
  0.0 0.7 slice.41
  0.7 1.3 collective-permute-start
  2.0 0.7 pad_add_fusion
  2.7 0.7 reshape.205
  3.5 8.5 %all-to-all-start = ((s32[16,1,512]{2,1,0:T(1,128)}), s32[16,1,512]{2,1,0:T(1,128)S(1)}, u32[]{:S(2)}, u32[]{:S(2)}) async-start(s32[16,1,512]{2,1,0:T(1,128)} %reshape.205), calls=%async_computation | async-start | bytes 65536 | tf_op jit(solution)/shard_map/all_to_all | solution.py:140
  12.1 1.1 multiply_convert_fusion.2
  13.2 0.7 fusion.53
  13.9 1.1 pad_maximum_fusion
  15.0 0.8 reshape.195
  15.8 0.9 fusion.59
  16.8 4.0 %convolution_convert_fusion.1 = bf16[512,32,128]{2,0,1:T(8,128)(2,1)} fusion(bf16[32,128,64]{2,1,0:T(8,128)(2,1)S(1)} %get-tuple-element.8, bf16[32,128,64]{2,1,0:T(8,128)(2,1)S(1)} %get-tuple-element.9, bf16[32,128,64]{2,1,0:T(8,128)(2,1)S(1)} %get-tuple-element.10, bf16[32,128,64]{2,1,0:T(8,128)(2,1)S(1)} %get-tuple-element.7, ...), kind=kOutput, calls=%fused_computation.8 | convolution fusion | flops 1084751872 | bytes 6553600 | tf_op jit(solution)/shard_map/cmn,nk->ckm/dot_general | solution.py:133
  21.3 0.7 reduce.2
  22.2 0.7 add_select_fusion.3
  22.9 6.7 %shard_map.46 = bf16[16,2,32,8,128]{4,3,2,1,0:T(8,128)(2,1)} custom-call(bf16[32,2,256,128]{3,2,1,0:T(8,128)(2,1)} %bitcast.68, s32[32,128]{1,0:T(8,128)} %copy-done, s32[32,128]{1,0:T(8,128)} %get-tuple-element.16.second_ref, s32[32,128]{1,0:T(8,128)} %get-tuple-element.15.turn_ref, f32[4,128]{1,0:T(4,128)} %get-tuple-element.18.cos_ref, ...), custom_call_target="tpu_custom_call" | custom-call | tf_op jit(solution)/shard_map/pallas_call | solution.py:103
  29.6 6.7 %all-to-all-start.1 = ((bf16[16,2,32,8,128]{4,3,2,1,0:T(8,128)(2,1)}), bf16[16,2,32,8,128]{4,3,2,1,0:T(8,128)(2,1)S(1)}, u32[]{:S(2)}, u32[]{:S(2)}) async-start(bf16[16,2,32,8,128]{4,3,2,1,0:T(8,128)(2,1)} %shard_map.46), calls=%async_computation.1 | async-start | bytes 4194304 | tf_op jit(solution)/shard_map/all_to_all | solution.py:154
  36.5 0.6 reduce-window.6
  37.5 0.5 fusion.42
  38.0 1.1 fusion.40
  39.1 5.3 %multiply_convert_fusion.1 = (bf16[64,32,1024]{2,1,0:T(8,128)(2,1)}, bf16[64,32,1024]{2,1,0:T(8,128)(2,1)}) fusion(f32[32,1024]{1,0:T(8,128)S(1)} %get-tuple-element.21, f32[64,1024]{1,0:T(8,128)S(1)} %get-tuple-element.20, f32[32,1024]{1,0:T(8,128)S(1)} %get-tuple-element.22, f32[64,1024]{1,0:T(8,128)S(1)} %get-tuple-element.19), kind=kLoop, calls=%fused_computation.5 | loop fusion | flops 20971520 | bytes 9175040 | tf_op jit(solution)/shard_map/convert_element_type | solution.py:51
  44.4 17.7 %all-to-all-done.1 = bf16[16,2,32,8,128]{4,3,2,1,0:T(8,128)(2,1)S(1)} async-done(((bf16[16,2,32,8,128]{4,3,2,1,0:T(8,128)(2,1)}), bf16[16,2,32,8,128]{4,3,2,1,0:T(8,128)(2,1)S(1)}, u32[]{:S(2)}, u32[]{:S(2)}) %all-to-all-start.1) | async-done | bytes 2097184 | tf_op jit(solution)/shard_map/all_to_all | solution.py:154
  62.0 7.3 %fusion.3 = f32[2,256,2048]{2,1,0:T(8,128)S(1)} fusion(bf16[16,128,1024]{2,1,0:T(8,128)(2,1)} %bitcast.70, bf16[16,128,1024]{2,1,0:T(8,128)(2,1)} %bitcast.69, bf16[16,2,32,8,128]{4,3,2,1,0:T(8,128)(2,1)S(1)} %all-to-all-done.1), kind=kOutput, calls=%fused_computation.7 | convolution fusion | flops 4311744512 | bytes 14680064 | tf_op jit(solution)/shard_map/tpcqm,tmf->pcqf/dot_general | solution.py:160
  69.6 1.0 convolution_convert_fusion
  70.6 86.6 %all_to_all.15 = bf16[16,48,2048]{2,1,0:T(8,128)(2,1)S(1)} all-to-all(bf16[16,48,2048]{2,1,0:T(8,128)(2,1)S(1)} %bitcast.66), channel_id=1, replica_groups=mesh['chan'=16,'tm'=16] {'chan'}, dimensions={0} | all-to-all | bytes 6291456 | tf_op jit(solution)/shard_map/all_to_all | solution.py:180
  157.2 1.7 %copy.26 = bf16[1,1,16,48,2048]{4,3,2,1,0:T(8,128)(2,1)} copy(bf16[1,1,16,48,2048]{4,3,2,1,0:T(8,128)(2,1)S(1)} %bitcast.67) | data formatting | bytes 6291456
  (27 shorter events, 1.8 us)
Async XLA Ops:
  0.7 13.2 %collective-permute-start = (bf16[32,192]{1,0:T(8,128)(2,1)S(1)}, bf16[32,192]{1,0:T(8,128)(2,1)S(1)}, u32[]{:S(2)}, u32[]{:S(2)}) collective-permute-start(bf16[32,192]{1,0:T(8,128)(2,1)S(1)} %slice.41), channel_id=1, source_target_pairs={{1,0},{2,1},{3,2},{4,3},{5,4},{6,5},{7,6},{8,7},{9,8},{10,9},{11,1... | collective-permute-start | bytes 36872 | tf_op jit(solution)/shard_map/ppermute | solution.py:19
  3.5 17.3 %all-to-all-start = ((s32[16,1,512]{2,1,0:T(1,128)}), s32[16,1,512]{2,1,0:T(1,128)S(1)}, u32[]{:S(2)}, u32[]{:S(2)}) async-start(s32[16,1,512]{2,1,0:T(1,128)} %reshape.205), calls=%async_computation | async-start | bytes 65536 | tf_op jit(solution)/shard_map/all_to_all | solution.py:140
  22.2 0.7 copy-start
  22.9 13.4 %copy-start.1 = (s32[1,32,8,1]{1,3,2,0:T(1,128)S(1)}, s32[1,32,8,1]{1,3,2,0:T(1,128)}, u32[]{:S(2)}) copy-start(s32[1,32,8,1]{1,3,2,0:T(1,128)} %param.7) | copy-start | bytes 3076
  29.6 32.4 %all-to-all-start.1 = ((bf16[16,2,32,8,128]{4,3,2,1,0:T(8,128)(2,1)}), bf16[16,2,32,8,128]{4,3,2,1,0:T(8,128)(2,1)S(1)}, u32[]{:S(2)}, u32[]{:S(2)}) async-start(bf16[16,2,32,8,128]{4,3,2,1,0:T(8,128)(2,1)} %shard_map.46), calls=%async_computation.1 | async-start | bytes 4194304 | tf_op jit(solution)/shard_map/all_to_all | solution.py:154

commit v15 on v11

--- a/solution.py
+++ b/solution.py
@@ -65,19 +65,14 @@
     second_all = second_ref[...].T
     turn_all = turn_ref[...].T
     for index in range(per_block):
-        spectra = jnp.concatenate([spec_ref[index, 0], spec_ref[index, 1]], axis=1)
-        pick = jnp.concatenate(
-            [
-                (first_all[:, index : index + 1] == positions).astype(jnp.bfloat16),
-                (second_all[:, index : index + 1] == positions).astype(jnp.bfloat16),
-            ],
-            axis=0,
-        )
-        picked = jnp.dot(pick, spectra, preferred_element_type=jnp.float32)
-        a_re = picked[:rows, :frames]
-        a_im = picked[:rows, frames:]
-        b_re = picked[rows:, :frames]
-        b_im = picked[rows:, frames:]
+        spec_re = spec_ref[index, 0]
+        spec_im = spec_ref[index, 1]
+        pick_a = (first_all[:, index : index + 1] == positions).astype(jnp.bfloat16)
+        pick_b = (second_all[:, index : index + 1] == positions).astype(jnp.bfloat16)
+        a_re = jnp.dot(pick_a, spec_re, preferred_element_type=jnp.float32)
+        a_im = jnp.dot(pick_a, spec_im, preferred_element_type=jnp.float32)
+        b_re = jnp.dot(pick_b, spec_re, preferred_element_type=jnp.float32)
+        b_im = jnp.dot(pick_b, spec_im, preferred_element_type=jnp.float32)
         real_part = a_re * b_re + a_im * b_im
         imag_part = a_im * b_re - a_re * b_im
         turn = turn_all[:, index : index + 1]

time: 159 us -> 160 us (level)
  no operation moved by 1% of the time
where the time goes in v15:
time: 160 us; the launch traced here: 159 us
  blocking collectives  86.6 us (54%)
  waiting for transfers between devices  17.7 us (11%)
  starting transfers between devices  16.4 us (10%)
  other arithmetic  13.1 us (8%)
  matrix products  12.2 us (8%)
  Pallas kernels  7.2 us (4%)
  local copies, waits for them, and re-layouts  6.05 us (4%)
    all_to_all x1, blocking collectives, on_device(): lax.all_to_all(outgoing, 'chan', split_axis=0, concat_axis=0, tiled=True)  86.6 us
    all_to_all x1, waiting for transfers between devices, on_device(): lax.all_to_all(demod, 'tm', split_axis=0, concat_axis=0, tiled=True)  17.7 us
    all_to_all x1, starting transfers between devices, on_device(): lax.all_to_all(spread, 'tm', split_axis=0, concat_axis=0, tiled=True)  8.47 us
    dot_general x1, matrix products, on_device(): jnp.einsum('tpcqm,tmf->pcqf', arrived, both_tables, preferred_element_typ...  7.26 us
    pallas_call x1, Pallas kernels, demodulated(): pl.pallas_call(demod_kernel, out_shape=jax.ShapeDtypeStruct((blocks, 2, c...  7.2 us
    all_to_all x1, starting transfers between devices, on_device(): lax.all_to_all(demod, 'tm', split_axis=0, concat_axis=0, tiled=True)  6.67 us
    convert_element_type x1, other arithmetic, fourier_tables(): cosine.reshape(FRAMES, KEEP).astype(jnp.bfloat16)  5.25 us
    dot_general x1, matrix products, on_device(): jnp.einsum('cmn,nk->ckm', framed, bank_table, preferred_element_type=jnp....  3.99 us
  transfers between devices with their start and end apart: 3, of which 1 were waited for; matrix products, arithmetic and copies ran while one was open for 11% of the time, Pallas kernels for 0%

profile of v15, /device:TPU:1, one launch (start us, length us, event | category | flops | bytes accessed | tf_op | source)
XLA Modules:
  0.0 159.4 jit_solution(12465763521573124168)
XLA Ops:
  0.0 0.7 slice.41
  0.7 1.3 collective-permute-start
  2.0 0.7 pad_add_fusion
  2.7 0.7 reshape.205
  3.5 8.5 %all-to-all-start = ((s32[16,1,512]{2,1,0:T(1,128)}), s32[16,1,512]{2,1,0:T(1,128)S(1)}, u32[]{:S(2)}, u32[]{:S(2)}) async-start(s32[16,1,512]{2,1,0:T(1,128)} %reshape.205), calls=%async_computation | async-start | bytes 65536 | tf_op jit(solution)/shard_map/all_to_all | solution.py:134
  12.1 1.1 multiply_convert_fusion.2
  13.2 0.7 fusion.53
  13.9 1.1 pad_maximum_fusion
  15.0 0.8 reshape.195
  15.8 0.9 fusion.59
  16.8 4.0 %convolution_convert_fusion.1 = bf16[512,32,128]{2,0,1:T(8,128)(2,1)} fusion(bf16[32,128,64]{2,1,0:T(8,128)(2,1)S(1)} %get-tuple-element.8, bf16[32,128,64]{2,1,0:T(8,128)(2,1)S(1)} %get-tuple-element.9, bf16[32,128,64]{2,1,0:T(8,128)(2,1)S(1)} %get-tuple-element.10, bf16[32,128,64]{2,1,0:T(8,128)(2,1)S(1)} %get-tuple-element.7, ...), kind=kOutput, calls=%fused_computation.8 | convolution fusion | flops 1084751872 | bytes 6553600 | tf_op jit(solution)/shard_map/cmn,nk->ckm/dot_general | solution.py:127
  21.3 0.7 reduce.2
  22.2 0.7 add_select_fusion.3
  22.9 7.2 %shard_map.46 = bf16[16,2,32,8,128]{4,3,2,1,0:T(8,128)(2,1)} custom-call(bf16[32,2,256,128]{3,2,1,0:T(8,128)(2,1)} %bitcast.68, s32[32,128]{1,0:T(8,128)} %copy-done, s32[32,128]{1,0:T(8,128)} %get-tuple-element.16.second_ref, s32[32,128]{1,0:T(8,128)} %get-tuple-element.15.turn_ref, f32[4,128]{1,0:T(4,128)} %get-tuple-element.18.cos_ref, ...), custom_call_target="tpu_custom_call" | custom-call | tf_op jit(solution)/shard_map/pallas_call | solution.py:97
  30.1 6.7 %all-to-all-start.1 = ((bf16[16,2,32,8,128]{4,3,2,1,0:T(8,128)(2,1)}), bf16[16,2,32,8,128]{4,3,2,1,0:T(8,128)(2,1)S(1)}, u32[]{:S(2)}, u32[]{:S(2)}) async-start(bf16[16,2,32,8,128]{4,3,2,1,0:T(8,128)(2,1)} %shard_map.46), calls=%async_computation.1 | async-start | bytes 4194304 | tf_op jit(solution)/shard_map/all_to_all | solution.py:148
  37.1 0.6 reduce-window.6
  38.0 0.5 fusion.42
  38.5 1.1 fusion.40
  39.6 5.3 %multiply_convert_fusion.1 = (bf16[64,32,1024]{2,1,0:T(8,128)(2,1)}, bf16[64,32,1024]{2,1,0:T(8,128)(2,1)}) fusion(f32[32,1024]{1,0:T(8,128)S(1)} %get-tuple-element.21, f32[64,1024]{1,0:T(8,128)S(1)} %get-tuple-element.20, f32[32,1024]{1,0:T(8,128)S(1)} %get-tuple-element.22, f32[64,1024]{1,0:T(8,128)S(1)} %get-tuple-element.19), kind=kLoop, calls=%fused_computation.5 | loop fusion | flops 20971520 | bytes 9175040 | tf_op jit(solution)/shard_map/convert_element_type | solution.py:51
  44.9 17.7 %all-to-all-done.1 = bf16[16,2,32,8,128]{4,3,2,1,0:T(8,128)(2,1)S(1)} async-done(((bf16[16,2,32,8,128]{4,3,2,1,0:T(8,128)(2,1)}), bf16[16,2,32,8,128]{4,3,2,1,0:T(8,128)(2,1)S(1)}, u32[]{:S(2)}, u32[]{:S(2)}) %all-to-all-start.1) | async-done | bytes 2097184 | tf_op jit(solution)/shard_map/all_to_all | solution.py:148
  62.5 7.3 %fusion.3 = f32[2,256,2048]{2,1,0:T(8,128)S(1)} fusion(bf16[16,128,1024]{2,1,0:T(8,128)(2,1)} %bitcast.70, bf16[16,128,1024]{2,1,0:T(8,128)(2,1)} %bitcast.69, bf16[16,2,32,8,128]{4,3,2,1,0:T(8,128)(2,1)S(1)} %all-to-all-done.1), kind=kOutput, calls=%fused_computation.7 | convolution fusion | flops 4311744512 | bytes 14680064 | tf_op jit(solution)/shard_map/tpcqm,tmf->pcqf/dot_general | solution.py:154
  70.1 1.0 convolution_convert_fusion
  71.1 86.6 %all_to_all.15 = bf16[16,48,2048]{2,1,0:T(8,128)(2,1)S(1)} all-to-all(bf16[16,48,2048]{2,1,0:T(8,128)(2,1)S(1)} %bitcast.66), channel_id=1, replica_groups=mesh['chan'=16,'tm'=16] {'chan'}, dimensions={0} | all-to-all | bytes 6291456 | tf_op jit(solution)/shard_map/all_to_all | solution.py:174
  157.7 1.7 %copy.26 = bf16[1,1,16,48,2048]{4,3,2,1,0:T(8,128)(2,1)} copy(bf16[1,1,16,48,2048]{4,3,2,1,0:T(8,128)(2,1)S(1)} %bitcast.67) | data formatting | bytes 6291456
  (27 shorter events, 1.8 us)
Async XLA Ops:
  0.7 13.2 %collective-permute-start = (bf16[32,192]{1,0:T(8,128)(2,1)S(1)}, bf16[32,192]{1,0:T(8,128)(2,1)S(1)}, u32[]{:S(2)}, u32[]{:S(2)}) collective-permute-start(bf16[32,192]{1,0:T(8,128)(2,1)S(1)} %slice.41), channel_id=1, source_target_pairs={{1,0},{2,1},{3,2},{4,3},{5,4},{6,5},{7,6},{8,7},{9,8},{10,9},{11,1... | collective-permute-start | bytes 36872 | tf_op jit(solution)/shard_map/ppermute | solution.py:19
  3.5 17.3 %all-to-all-start = ((s32[16,1,512]{2,1,0:T(1,128)}), s32[16,1,512]{2,1,0:T(1,128)S(1)}, u32[]{:S(2)}, u32[]{:S(2)}) async-start(s32[16,1,512]{2,1,0:T(1,128)} %reshape.205), calls=%async_computation | async-start | bytes 65536 | tf_op jit(solution)/shard_map/all_to_all | solution.py:134
  22.2 0.7 copy-start
  22.9 13.9 %copy-start.1 = (s32[1,32,8,1]{1,3,2,0:T(1,128)S(1)}, s32[1,32,8,1]{1,3,2,0:T(1,128)}, u32[]{:S(2)}) copy-start(s32[1,32,8,1]{1,3,2,0:T(1,128)} %param.7) | copy-start | bytes 3076
  30.1 32.4 %all-to-all-start.1 = ((bf16[16,2,32,8,128]{4,3,2,1,0:T(8,128)(2,1)}), bf16[16,2,32,8,128]{4,3,2,1,0:T(8,128)(2,1)S(1)}, u32[]{:S(2)}, u32[]{:S(2)}) async-start(bf16[16,2,32,8,128]{4,3,2,1,0:T(8,128)(2,1)} %shard_map.46), calls=%async_computation.1 | async-start | bytes 4194304 | tf_op jit(solution)/shard_map/all_to_all | solution.py:148

commit v16 on v11

--- a/solution.py
+++ b/solution.py
@@ -94,7 +94,7 @@
             out_ref[block, 1, index] = demod_im[block * pairs : (block + 1) * pairs]
 
 
-def demodulated(spectra, first, second, turn, cos_table, sin_table, blocks, per_block=8, interpret=False):
+def demodulated(spectra, first, second, turn, cos_table, sin_table, blocks, per_block=16, interpret=False):
     channels, parts, bands, frames = spectra.shape
     rows = first.shape[1]
     pairs = rows // blocks

time: 159 us -> 159 us (level)
  transfers between devices with their start and end apart: 3 -> 3, of which waited for: 1 -> 1; matrix products, arithmetic and copies ran while one was open for 11% -> 12% of each run, Pallas kernels for 0% -> 0%
where the time goes in v16:
time: 159 us; the launch traced here: 158 us
  blocking collectives  86.6 us (54%)
  waiting for transfers between devices  17.7 us (11%)
  starting transfers between devices  16.4 us (10%)
  other arithmetic  13.1 us (8%)
  matrix products  12.2 us (8%)
  Pallas kernels  6.14 us (4%)
  local copies, waits for them, and re-layouts  6.05 us (4%)
    all_to_all x1, blocking collectives, on_device(): lax.all_to_all(outgoing, 'chan', split_axis=0, concat_axis=0, tiled=True)  86.6 us
    all_to_all x1, waiting for transfers between devices, on_device(): lax.all_to_all(demod, 'tm', split_axis=0, concat_axis=0, tiled=True)  17.7 us
    all_to_all x1, starting transfers between devices, on_device(): lax.all_to_all(spread, 'tm', split_axis=0, concat_axis=0, tiled=True)  8.47 us
    dot_general x1, matrix products, on_device(): jnp.einsum('tpcqm,tmf->pcqf', arrived, both_tables, preferred_element_typ...  7.26 us
    all_to_all x1, starting transfers between devices, on_device(): lax.all_to_all(demod, 'tm', split_axis=0, concat_axis=0, tiled=True)  6.68 us
    pallas_call x1, Pallas kernels, demodulated(): pl.pallas_call(demod_kernel, out_shape=jax.ShapeDtypeStruct((blocks, 2, c...  6.14 us
    convert_element_type x1, other arithmetic, fourier_tables(): cosine.reshape(FRAMES, KEEP).astype(jnp.bfloat16)  5.25 us
    dot_general x1, matrix products, on_device(): jnp.einsum('cmn,nk->ckm', framed, bank_table, preferred_element_type=jnp....  3.99 us
  transfers between devices with their start and end apart: 3, of which 1 were waited for; matrix products, arithmetic and copies ran while one was open for 12% of the time, Pallas kernels for 0%

profile of v16, /device:TPU:1, one launch (start us, length us, event | category | flops | bytes accessed | tf_op | source)
XLA Modules:
  0.0 158.3 jit_solution(12365175632079450843)
XLA Ops:
  0.0 0.7 slice.41
  0.7 1.3 collective-permute-start
  2.0 0.7 pad_add_fusion
  2.7 0.7 reshape.205
  3.5 8.5 %all-to-all-start = ((s32[16,1,512]{2,1,0:T(1,128)}), s32[16,1,512]{2,1,0:T(1,128)S(1)}, u32[]{:S(2)}, u32[]{:S(2)}) async-start(s32[16,1,512]{2,1,0:T(1,128)} %reshape.205), calls=%async_computation | async-start | bytes 65536 | tf_op jit(solution)/shard_map/all_to_all | solution.py:139
  12.1 1.1 multiply_convert_fusion.2
  13.2 0.7 fusion.53
  13.9 1.1 pad_maximum_fusion
  15.0 0.8 reshape.195
  15.8 0.9 fusion.59
  16.8 4.0 %convolution_convert_fusion.1 = bf16[512,32,128]{2,0,1:T(8,128)(2,1)} fusion(bf16[32,128,64]{2,1,0:T(8,128)(2,1)S(1)} %get-tuple-element.8, bf16[32,128,64]{2,1,0:T(8,128)(2,1)S(1)} %get-tuple-element.9, bf16[32,128,64]{2,1,0:T(8,128)(2,1)S(1)} %get-tuple-element.10, bf16[32,128,64]{2,1,0:T(8,128)(2,1)S(1)} %get-tuple-element.7, ...), kind=kOutput, calls=%fused_computation.8 | convolution fusion | flops 1084751872 | bytes 6553600 | tf_op jit(solution)/shard_map/cmn,nk->ckm/dot_general | solution.py:132
  21.3 0.7 reduce.2
  22.2 0.7 add_select_fusion.3
  22.9 6.1 %shard_map.46 = bf16[16,2,32,8,128]{4,3,2,1,0:T(8,128)(2,1)} custom-call(bf16[32,2,256,128]{3,2,1,0:T(8,128)(2,1)} %bitcast.68, s32[32,128]{1,0:T(8,128)} %copy-done, s32[32,128]{1,0:T(8,128)} %get-tuple-element.16.second_ref, s32[32,128]{1,0:T(8,128)} %get-tuple-element.15.turn_ref, f32[4,128]{1,0:T(4,128)} %get-tuple-element.18.cos_ref, ...), custom_call_target="tpu_custom_call" | custom-call | tf_op jit(solution)/shard_map/pallas_call | solution.py:102
  29.0 6.7 %all-to-all-start.1 = ((bf16[16,2,32,8,128]{4,3,2,1,0:T(8,128)(2,1)}), bf16[16,2,32,8,128]{4,3,2,1,0:T(8,128)(2,1)S(1)}, u32[]{:S(2)}, u32[]{:S(2)}) async-start(bf16[16,2,32,8,128]{4,3,2,1,0:T(8,128)(2,1)} %shard_map.46), calls=%async_computation.1 | async-start | bytes 4194304 | tf_op jit(solution)/shard_map/all_to_all | solution.py:153
  36.0 0.6 reduce-window.6
  36.9 0.5 fusion.42
  37.5 1.1 fusion.40
  38.6 5.3 %multiply_convert_fusion.1 = (bf16[64,32,1024]{2,1,0:T(8,128)(2,1)}, bf16[64,32,1024]{2,1,0:T(8,128)(2,1)}) fusion(f32[32,1024]{1,0:T(8,128)S(1)} %get-tuple-element.21, f32[64,1024]{1,0:T(8,128)S(1)} %get-tuple-element.20, f32[32,1024]{1,0:T(8,128)S(1)} %get-tuple-element.22, f32[64,1024]{1,0:T(8,128)S(1)} %get-tuple-element.19), kind=kLoop, calls=%fused_computation.5 | loop fusion | flops 20971520 | bytes 9175040 | tf_op jit(solution)/shard_map/convert_element_type | solution.py:51
  43.8 17.7 %all-to-all-done.1 = bf16[16,2,32,8,128]{4,3,2,1,0:T(8,128)(2,1)S(1)} async-done(((bf16[16,2,32,8,128]{4,3,2,1,0:T(8,128)(2,1)}), bf16[16,2,32,8,128]{4,3,2,1,0:T(8,128)(2,1)S(1)}, u32[]{:S(2)}, u32[]{:S(2)}) %all-to-all-start.1) | async-done | bytes 2097184 | tf_op jit(solution)/shard_map/all_to_all | solution.py:153
  61.5 7.3 %fusion.3 = f32[2,256,2048]{2,1,0:T(8,128)S(1)} fusion(bf16[16,128,1024]{2,1,0:T(8,128)(2,1)} %bitcast.70, bf16[16,128,1024]{2,1,0:T(8,128)(2,1)} %bitcast.69, bf16[16,2,32,8,128]{4,3,2,1,0:T(8,128)(2,1)S(1)} %all-to-all-done.1), kind=kOutput, calls=%fused_computation.7 | convolution fusion | flops 4311744512 | bytes 14680064 | tf_op jit(solution)/shard_map/tpcqm,tmf->pcqf/dot_general | solution.py:159
  69.1 1.0 convolution_convert_fusion
  70.1 86.6 %all_to_all.15 = bf16[16,48,2048]{2,1,0:T(8,128)(2,1)S(1)} all-to-all(bf16[16,48,2048]{2,1,0:T(8,128)(2,1)S(1)} %bitcast.66), channel_id=1, replica_groups=mesh['chan'=16,'tm'=16] {'chan'}, dimensions={0} | all-to-all | bytes 6291456 | tf_op jit(solution)/shard_map/all_to_all | solution.py:179
  156.7 1.7 %copy.26 = bf16[1,1,16,48,2048]{4,3,2,1,0:T(8,128)(2,1)} copy(bf16[1,1,16,48,2048]{4,3,2,1,0:T(8,128)(2,1)S(1)} %bitcast.67) | data formatting | bytes 6291456
  (27 shorter events, 1.8 us)
Async XLA Ops:
  0.7 13.2 %collective-permute-start = (bf16[32,192]{1,0:T(8,128)(2,1)S(1)}, bf16[32,192]{1,0:T(8,128)(2,1)S(1)}, u32[]{:S(2)}, u32[]{:S(2)}) collective-permute-start(bf16[32,192]{1,0:T(8,128)(2,1)S(1)} %slice.41), channel_id=1, source_target_pairs={{1,0},{2,1},{3,2},{4,3},{5,4},{6,5},{7,6},{8,7},{9,8},{10,9},{11,1... | collective-permute-start | bytes 36872 | tf_op jit(solution)/shard_map/ppermute | solution.py:19
  3.5 17.3 %all-to-all-start = ((s32[16,1,512]{2,1,0:T(1,128)}), s32[16,1,512]{2,1,0:T(1,128)S(1)}, u32[]{:S(2)}, u32[]{:S(2)}) async-start(s32[16,1,512]{2,1,0:T(1,128)} %reshape.205), calls=%async_computation | async-start | bytes 65536 | tf_op jit(solution)/shard_map/all_to_all | solution.py:139
  22.2 0.7 copy-start
  22.9 12.8 %copy-start.1 = (s32[1,32,8,1]{1,3,2,0:T(1,128)S(1)}, s32[1,32,8,1]{1,3,2,0:T(1,128)}, u32[]{:S(2)}) copy-start(s32[1,32,8,1]{1,3,2,0:T(1,128)} %param.7) | copy-start | bytes 3076
  29.0 32.4 %all-to-all-start.1 = ((bf16[16,2,32,8,128]{4,3,2,1,0:T(8,128)(2,1)}), bf16[16,2,32,8,128]{4,3,2,1,0:T(8,128)(2,1)S(1)}, u32[]{:S(2)}, u32[]{:S(2)}) async-start(bf16[16,2,32,8,128]{4,3,2,1,0:T(8,128)(2,1)} %shard_map.46), calls=%async_computation.1 | async-start | bytes 4194304 | tf_op jit(solution)/shard_map/all_to_all | solution.py:153
